TPU v7x, 256 devices: a whole 4x4x8 slice. The times are simulated.
256 devices in a mesh: section: 4 (over y), expert: 64 (over x, z, core).
Axes of the slice: x: 4, y: 4, z: 8, core: 2. Of those that a mesh axis runs over, the one named last changes fastest.
Arguments:
- tokens: bfloat16 [1024, 4096], P('expert', 'section'), may hold values from -6 to 6
- cotangent: bfloat16 [1024, 4096], P('expert', 'section'), may hold values from -6 to 6
- routes: int32 [1024, 2], P('expert'), may hold values from 0 to 7, all different within a row; in each aligned block of 16 rows (0 to 15, 16 to 31, ...) at most 6 rows name the same one
- w_router: bfloat16 [4096, 8], P('section'), may hold values from -0.09375 to 0.09375
- w_gate: bfloat16 [64, 4096, 1024], P('expert', None, 'section'), may hold values from -0.09375 to 0.09375
- w_up: bfloat16 [64, 4096, 1024], P('expert', None, 'section'), may hold values from -0.09375 to 0.09375
- w_down: bfloat16 [64, 1024, 4096], P('expert', 'section'), may hold values from -0.0625 to 0.0625
Outputs:
- mixed: bfloat16 [1024, 4096], P('expert', 'section')
- grad_tokens: bfloat16 [1024, 4096], P('expert', 'section')
- grad_router: float32 [4096, 8], P('section')
- grad_gate: bfloat16 [64, 4096, 1024], P('expert', None, 'section')
- grad_up: bfloat16 [64, 4096, 1024], P('expert', None, 'section')
- grad_down: bfloat16 [64, 1024, 4096], P('expert', 'section')
Inputs may be any that keep to these rules, and one draw needn't show every extreme that they name: `routes`: each token names two different experts. Within each aligned block of 16 tokens no expert is named by more than 6 tokens, and in every draw some block has an expert named by exactly 6 tokens.
All inputs are finite; a program needn't handle non-finite values.
Results may differ from a plain program's by a relative error of at most 0.023.
Values may be sent and summed in bfloat16 or wider, within the bound.
No kernel may reach another device: no remote copies, remote signals or barrier semaphores. Data moves between devices by JAX's collectives and lax.ppermute only.
A program may use at most 128 MiB of HBM per device.

v0:
```python
import jax
import jax.numpy as jnp
from jax import lax
from jax.sharding import PartitionSpec as P

CAP = 6


def spread_rows(buffer, experts, groups, capacity):
    width = buffer.shape[1]
    tiled = jnp.repeat(buffer.reshape(experts, capacity, width), groups, axis=0)
    return tiled.reshape(experts * groups * capacity, width)


def fold_groups(received, experts, groups, capacity):
    height = received.shape[0]
    folded = received.reshape(height, experts, groups, capacity)
    return jnp.sum(folded, axis=2).reshape(height, experts * capacity)


def per_device(tokens, cotangent, routes, w_router, w_gate, w_up, w_down):
    highest = lax.Precision.HIGHEST
    experts = w_router.shape[1]
    groups = lax.axis_size("expert") // experts
    capacity = CAP
    tok_count = tokens.shape[0]
    slot_total = experts * capacity
    partial_logits = jnp.dot(tokens, w_router, preferred_element_type=jnp.float32)
    logits = lax.psum(partial_logits, "section")
    route_hot = routes[:, :, None] == jnp.arange(experts, dtype=jnp.int32)[None, None, :]
    zero_f = jnp.zeros((), jnp.float32)
    chosen = jnp.sum(jnp.where(route_hot, logits[:, None, :], zero_f), axis=2)
    gate_first = 1.0 / (1.0 + jnp.exp(chosen[:, 1] - chosen[:, 0]))
    gate_second = 1.0 / (1.0 + jnp.exp(chosen[:, 0] - chosen[:, 1]))
    counts_flat = route_hot.astype(jnp.int32).reshape(2 * tok_count, experts)
    earlier = jnp.cumsum(counts_flat, axis=0) - counts_flat
    position = jnp.sum(earlier * counts_flat, axis=1).reshape(tok_count, 2)
    slot_row = routes * capacity + position
    slot_ids = jnp.arange(slot_total, dtype=jnp.int32)[None, :]
    pick_first = slot_row[:, 0:1] == slot_ids
    pick_second = slot_row[:, 1:2] == slot_ids
    pick_both = (pick_first | pick_second).astype(jnp.bfloat16)
    x_source = jnp.einsum(
        "ts,td->sd", pick_both, tokens, preferred_element_type=jnp.float32
    ).astype(jnp.bfloat16)
    cot_float = cotangent.astype(jnp.float32)
    scaled_first = (gate_first[:, None] * cot_float).astype(jnp.bfloat16)
    scaled_second = (gate_second[:, None] * cot_float).astype(jnp.bfloat16)
    dy_source = jnp.einsum(
        "ts,td->sd",
        pick_first.astype(jnp.bfloat16),
        scaled_first,
        preferred_element_type=jnp.float32,
    )
    dy_source = dy_source + jnp.einsum(
        "ts,td->sd",
        pick_second.astype(jnp.bfloat16),
        scaled_second,
        preferred_element_type=jnp.float32,
    )
    dy_source = dy_source.astype(jnp.bfloat16)
    sent_x = spread_rows(x_source, experts, groups, capacity)
    sent_dy = spread_rows(dy_source, experts, groups, capacity)
    recv_x, recv_dy = (
        lax.all_to_all(sent_x, "expert", split_axis=0, concat_axis=0, tiled=True),
        lax.all_to_all(sent_dy, "expert", split_axis=0, concat_axis=0, tiled=True),
    )
    x_rows, dy_rows = (
        lax.all_gather(recv_x, "section", axis=1, tiled=True),
        lax.all_gather(recv_dy, "section", axis=1, tiled=True),
    )
    gate_local = w_gate[0]
    up_local = w_up[0]
    down_local = w_down[0]
    pre_gate = jnp.dot(x_rows, gate_local, preferred_element_type=jnp.float32)
    pre_up = jnp.dot(x_rows, up_local, preferred_element_type=jnp.float32)
    sigmoid_gate = jax.nn.sigmoid(pre_gate)
    activated = pre_gate * sigmoid_gate
    hidden = (activated * pre_up).astype(jnp.bfloat16)
    d_hidden = jnp.einsum("pd,fd->pf", dy_rows, down_local, preferred_element_type=jnp.float32)
    grad_down = jnp.einsum("pf,pd->fd", hidden, dy_rows, preferred_element_type=jnp.float32).astype(
        jnp.bfloat16
    )
    d_pre_gate = (
        d_hidden * pre_up * sigmoid_gate * (1.0 + pre_gate * (1.0 - sigmoid_gate))
    ).astype(jnp.bfloat16)
    d_pre_up = (d_hidden * activated).astype(jnp.bfloat16)
    grad_gate = jnp.einsum(
        "pd,pf->df", x_rows, d_pre_gate, preferred_element_type=jnp.float32
    ).astype(jnp.bfloat16)
    grad_up = jnp.einsum("pd,pf->df", x_rows, d_pre_up, preferred_element_type=jnp.float32).astype(
        jnp.bfloat16
    )
    row_total = x_rows.shape[0]
    out_piece = jnp.einsum("fd,pf->dp", down_local, hidden, preferred_element_type=jnp.float32)
    dx_piece = jnp.einsum("df,pf->dp", gate_local, d_pre_gate, preferred_element_type=jnp.float32)
    dx_piece = dx_piece + jnp.einsum(
        "df,pf->dp", up_local, d_pre_up, preferred_element_type=jnp.float32
    )
    reduced = lax.psum_scatter(
        jnp.concatenate([out_piece, dx_piece], axis=1).astype(jnp.bfloat16),
        "section",
        scatter_dimension=0,
        tiled=True,
    ).astype(jnp.float32)
    out_part = reduced[:, :row_total]
    dx_part = reduced[:, row_total:]
    back_out, back_dx = (
        lax.all_to_all(
            out_part.astype(jnp.bfloat16), "expert", split_axis=1, concat_axis=1, tiled=True
        ).astype(out_part.dtype),
        lax.all_to_all(
            dx_part.astype(jnp.bfloat16), "expert", split_axis=1, concat_axis=1, tiled=True
        ).astype(dx_part.dtype),
    )
    slot_out = fold_groups(back_out, experts, groups, capacity)
    slot_dx = fold_groups(back_dx, experts, groups, capacity)
    first_float = pick_first.astype(jnp.float32)
    second_float = pick_second.astype(jnp.float32)
    out_first = jnp.einsum("ts,ds->td", first_float, slot_out, precision=highest)
    out_second = jnp.einsum("ts,ds->td", second_float, slot_out, precision=highest)
    mixed = (gate_first[:, None] * out_first + gate_second[:, None] * out_second).astype(
        jnp.bfloat16
    )
    local_inner = jnp.stack(
        [jnp.sum(cot_float * out_first, axis=1), jnp.sum(cot_float * out_second, axis=1)], axis=1
    )
    gate_inner = lax.psum(local_inner, "section")
    d_first = gate_first * gate_second * (gate_inner[:, 0] - gate_inner[:, 1])
    d_logits = jnp.where(route_hot[:, 0, :], d_first[:, None], zero_f) - jnp.where(
        route_hot[:, 1, :], d_first[:, None], zero_f
    )
    dx_expert = jnp.einsum("ts,ds->td", first_float, slot_dx, precision=highest)
    dx_expert = dx_expert + jnp.einsum("ts,ds->td", second_float, slot_dx, precision=highest)
    router_float = w_router.astype(jnp.float32)
    grad_tokens = (dx_expert + jnp.dot(d_logits, router_float.T, precision=highest)).astype(
        jnp.bfloat16
    )
    router_part = jnp.dot(tokens.astype(jnp.float32).T, d_logits, precision=highest)
    grad_router = lax.psum(router_part, "expert")
    return (mixed, grad_tokens, grad_router, grad_gate[None], grad_up[None], grad_down[None])


def solution(mesh):
    in_specs = (
        P("expert", "section"),
        P("expert", "section"),
        P("expert", None),
        P("section", None),
        P("expert", None, "section"),
        P("expert", None, "section"),
        P("expert", "section", None),
    )
    out_specs = (
        P("expert", "section"),
        P("expert", "section"),
        P("section", None),
        P("expert", None, "section"),
        P("expert", None, "section"),
        P("expert", "section", None),
    )
    return jax.shard_map(
        per_device, mesh=mesh, in_specs=in_specs, out_specs=out_specs, check_vma=False
    )
```

profile of v0, /device:TPU:8, one launch (start us, length us, event | category | flops | bytes accessed | tf_op | source)
XLA Modules:
  0.0 568.5 jit_solution(8639622228040765927)
XLA Ops:
  7.2 0.0 copy-start
  7.2 0.0 all-gather.5.cloned.1.call-start
  7.2 1.0 fusion.48
  8.2 9.9 %psum.21 = f32[16,8]{0,1:T(8,128)S(1)} all-reduce(f32[16,8]{0,1:T(8,128)S(1)} %fusion.48), channel_id=1, replica_groups=mesh['section'=4,'expert'=64] {'section'}, use_global_device_ids=true, to_apply=%region_0.0 | all-reduce | flops 128 | bytes 1024 | tf_op jit(solution)/shard_map/psum | solution.py:29
  18.1 0.8 copy.19
  18.9 0.7 select_reduce_fusion.1
  19.6 0.0 copy-start.12
  19.6 0.1 eq.55
  19.7 0.1 fusion.27
  19.8 0.1 reduce_window_sum.11
  19.8 0.2 select_reduce_fusion
  20.0 0.1 reshape.49
  20.1 0.1 copy.20
  20.2 0.7 multiply_add_fusion
  20.9 1.0 fusion.23
  22.0 1.0 fusion.15
  23.0 0.0 copy-start.4
  23.1 0.1 broadcast_in_dim.58
  23.2 38.7 %all_to_all.42 = bf16[64,6,1024]{2,1,0:T(8,128)(2,1)S(1)} all-to-all(bf16[64,6,1024]{2,1,0:T(8,128)(2,1)S(1)} %bitcast.92), channel_id=1, replica_groups=mesh['section'=4,'expert'=64] {'expert'}, dimensions={0} | all-to-all | bytes 1572864 | tf_op jit(solution)/shard_map/all_to_all | solution.py:66
  61.9 1.1 all_to_all.33
  63.0 0.0 all-gather.5.cloned.1.call-update
  63.1 0.0 all-gather.3.cloned.1.call-start
  63.1 0.3 convolution_convert_fusion.4
  63.4 0.1 broadcast_in_dim.57
  63.6 34.5 %all_to_all.43 = bf16[64,6,1024]{2,1,0:T(8,128)(2,1)S(1)} all-to-all(bf16[64,6,1024]{2,1,0:T(8,128)(2,1)S(1)} %bitcast.93), channel_id=1, replica_groups=mesh['section'=4,'expert'=64] {'expert'}, dimensions={0} | all-to-all | bytes 1572864 | tf_op jit(solution)/shard_map/all_to_all | solution.py:65
  98.1 1.1 all_to_all.30
  99.3 0.0 all-gather.3.cloned.1.call-update
  99.3 0.0 reduce-scatter.2.cloned.1.call-start
  99.3 2.4 all-gather.5.cloned.1.call-done
  101.7 3.6 fusion.5
  105.3 41.2 %all-gather.3.cloned.1.call-done = bf16[384,4096]{1,0:T(8,128)(2,1)} async-done(((bf16[384,1024]{1,0:T(8,128)(2,1)}), bf16[384,4096]{1,0:T(8,128)(2,1)}) %all-gather.3.cloned.1.call-update) | async-done | bytes 3145744 | tf_op jit(solution)/shard_map/all_gather | solution.py:69
  146.5 3.7 fusion.13
  150.2 0.0 copy-start.1
  150.2 1.1 multiply_convert_fusion.2
  151.3 0.5 copy-done.1
  151.8 1.0 fusion
  152.8 0.6 copy-done.2
  153.4 1.0 fusion.11
  154.4 1.2 fusion.1
  155.5 3.4 pad_maximum_fusion
  159.0 0.0 reduce-scatter.2.cloned.1.call-update
  159.0 0.0 copy-start.9
  159.0 66.4 %reduce-scatter.2.cloned.1.call-done = bf16[1024,768]{0,1:T(8,128)(2,1)} async-done(((bf16[4096,768]{0,1:T(8,128)(2,1)}), bf16[1024,768]{0,1:T(8,128)(2,1)}) %reduce-scatter.2.cloned.1.call-update) | async-done | bytes 1572880 | tf_op jit(solution)/shard_map/reduce_scatter | solution.py:100
  225.4 2.4 fusion.47
  227.8 1.2 all_to_all.36
  229.0 10.4 %all-to-all-start.3 = ((bf16[1024,64,6]{0,2,1:T(8,128)(2,1)}), bf16[1024,64,6]{0,2,1:T(8,128)(2,1)S(1)}, u32[]{:S(2)}, u32[]{:S(2)}) async-start(bf16[1024,64,6]{0,2,1:T(8,128)(2,1)} %all_to_all.36), calls=%async_computation.4 | async-start | bytes 2097152 | tf_op jit(solution)/shard_map/all_to_all | solution.py:112
  239.5 2.2 all_to_all.34
  241.7 25.9 %all-to-all-done.3 = bf16[1024,64,6]{0,2,1:T(8,128)(2,1)S(1)} async-done(((bf16[1024,64,6]{0,2,1:T(8,128)(2,1)}), bf16[1024,64,6]{0,2,1:T(8,128)(2,1)S(1)}, u32[]{:S(2)}, u32[]{:S(2)}) %all-to-all-start.3) | async-done | bytes 786464 | tf_op jit(solution)/shard_map/all_to_all | solution.py:112
  267.7 6.8 %all-to-all-start.2 = ((bf16[1024,64,6]{0,2,1:T(8,128)(2,1)}), bf16[1024,64,6]{0,2,1:T(8,128)(2,1)}, u32[]{:S(2)}, u32[]{:S(2)}) async-start(bf16[1024,64,6]{0,2,1:T(8,128)(2,1)} %all_to_all.34), calls=%async_computation.3 | async-start | bytes 2097152 | tf_op jit(solution)/shard_map/all_to_all | solution.py:109
  274.5 4.6 fusion.4
  279.1 2.6 fusion.2
  281.8 2.6 fusion.3
  284.4 0.0 copy-start.8
  284.4 0.2 convert_reduce_fusion
  284.7 0.2 fusion.30
  284.9 0.2 convolution_add_fusion.2
  285.2 17.4 %all-to-all-done.2 = bf16[1024,64,6]{0,2,1:T(8,128)(2,1)} async-done(((bf16[1024,64,6]{0,2,1:T(8,128)(2,1)}), bf16[1024,64,6]{0,2,1:T(8,128)(2,1)}, u32[]{:S(2)}, u32[]{:S(2)}) %all-to-all-start.2) | async-done | bytes 786464 | tf_op jit(solution)/shard_map/all_to_all | solution.py:109
  302.5 1.5 convert_reduce_fusion.1
  304.0 0.2 fusion.28
  304.3 1.0 fusion.20
  305.3 9.5 %psum.22 = f32[16,2]{0,1:T(2,128)S(1)} all-reduce(f32[16,2]{0,1:T(2,128)S(1)} %pad_maximum_fusion.1), channel_id=1, replica_groups=mesh['section'=4,'expert'=64] {'section'}, use_global_device_ids=true, to_apply=%region_9.10 | all-reduce | flops 32 | bytes 256 | tf_op jit(solution)/shard_map/psum | solution.py:128
  314.8 0.1 convolution_bitcast_fusion
  315.0 0.8 fusion.16
  315.8 246.1 %psum.23 = f32[1024,8]{0,1:T(8,128)} all-reduce(f32[1024,8]{0,1:T(8,128)S(1)} %convolution_bitcast_fusion), channel_id=1, replica_groups=mesh['section'=4,'expert'=64] {'expert'}, use_global_device_ids=true, to_apply=%region_10.11 | all-reduce | flops 8192 | bytes 65536 | tf_op jit(solution)/shard_map/psum | solution.py:140
  (33 shorter events, 0.2 us)
Async XLA Ops:
  7.2 143.0 %copy-start = (bf16[1,4096,256]{2,1,0:T(8,128)(2,1)S(1)}, bf16[1,4096,256]{2,1,0:T(8,128)(2,1)}, u32[]{:S(2)}) copy-start(bf16[1,4096,256]{2,1,0:T(8,128)(2,1)} %param.12) | copy-start | bytes 6291460
  7.2 94.6 %all-gather.5.cloned.1.call-start = ((), (), s32[]{:S(2)}) async-start(), calls=%async_computation.6 | async-start | bytes 3932160 | tf_op jit(solution)/shard_map/all_gather | solution.py:70
  19.6 2.3 copy-start.10
  19.6 2.3 copy-start.12
  23.0 40.1 %copy-start.4 = (bf16[16,1024]{1,0:T(8,128)(2,1)S(1)}, bf16[16,1024]{1,0:T(8,128)(2,1)}, u32[]{:S(2)}) copy-start(bf16[16,1024]{1,0:T(8,128)(2,1)} %param.7) | copy-start | bytes 98308
  63.1 83.4 %all-gather.3.cloned.1.call-start = ((), (), s32[]{:S(2)}) async-start(), calls=%async_computation.5 | async-start | bytes 3932160 | tf_op jit(solution)/shard_map/all_gather | solution.py:69
  99.3 126.1 %reduce-scatter.2.cloned.1.call-start = ((), (), s32[]{:S(2)}) async-start(), calls=%async_computation.7 | async-start | bytes 7864320 | tf_op jit(solution)/shard_map/reduce_scatter | solution.py:100
  146.5 3.7 copy-start.14
  150.2 1.6 copy-start.1
  151.3 3.1 copy-start.6
  151.8 1.6 copy-start.2
  159.0 80.5 %copy-start.9 = (s32[16,2]{0,1:T(2,128)S(1)}, s32[16,2]{0,1:T(2,128)}, u32[]{:S(2)}) copy-start(s32[16,2]{0,1:T(2,128)} %param.9) | copy-start | bytes 388
  229.0 38.6 %all-to-all-start.3 = ((bf16[1024,64,6]{0,2,1:T(8,128)(2,1)}), bf16[1024,64,6]{0,2,1:T(8,128)(2,1)S(1)}, u32[]{:S(2)}, u32[]{:S(2)}) async-start(bf16[1024,64,6]{0,2,1:T(8,128)(2,1)} %all_to_all.36), calls=%async_computation.4 | async-start | bytes 2097152 | tf_op jit(solution)/shard_map/all_to_all | solution.py:112
  267.7 34.9 %all-to-all-start.2 = ((bf16[1024,64,6]{0,2,1:T(8,128)(2,1)}), bf16[1024,64,6]{0,2,1:T(8,128)(2,1)}, u32[]{:S(2)}, u32[]{:S(2)}) async-start(bf16[1024,64,6]{0,2,1:T(8,128)(2,1)} %all_to_all.34), calls=%async_computation.3 | async-start | bytes 2097152 | tf_op jit(solution)/shard_map/all_to_all | solution.py:109
  274.5 4.6 copy-start.15
  279.1 2.6 copy-start.7
  284.4 19.9 %copy-start.3 = (bf16[16,1024]{1,0:T(8,128)(2,1)S(1)}, bf16[16,1024]{1,0:T(8,128)(2,1)}, u32[]{:S(2)}) copy-start(bf16[16,1024]{1,0:T(8,128)(2,1)} %param.8) | copy-start | bytes 98308
  284.4 19.9 %copy-start.11 = (f32[16,1]{0,1:T(1,128)S(1)}, f32[16,1]{0,1:T(1,128)}, u32[]{:S(2)}) copy-start(f32[16,1]{0,1:T(1,128)} %copy-done.10) | copy-start | bytes 196
  284.4 19.9 %copy-start.13 = (f32[16,1]{0,1:T(1,128)S(1)}, f32[16,1]{0,1:T(1,128)}, u32[]{:S(2)}) copy-start(f32[16,1]{0,1:T(1,128)} %copy-done.12) | copy-start | bytes 196
  284.4 30.4 %copy-start.5 = (bf16[16,1024]{1,0:T(8,128)(2,1)S(1)}, bf16[16,1024]{1,0:T(8,128)(2,1)}, u32[]{:S(2)}) copy-start(bf16[16,1024]{1,0:T(8,128)(2,1)} %param.7) | copy-start | bytes 98308
  284.4 30.6 %copy-start.8 = (bf16[1024,8]{0,1:T(8,128)(2,1)S(1)}, bf16[1024,8]{0,1:T(8,128)(2,1)}, u32[]{:S(2)}) copy-start(bf16[1024,8]{0,1:T(8,128)(2,1)} %param.10) | copy-start | bytes 49156
Sparse Core Ops, SparseCore 0:
  63.2 38.5 all-gather.4
  104.1 42.3 all-gather.2
  159.1 66.2 reduce-scatter.1
where the time goes:
time: 569 us; the launch traced here: 568 us
  blocking collectives  339 us (60%)
  waiting for transfers between devices  153 us (27%)
  matrix products  27.3 us (5%)
  starting transfers between devices  17.4 us (3%)
  between operations  14.1 us (2%)
  local copies, waits for them, and re-layouts  10.6 us (2%)
  other arithmetic  6.92 us (1%)
    psum x1, blocking collectives, per_device(): grad_router = lax.psum(router_part, 'expert')  246 us
    reduce_scatter x1, waiting for transfers between devices, per_device(): lax.psum_scatter(jnp.concatenate([out_piece, dx_piece], axis=1).astype(jn...  66.4 us
    all_gather x1, waiting for transfers between devices, per_device(): lax.all_gather(recv_x, 'section', axis=1, tiled=True)  41.2 us
    all_to_all x1, blocking collectives, per_device(): lax.all_to_all(sent_dy, 'expert', split_axis=0, concat_axis=0, tiled=True)  38.7 us
    all_to_all x1, blocking collectives, per_device(): lax.all_to_all(sent_x, 'expert', split_axis=0, concat_axis=0, tiled=True)  34.5 us
    all_to_all x1, waiting for transfers between devices, per_device(): lax.all_to_all(dx_part.astype(jnp.bfloat16), 'expert', split_axis=1, conc...  25.9 us
    all_to_all x1, waiting for transfers between devices, per_device(): lax.all_to_all(out_part.astype(jnp.bfloat16), 'expert', split_axis=1, con...  17.4 us
  transfers between devices with their start and end apart: 5, of which 5 were waited for; matrix products, arithmetic and copies ran while one was open for 3% of the time, Pallas kernels for 0%

commit v1 on v0

v1 whole, which is shorter than its diff:
```python
import jax
import jax.numpy as jnp
import numpy as np
from jax import lax
from jax.sharding import Mesh
from jax.sharding import PartitionSpec as P

CAP = 6
LANES = 128
EXPERT_AXES = ("ex", "ez", "ec")


def expert_size():
    size = 1
    for name in EXPERT_AXES:
        size = size * lax.axis_size(name)
    return size


def per_device(tokens, cotangent, routes, w_router, w_gate, w_up, w_down):
    highest = lax.Precision.HIGHEST
    experts = w_router.shape[1]
    groups = expert_size() // experts
    capacity = CAP
    tok_count, width = tokens.shape
    n_section = lax.axis_size("section")
    slot_total = experts * capacity
    partial_logits = jnp.dot(tokens, w_router, preferred_element_type=jnp.float32)
    logits = lax.psum(partial_logits, "section")
    route_hot = routes[:, :, None] == jnp.arange(experts, dtype=jnp.int32)[None, None, :]
    zero_f = jnp.zeros((), jnp.float32)
    chosen = jnp.sum(jnp.where(route_hot, logits[:, None, :], zero_f), axis=2)
    gate_first = 1.0 / (1.0 + jnp.exp(chosen[:, 1] - chosen[:, 0]))
    gate_second = 1.0 / (1.0 + jnp.exp(chosen[:, 0] - chosen[:, 1]))
    counts_flat = route_hot.astype(jnp.int32).reshape(2 * tok_count, experts)
    earlier = jnp.cumsum(counts_flat, axis=0) - counts_flat
    position = jnp.sum(earlier * counts_flat, axis=1).reshape(tok_count, 2)
    slot_row = routes * capacity + position
    slot_ids = jnp.arange(slot_total, dtype=jnp.int32)[None, :]
    pick_first = slot_row[:, 0:1] == slot_ids
    pick_second = slot_row[:, 1:2] == slot_ids
    pick_both = (pick_first | pick_second).astype(jnp.bfloat16)
    x_source = jnp.einsum(
        "ts,td->sd", pick_both, tokens, preferred_element_type=jnp.float32
    ).astype(jnp.bfloat16)
    cot_float = cotangent.astype(jnp.float32)
    scaled_first = (gate_first[:, None] * cot_float).astype(jnp.bfloat16)
    scaled_second = (gate_second[:, None] * cot_float).astype(jnp.bfloat16)
    dy_source = jnp.einsum(
        "ts,td->sd",
        pick_first.astype(jnp.bfloat16),
        scaled_first,
        preferred_element_type=jnp.float32,
    )
    dy_source = dy_source + jnp.einsum(
        "ts,td->sd",
        pick_second.astype(jnp.bfloat16),
        scaled_second,
        preferred_element_type=jnp.float32,
    )
    dy_source = dy_source.astype(jnp.bfloat16)
    both_source = jnp.stack(
        [x_source.reshape(experts, capacity * width), dy_source.reshape(experts, capacity * width)],
        axis=1,
    )
    block_rows = 2 * capacity * width // LANES
    sent = jnp.broadcast_to(
        both_source.reshape(experts, 1, block_rows, LANES), (experts, groups, block_rows, LANES)
    ).reshape(experts * groups, block_rows, LANES)
    received = lax.all_to_all(sent, EXPERT_AXES, 0, 0, tiled=True)
    row_total = received.shape[0] * capacity
    received = received.reshape(-1, 2, capacity, width).transpose(1, 0, 2, 3)
    received = received.reshape(2, row_total, width)
    gathered = lax.all_gather(received, "section", axis=2, tiled=True)
    x_rows = gathered[0]
    dy_rows = gathered[1]
    gate_local = w_gate[0]
    up_local = w_up[0]
    down_local = w_down[0]
    pre_gate = jnp.dot(x_rows, gate_local, preferred_element_type=jnp.float32)
    pre_up = jnp.dot(x_rows, up_local, preferred_element_type=jnp.float32)
    sigmoid_gate = jax.nn.sigmoid(pre_gate)
    activated = pre_gate * sigmoid_gate
    hidden = (activated * pre_up).astype(jnp.bfloat16)
    d_hidden = jnp.einsum("pd,fd->pf", dy_rows, down_local, preferred_element_type=jnp.float32)
    grad_down = jnp.einsum("pf,pd->fd", hidden, dy_rows, preferred_element_type=jnp.float32).astype(
        jnp.bfloat16
    )
    d_pre_gate = (
        d_hidden * pre_up * sigmoid_gate * (1.0 + pre_gate * (1.0 - sigmoid_gate))
    ).astype(jnp.bfloat16)
    d_pre_up = (d_hidden * activated).astype(jnp.bfloat16)
    grad_gate = jnp.einsum(
        "pd,pf->df", x_rows, d_pre_gate, preferred_element_type=jnp.float32
    ).astype(jnp.bfloat16)
    grad_up = jnp.einsum("pd,pf->df", x_rows, d_pre_up, preferred_element_type=jnp.float32).astype(
        jnp.bfloat16
    )
    hid = gate_local.shape[1]
    down_blocks = down_local.reshape(hid, n_section, width)
    gate_blocks = gate_local.reshape(n_section, width, hid)
    up_blocks = up_local.reshape(n_section, width, hid)
    out_piece = jnp.einsum("pf,fsd->spd", hidden, down_blocks, preferred_element_type=jnp.float32)
    dx_piece = jnp.einsum("pf,sdf->spd", d_pre_gate, gate_blocks, preferred_element_type=jnp.float32)
    dx_piece = dx_piece + jnp.einsum(
        "pf,sdf->spd", d_pre_up, up_blocks, preferred_element_type=jnp.float32
    )
    pieces = jnp.stack([out_piece, dx_piece], axis=1).astype(jnp.bfloat16)
    pieces = pieces.reshape(n_section * 2 * pieces.shape[2], width)
    reduced = lax.psum_scatter(pieces, "section", scatter_dimension=0, tiled=True)
    n_dev = row_total // capacity
    back = reduced.reshape(2, n_dev, capacity, width).transpose(1, 0, 2, 3)
    back = back.reshape(n_dev, block_rows, LANES)
    returned = lax.all_to_all(back, EXPERT_AXES, 0, 0, tiled=True)
    returned = returned.reshape(experts, groups, 2, capacity, width).astype(jnp.float32)
    folded = jnp.sum(returned, axis=1)
    slot_out = folded[:, 0].reshape(slot_total, width)
    slot_dx = folded[:, 1].reshape(slot_total, width)
    first_float = pick_first.astype(jnp.float32)
    second_float = pick_second.astype(jnp.float32)
    out_first = jnp.dot(first_float, slot_out, precision=highest)
    out_second = jnp.dot(second_float, slot_out, precision=highest)
    mixed = (gate_first[:, None] * out_first + gate_second[:, None] * out_second).astype(
        jnp.bfloat16
    )
    local_inner = jnp.stack(
        [jnp.sum(cot_float * out_first, axis=1), jnp.sum(cot_float * out_second, axis=1)], axis=1
    )
    gate_inner = lax.psum(local_inner, "section")
    d_first = gate_first * gate_second * (gate_inner[:, 0] - gate_inner[:, 1])
    d_logits = jnp.where(route_hot[:, 0, :], d_first[:, None], zero_f) - jnp.where(
        route_hot[:, 1, :], d_first[:, None], zero_f
    )
    dx_expert = jnp.dot(first_float, slot_dx, precision=highest)
    dx_expert = dx_expert + jnp.dot(second_float, slot_dx, precision=highest)
    router_float = w_router.astype(jnp.float32)
    grad_tokens = (dx_expert + jnp.dot(d_logits, router_float.T, precision=highest)).astype(
        jnp.bfloat16
    )
    router_part = jnp.einsum(
        "te,tf->ef", d_logits, tokens.astype(jnp.float32), precision=highest
    )
    for name in reversed(EXPERT_AXES):
        router_part = lax.psum(router_part, name)
    grad_router = router_part.T
    return (mixed, grad_tokens, grad_router, grad_gate[None], grad_up[None], grad_down[None])


def expert_shape(devices):
    try:
        xs = sorted({d.coords[0] for d in devices.flat})
        zs = sorted({d.coords[2] for d in devices.flat})
        cores = sorted({d.core_on_chip for d in devices.flat})
        shape = (len(xs), len(zs), len(cores))
    except AttributeError:
        shape = (4, 8, 2)
    if int(np.prod(shape)) != devices.shape[1]:
        shape = (devices.shape[1] // 16, 8, 2)
    return shape


def solution(mesh):
    devices = mesh.devices
    fine = Mesh(
        devices.reshape((devices.shape[0],) + expert_shape(devices)),
        ("section",) + EXPERT_AXES,
    )
    ex = EXPERT_AXES
    in_specs = (
        P(ex, "section"),
        P(ex, "section"),
        P(ex, None),
        P("section", None),
        P(ex, None, "section"),
        P(ex, None, "section"),
        P(ex, "section", None),
    )
    out_specs = (
        P(ex, "section"),
        P(ex, "section"),
        P("section", None),
        P(ex, None, "section"),
        P(ex, None, "section"),
        P(ex, "section", None),
    )
    return jax.shard_map(
        per_device, mesh=fine, in_specs=in_specs, out_specs=out_specs, check_vma=False
    )
```

time: 569 us -> 388 us (0.68)
  blocking collectives: 339 us -> 118 us
  local copies, waits for them, and re-layouts: 10.6 us -> 51.2 us
  starting transfers between devices: 17.4 us -> 10.7 us
    psum x1 -> x3, blocking collectives: 246 us -> 48.7 us  [per_device(): router_part = lax.psum(router_part, name)]
    all_to_all x2 -> x1, blocking collectives: 73.3 us -> 50.1 us  [per_device(): received = lax.all_to_all(sent, EXPERT_AXES, 0, 0, tiled=True)]
    all_gather x2 -> x1, waiting for transfers between devices: 43.6 us -> 63.9 us  [per_device(): gathered = lax.all_gather(received, 'section', axis=2, tiled=True)]
    all_to_all x2 -> x1, waiting for transfers between devices: 43.3 us -> 25.9 us  [per_device(): returned = lax.all_to_all(back, EXPERT_AXES, 0, 0, tiled=True)]
    slice x1 -> x2, local copies, waits for them, and re-layouts: 2.37 us -> 15.7 us  [the longest x1 15.7 us: per_device(): dy_rows = gathered[1]]
    reshape x4 -> x3, local copies, waits for them, and re-layouts: 0.14 us -> 11.2 us  [the longest x1 4.39 us: per_device(): back = back.reshape(n_dev, block_rows, LANES)]
    another operation x0 -> x6, local copies, waits for them, and re-layouts: none -> 8.07 us  [the longest x1 4.49 us: per_device(): down_blocks = down_local.reshape(hid, n_section, width)]
    all_to_all x2 -> x1, starting transfers between devices: 17.3 us -> 10.7 us  [per_device(): returned = lax.all_to_all(back, EXPERT_AXES, 0, 0, tiled=True)]
  transfers between devices with their start and end apart: 5 -> 3, of which waited for: 5 -> 3; matrix products, arithmetic and copies ran while one was open for 3% -> 5% of each run, Pallas kernels for 0% -> 0%
where the time goes in v1:
time: 388 us; the launch traced here: 387 us
  waiting for transfers between devices  157 us (40%)
  blocking collectives  118 us (30%)
  local copies, waits for them, and re-layouts  51.2 us (13%)
  matrix products  30 us (8%)
  between operations  14.4 us (4%)
  starting transfers between devices  10.7 us (3%)
  other arithmetic  5.51 us (1%)
    reduce_scatter x1, waiting for transfers between devices, per_device(): lax.psum_scatter(pieces, 'section', scatter_dimension=0, tiled=True)  67.1 us
    all_gather x1, waiting for transfers between devices, per_device(): gathered = lax.all_gather(received, 'section', axis=2, tiled=True)  63.9 us
    all_to_all x1, blocking collectives, per_device(): received = lax.all_to_all(sent, EXPERT_AXES, 0, 0, tiled=True)  50.1 us
    psum x3, blocking collectives, per_device(): router_part = lax.psum(router_part, name)  48.7 us
    all_to_all x1, waiting for transfers between devices, per_device(): returned = lax.all_to_all(back, EXPERT_AXES, 0, 0, tiled=True)  25.9 us
    slice x1, local copies, waits for them, and re-layouts, per_device(): dy_rows = gathered[1]  15.7 us
    all_to_all x1, starting transfers between devices, per_device(): returned = lax.all_to_all(back, EXPERT_AXES, 0, 0, tiled=True)  10.7 us
    psum x1, blocking collectives, per_device(): logits = lax.psum(partial_logits, 'section')  9.88 us
  transfers between devices with their start and end apart: 3, of which 3 were waited for; matrix products, arithmetic and copies ran while one was open for 5% of the time, Pallas kernels for 0%

profile of v1, /device:TPU:8, one launch (start us, length us, event | category | flops | bytes accessed | tf_op | source)
XLA Modules:
  0.0 387.1 jit_solution(12677243295857633148)
XLA Ops:
  7.2 0.0 copy-start
  7.2 0.0 all-gather.2.cloned.1.call-start
  7.2 1.0 fusion.58
  8.2 9.9 %psum.35 = f32[16,8]{0,1:T(8,128)S(1)} all-reduce(f32[16,8]{0,1:T(8,128)S(1)} %fusion.58), channel_id=1, replica_groups=mesh['section'=4,'ex'=4,'ez'=8,'ec'=2] {'section'}, use_global_device_ids=true, to_apply=%region_0.0 | all-reduce | flops 128 | bytes 1024 | tf_op jit(solution)/shard_map/psum | solution.py:29
  18.1 0.8 copy.44
  18.9 0.7 select_reduce_fusion.1
  19.6 0.1 eq.55
  19.7 0.1 fusion.35
  19.8 0.1 reduce_window_sum.11
  19.8 0.2 select_reduce_fusion
  20.0 0.1 reshape.42
  20.1 0.1 copy.45
  20.2 0.7 multiply_add_fusion
  20.9 1.0 convolution_convert_fusion.3
  21.9 0.1 stack_reshape.8
  22.0 1.0 fusion.31
  23.1 1.0 fusion.19
  24.1 0.1 stack_reshape.9
  24.2 0.5 pad_maximum_fusion.1
  24.6 0.1 broadcast_in_dim.58
  24.8 0.2 broadcast_in_dim.59
  25.0 50.1 %all_to_all.10 = bf16[64,96,128]{2,1,0:T(8,128)(2,1)} all-to-all(bf16[64,96,128]{2,1,0:T(8,128)(2,1)S(1)} %bitcast.103), channel_id=1, replica_groups=mesh['section'=4,'ex'=4,'ez'=8,'ec'=2] {'ex','ez','ec'}, dimensions={0} | all-to-all | bytes 3145728 | tf_op jit(solution)/shard_map/all_to_all | solution.py:70
  75.1 4.3 %reshape.44 = bf16[64,2,6,1024]{3,2,1,0:T(8,128)(2,1)} reshape(bf16[64,96,128]{2,1,0:T(8,128)(2,1)} %all_to_all.10) | data formatting | bytes 3145728 | tf_op jit(solution)/shard_map/reshape | solution.py:72
  79.5 4.4 %copy.48 = bf16[2,64,6,1024]{3,0,2,1:T(2,128)(2,1)} copy(bf16[2,64,6,1024]{3,2,0,1:T(8,128)(2,1)} %bitcast.100) | data formatting | bytes 3145728 | tf_op jit(solution)/shard_map/transpose | solution.py:72
  83.8 0.0 all-gather.2.cloned.1.call-update
  83.8 0.0 reduce-scatter.2.cloned.1.call-start
  83.9 4.5 %reshape_squeeze.15 = bf16[256,4,1024]{2,1,0:T(4,128)(2,1)} reshape(bf16[1,256,4096]{2,1,0:T(8,128)(2,1)} %param.13) | data formatting | bytes 4194304 | tf_op jit(solution)/shard_map/reshape;squeeze | solution.py:100
  88.4 63.9 %all-gather.2.cloned.1.call-done = bf16[2,384,4096]{2,0,1:T(2,128)(2,1)} async-done(((bf16[2,384,1024]{2,0,1:T(2,128)(2,1)}), bf16[2,384,4096]{2,0,1:T(2,128)(2,1)}) %all-gather.2.cloned.1.call-update) | async-done | bytes 6291472 | tf_op jit(solution)/shard_map/all_gather | solution.py:74
  152.3 15.7 %fusion.56 = (bf16[1,384,4096]{2,0,1:T(2,128)(2,1)S(1)}, bf16[1,384,4096]{2,0,1:T(2,128)(2,1)S(1)}) fusion(bf16[2,384,4096]{2,0,1:T(2,128)(2,1)} %all-gather.2.cloned.1.call-done), kind=kLoop, calls=%fused_computation.89 | loop fusion | bytes 12582912 | tf_op jit(solution)/shard_map/slice | solution.py:76
  168.0 0.0 copy-start.6
  168.0 3.7 copy.52
  171.7 0.0 copy-start.7
  171.7 3.6 fusion.5
  175.4 1.0 fusion.11
  176.4 0.0 copy-start.3
  176.4 1.1 multiply_convert_fusion.2
  177.5 0.5 copy-done.3
  178.0 1.7 convert_bitcast_fusion
  179.7 1.0 fusion.23
  180.7 1.4 fusion.3
  182.1 0.6 pad_maximum_fusion
  182.7 3.4 copy.50
  186.1 0.0 reduce-scatter.2.cloned.1.call-update
  186.1 67.1 %reduce-scatter.2.cloned.1.call-done = bf16[768,1024]{1,0:T(8,128)(2,1)} async-done(((bf16[3072,1024]{1,0:T(8,128)(2,1)}), bf16[768,1024]{1,0:T(8,128)(2,1)}) %reduce-scatter.2.cloned.1.call-update) | async-done | bytes 1572880 | tf_op jit(solution)/shard_map/reduce_scatter | solution.py:110
  253.2 2.5 reshape.46
  255.7 1.6 copy.51
  257.3 4.4 %reshape.47 = bf16[64,96,128]{2,1,0:T(8,128)(2,1)} reshape(bf16[64,2,6,1024]{3,2,1,0:T(8,128)(2,1)} %copy.51) | data formatting | bytes 3145728 | tf_op jit(solution)/shard_map/reshape | solution.py:113
  261.7 10.7 %all-to-all-start.1 = ((bf16[64,96,128]{2,1,0:T(8,128)(2,1)}), bf16[64,96,128]{2,1,0:T(8,128)(2,1)}, u32[]{:S(2)}, u32[]{:S(2)}) async-start(bf16[64,96,128]{2,1,0:T(8,128)(2,1)} %reshape.47), calls=%async_computation.2 | async-start | bytes 3145728 | tf_op jit(solution)/shard_map/all_to_all | solution.py:114
  272.4 8.2 %fusion.2 = bf16[1,256,4096]{2,1,0:T(8,128)(2,1)} fusion(bf16[384,256]{1,0:T(8,128)(2,1)S(1)} %get-tuple-element.10, bf16[1,384,4096]{2,0,1:T(2,128)(2,1)} %copy-done.2), kind=kOutput, calls=%fused_computation.7 | convolution fusion | flops 806354944 | bytes 5439488 | tf_op jit(solution)/shard_map/pf,pd->fd/dot_general | solution.py:86
  280.6 2.6 fusion
  283.2 2.6 fusion.1
  285.8 25.9 %all-to-all-done.1 = bf16[64,96,128]{2,1,0:T(8,128)(2,1)} async-done(((bf16[64,96,128]{2,1,0:T(8,128)(2,1)}), bf16[64,96,128]{2,1,0:T(8,128)(2,1)}, u32[]{:S(2)}, u32[]{:S(2)}) %all-to-all-start.1) | async-done | bytes 1572896 | tf_op jit(solution)/shard_map/all_to_all | solution.py:114
  311.7 4.7 %reshape.48 = f32[8,8,2,6,1024]{4,3,2,1,0:T(8,128)} reshape(bf16[64,96,128]{2,1,0:T(8,128)(2,1)} %all-to-all-done.1) | data formatting | bytes 4718592 | tf_op jit(solution)/shard_map/convert_element_type | solution.py:115
  316.4 2.7 reduce_sum.47
  319.2 0.2 fusion.38
  319.5 0.2 convolution_add_fusion.2
  319.7 0.2 fusion.36
  320.0 1.0 fusion.28
  321.0 9.5 %psum.36 = f32[16,2]{0,1:T(2,128)S(1)} all-reduce(f32[16,2]{0,1:T(2,128)S(1)} %pad_maximum_fusion.2), channel_id=1, replica_groups=mesh['section'=4,'ex'=4,'ez'=8,'ec'=2] {'section'}, use_global_device_ids=true, to_apply=%region_8.9 | all-reduce | flops 32 | bytes 256 | tf_op jit(solution)/shard_map/psum | solution.py:129
  330.5 0.1 fusion.41
  330.6 0.8 fusion.20
  331.5 3.4 psum.37
  334.9 28.5 %psum.38 = f32[8,1024]{1,0:T(8,128)S(1)} all-reduce(f32[8,1024]{1,0:T(8,128)S(1)} %psum.37), channel_id=1, replica_groups=mesh['section'=4,'ex'=4,'ez'=8,'ec'=2] {'ez'}, use_global_device_ids=true, to_apply=%region_10.11 | all-reduce | flops 8192 | bytes 65536 | tf_op jit(solution)/shard_map/psum | solution.py:144
  363.3 16.9 %psum.39 = f32[1024,8]{0,1:T(8,128)} all-reduce(f32[1024,8]{0,1:T(8,128)S(1)} %bitcast.105), channel_id=1, replica_groups=mesh['section'=4,'ex'=4,'ez'=8,'ec'=2] {'ex'}, use_global_device_ids=true, to_apply=%region_11.12 | all-reduce | flops 8192 | bytes 65536 | tf_op jit(solution)/shard_map/psum | solution.py:144
  (27 shorter events, 0.2 us)
Async XLA Ops:
  7.2 169.2 %copy-start = (bf16[1,4096,256]{2,1,0:T(8,128)(2,1)S(1)}, bf16[1,4096,256]{2,1,0:T(8,128)(2,1)}, u32[]{:S(2)}) copy-start(bf16[1,4096,256]{2,1,0:T(8,128)(2,1)} %param.12) | copy-start | bytes 6291460
  7.2 145.1 %all-gather.2.cloned.1.call-start = ((), (), s32[]{:S(2)}) async-start(), calls=%async_computation.3 | async-start | bytes 7864320 | tf_op jit(solution)/shard_map/all_gather | solution.py:74
  83.8 169.4 %reduce-scatter.2.cloned.1.call-start = ((), (), s32[]{:S(2)}) async-start(), calls=%async_computation.4 | async-start | bytes 7864320 | tf_op jit(solution)/shard_map/reduce_scatter | solution.py:110
  168.0 3.7 copy-start.2
  168.0 3.7 copy-start.6
  171.7 4.7 %copy-start.4 = (bf16[1,384,4096]{2,1,0:T(8,128)(2,1)}, bf16[1,384,4096]{2,1,0:T(8,128)(2,1)S(1)}, u32[]{:S(2)}) copy-start(bf16[1,384,4096]{2,1,0:T(8,128)(2,1)S(1)} %copy.52) | copy-start | bytes 9437188
  171.7 3.6 copy-start.7
  176.4 1.6 copy-start.3
  257.3 15.1 %copy-start.11 = (s32[16,2]{0,1:T(2,128)S(1)}, s32[16,2]{0,1:T(2,128)}, u32[]{:S(2)}) copy-start(s32[16,2]{0,1:T(2,128)} %param.9) | copy-start | bytes 388
  261.7 50.0 %all-to-all-start.1 = ((bf16[64,96,128]{2,1,0:T(8,128)(2,1)}), bf16[64,96,128]{2,1,0:T(8,128)(2,1)}, u32[]{:S(2)}, u32[]{:S(2)}) async-start(bf16[64,96,128]{2,1,0:T(8,128)(2,1)} %reshape.47), calls=%async_computation.2 | async-start | bytes 3145728 | tf_op jit(solution)/shard_map/all_to_all | solution.py:114
  272.3 8.3 %copy-start.5 = (bf16[1,384,4096]{2,1,0:T(8,128)(2,1)S(1)}, bf16[1,384,4096]{2,1,0:T(8,128)(2,1)}, u32[]{:S(2)}) copy-start(bf16[1,384,4096]{2,1,0:T(8,128)(2,1)} %copy-done.4) | copy-start | bytes 9437188
  311.7 68.5 %copy-start.1 = (bf16[1,4096,256]{2,1,0:T(8,128)(2,1)S(1)}, bf16[1,4096,256]{2,1,0:T(8,128)(2,1)}, u32[]{:S(2)}) copy-start(bf16[1,4096,256]{2,1,0:T(8,128)(2,1)} %param.12) | copy-start | bytes 6291460
  316.4 3.6 copy-start.8
  316.4 14.1 %copy-start.9 = (bf16[16,1024]{1,0:T(8,128)(2,1)S(1)}, bf16[16,1024]{1,0:T(8,128)(2,1)}, u32[]{:S(2)}) copy-start(bf16[16,1024]{1,0:T(8,128)(2,1)} %param.7) | copy-start | bytes 98308
  316.4 14.2 %copy-start.10 = (bf16[1024,8]{0,1:T(8,128)(2,1)S(1)}, bf16[1024,8]{0,1:T(8,128)(2,1)}, u32[]{:S(2)}) copy-start(bf16[1024,8]{0,1:T(8,128)(2,1)} %param.10) | copy-start | bytes 49156
Sparse Core Ops, SparseCore 0:
  84.0 68.2 all-gather.1
  186.2 66.9 reduce-scatter.1

commit v2 on v1

--- a/solution.py
+++ b/solution.py
@@ -69,11 +69,11 @@
     ).reshape(experts * groups, block_rows, LANES)
     received = lax.all_to_all(sent, EXPERT_AXES, 0, 0, tiled=True)
     row_total = received.shape[0] * capacity
-    received = received.reshape(-1, 2, capacity, width).transpose(1, 0, 2, 3)
-    received = received.reshape(2, row_total, width)
-    gathered = lax.all_gather(received, "section", axis=2, tiled=True)
-    x_rows = gathered[0]
-    dy_rows = gathered[1]
+    half = block_rows // 2
+    x_recv = received[:, :half].reshape(row_total, width)
+    dy_recv = received[:, half:].reshape(row_total, width)
+    x_rows = lax.all_gather(x_recv, "section", axis=1, tiled=True)
+    dy_rows = lax.all_gather(dy_recv, "section", axis=1, tiled=True)
     gate_local = w_gate[0]
     up_local = w_up[0]
     down_local = w_down[0]
@@ -105,12 +105,22 @@
     dx_piece = dx_piece + jnp.einsum(
         "pf,sdf->spd", d_pre_up, up_blocks, preferred_element_type=jnp.float32
     )
-    pieces = jnp.stack([out_piece, dx_piece], axis=1).astype(jnp.bfloat16)
-    pieces = pieces.reshape(n_section * 2 * pieces.shape[2], width)
-    reduced = lax.psum_scatter(pieces, "section", scatter_dimension=0, tiled=True)
+    out_red = lax.psum_scatter(
+        out_piece.astype(jnp.bfloat16).reshape(n_section * row_total, width),
+        "section",
+        scatter_dimension=0,
+        tiled=True,
+    )
+    dx_red = lax.psum_scatter(
+        dx_piece.astype(jnp.bfloat16).reshape(n_section * row_total, width),
+        "section",
+        scatter_dimension=0,
+        tiled=True,
+    )
     n_dev = row_total // capacity
-    back = reduced.reshape(2, n_dev, capacity, width).transpose(1, 0, 2, 3)
-    back = back.reshape(n_dev, block_rows, LANES)
+    back = jnp.stack(
+        [out_red.reshape(n_dev, half, LANES), dx_red.reshape(n_dev, half, LANES)], axis=1
+    ).reshape(n_dev, block_rows, LANES)
     returned = lax.all_to_all(back, EXPERT_AXES, 0, 0, tiled=True)
     returned = returned.reshape(experts, groups, 2, capacity, width).astype(jnp.float32)
     folded = jnp.sum(returned, axis=1)
@@ -140,8 +150,9 @@
     router_part = jnp.einsum(
         "te,tf->ef", d_logits, tokens.astype(jnp.float32), precision=highest
     )
-    for name in reversed(EXPERT_AXES):
-        router_part = lax.psum(router_part, name)
+    router_part = lax.psum(router_part, EXPERT_AXES[2])
+    for name in (EXPERT_AXES[1], EXPERT_AXES[0]):
+        router_part = jnp.sum(lax.all_gather(router_part, name, axis=0), axis=0)
     grad_router = router_part.T
     return (mixed, grad_tokens, grad_router, grad_gate[None], grad_up[None], grad_down[None])
 

time: 388 us -> 377 us (0.972)
  local copies, waits for them, and re-layouts: 51.2 us -> 19.3 us
  waiting for transfers between devices: 157 us -> 181 us
  blocking collectives: 118 us -> 110 us
    psum x3 -> x1, blocking collectives: 48.7 us -> 3.4 us  [per_device(): router_part = lax.psum(router_part, EXPERT_AXES[2])]
    all_gather x0 -> x2, blocking collectives: none -> 37 us  [per_device(): router_part = jnp.sum(lax.all_gather(router_part, name, axis=0), axis=0)]
    slice x1, local copies, waits for them, and re-layouts: 15.7 us -> 0.98 us  [per_device(): dy_recv = received[:, half:].reshape(row_total, width)]
    all_gather x1 -> x2, waiting for transfers between devices: 63.9 us -> 78.4 us  [the longest x1 41.2 us: per_device(): dy_rows = lax.all_gather(dy_recv, 'section', axis=1, tiled=True)]
    reshape x3 -> x2, local copies, waits for them, and re-layouts: 11.2 us -> 3.36 us  [the longest x1 2.15 us: per_device(): x_recv = received[:, :half].reshape(row_total, width)]
    transpose x2 -> x0, local copies, waits for them, and re-layouts: 5.92 us -> none  [the longest x1 4.35 us: per_device(): received = received.reshape(-1, 2, capacity, width).transpose(1, 0, 2, 3)]
    reduce_scatter x1 -> x2, waiting for transfers between devices: 67.1 us -> 72.8 us  [the longest x1 41.6 us: per_device(): lax.psum_scatter(out_piece.astype(jnp.bfloat16).reshape(n_section * row_t...]
  transfers between devices with their start and end apart: 3 -> 5, of which waited for: 3 -> 5; matrix products, arithmetic and copies ran while one was open for 5% -> 7% of each run, Pallas kernels for 0% -> 0%
where the time goes in v2:
time: 377 us; the launch traced here: 376 us
  waiting for transfers between devices  181 us (48%)
  blocking collectives  110 us (29%)
  matrix products  33.6 us (9%)
  local copies, waits for them, and re-layouts  19.3 us (5%)
  between operations  14 us (4%)
  starting transfers between devices  11 us (3%)
  other arithmetic  8.07 us (2%)
    all_to_all x1, blocking collectives, per_device(): received = lax.all_to_all(sent, EXPERT_AXES, 0, 0, tiled=True)  50 us
    reduce_scatter x1, waiting for transfers between devices, per_device(): lax.psum_scatter(out_piece.astype(jnp.bfloat16).reshape(n_section * row_t...  41.6 us
    all_gather x1, waiting for transfers between devices, per_device(): dy_rows = lax.all_gather(dy_recv, 'section', axis=1, tiled=True)  41.2 us
    all_gather x1, waiting for transfers between devices, per_device(): x_rows = lax.all_gather(x_recv, 'section', axis=1, tiled=True)  37.2 us
    all_gather x2, blocking collectives, per_device(): router_part = jnp.sum(lax.all_gather(router_part, name, axis=0), axis=0)  37 us
    reduce_scatter x1, waiting for transfers between devices, per_device(): lax.psum_scatter(dx_piece.astype(jnp.bfloat16).reshape(n_section * row_to...  31.2 us
    all_to_all x1, waiting for transfers between devices, per_device(): returned = lax.all_to_all(back, EXPERT_AXES, 0, 0, tiled=True)  29.5 us
    all_to_all x1, starting transfers between devices, per_device(): returned = lax.all_to_all(back, EXPERT_AXES, 0, 0, tiled=True)  10.8 us
  transfers between devices with their start and end apart: 5, of which 5 were waited for; matrix products, arithmetic and copies ran while one was open for 7% of the time, Pallas kernels for 0%

profile of v2, /device:TPU:8, one launch (start us, length us, event | category | flops | bytes accessed | tf_op | source)
XLA Modules:
  0.0 376.4 jit_solution(15602883923206184391)
XLA Ops:
  7.2 0.0 all-gather.4.cloned.1.call-start
  7.2 0.9 copy.35
  8.1 0.1 eq.55
  8.2 0.1 fusion.26
  8.3 0.1 reduce_window_sum.11
  8.3 0.2 select_reduce_fusion
  8.5 0.1 reshape.42
  8.6 0.1 copy.36
  8.7 0.7 multiply_add_fusion
  9.4 0.9 fusion.48
  10.3 9.9 %psum.21 = f32[16,8]{0,1:T(8,128)S(1)} all-reduce(f32[16,8]{0,1:T(8,128)S(1)} %fusion.48), channel_id=1, replica_groups=mesh['section'=4,'ex'=4,'ez'=8,'ec'=2] {'section'}, use_global_device_ids=true, to_apply=%region_0.0 | all-reduce | flops 128 | bytes 1024 | tf_op jit(solution)/shard_map/psum | solution.py:29
  20.2 0.7 select_reduce_fusion.1
  20.9 1.0 convolution_convert_fusion.4
  21.9 1.0 fusion.22
  23.0 1.0 fusion.10
  24.0 0.1 stack_reshape.17
  24.1 0.1 stack_reshape.16
  24.2 0.5 pad_maximum_fusion.1
  24.6 0.1 broadcast_in_dim.58
  24.8 0.2 broadcast_in_dim.59
  25.0 50.0 %all_to_all.10 = bf16[64,96,128]{2,1,0:T(8,128)(2,1)S(1)} all-to-all(bf16[64,96,128]{2,1,0:T(8,128)(2,1)S(1)} %bitcast.91), channel_id=1, replica_groups=mesh['section'=4,'ex'=4,'ez'=8,'ec'=2] {'ex','ez','ec'}, dimensions={0} | all-to-all | bytes 3145728 | tf_op jit(solution)/shard_map/all_to_all | solution.py:70
  75.0 1.0 fusion.46
  76.0 2.1 reshape.44
  78.2 0.0 all-gather.4.cloned.1.call-update
  78.2 0.0 all-gather.6.cloned.1.call-start
  78.2 1.2 reshape.46
  79.5 0.0 all-gather.6.cloned.1.call-update
  79.5 0.0 reduce-scatter.5.cloned.1.call-start
  79.5 37.2 %all-gather.4.cloned.1.call-done = bf16[384,4096]{1,0:T(8,128)(2,1)} async-done(((bf16[384,1024]{1,0:T(8,128)(2,1)}), bf16[384,4096]{1,0:T(8,128)(2,1)}) %all-gather.4.cloned.1.call-update) | async-done | bytes 3145744 | tf_op jit(solution)/shard_map/all_gather | solution.py:75
  116.7 3.5 fusion.7
  120.3 41.2 %all-gather.6.cloned.1.call-done = bf16[384,4096]{1,0:T(8,128)(2,1)} async-done(((bf16[384,1024]{1,0:T(8,128)(2,1)}), bf16[384,4096]{1,0:T(8,128)(2,1)}) %all-gather.6.cloned.1.call-update) | async-done | bytes 3145744 | tf_op jit(solution)/shard_map/all_gather | solution.py:76
  161.5 3.7 fusion.3
  165.2 1.1 multiply_convert_fusion.2
  166.3 0.5 copy-done.1
  166.8 1.0 fusion.14
  167.8 2.9 add_convert_fusion
  170.7 0.0 reduce-scatter.5.cloned.1.call-update
  170.7 0.0 reduce-scatter.3.cloned.1.call-start
  170.7 4.5 %reshape_squeeze.15 = bf16[256,4,1024]{2,1,0:T(4,128)(2,1)} reshape(bf16[1,256,4096]{2,1,0:T(8,128)(2,1)} %param.13) | data formatting | bytes 4194304 | tf_op jit(solution)/shard_map/reshape;squeeze | solution.py:100
  175.2 4.9 %convolution_convert_fusion.3 = bf16[384,4,1024]{2,0,1:T(8,128)(2,1)} fusion(bf16[256,4,1024]{2,1,0:T(4,128)(2,1)} %reshape_squeeze.15, bf16[384,256]{1,0:T(8,128)(2,1)S(1)} %get-tuple-element.10), kind=kOutput, calls=%fused_computation.7 | convolution fusion | flops 806879232 | bytes 5439488 | tf_op jit(solution)/shard_map/pf,fsd->spd/dot_general | solution.py:103
  180.1 0.0 reduce-scatter.3.cloned.1.call-update
  180.2 31.2 %reduce-scatter.5.cloned.1.call-done = bf16[384,1024]{1,0:T(8,128)(2,1)} async-done(((bf16[1536,1024]{1,0:T(8,128)(2,1)}), bf16[384,1024]{1,0:T(8,128)(2,1)}) %reduce-scatter.5.cloned.1.call-update) | async-done | bytes 786448 | tf_op jit(solution)/shard_map/reduce_scatter | solution.py:114
  211.4 1.4 stack_reshape.15
  212.8 41.6 %reduce-scatter.3.cloned.1.call-done = bf16[384,1024]{1,0:T(8,128)(2,1)} async-done(((bf16[1536,1024]{1,0:T(8,128)(2,1)}), bf16[384,1024]{1,0:T(8,128)(2,1)}) %reduce-scatter.3.cloned.1.call-update) | async-done | bytes 786448 | tf_op jit(solution)/shard_map/reduce_scatter | solution.py:108
  254.4 2.1 stack_reshape.14
  256.6 2.5 pad_maximum_fusion
  259.1 10.8 %all-to-all-start.1 = ((bf16[64,96,128]{2,1,0:T(8,128)(2,1)}), bf16[64,96,128]{2,1,0:T(8,128)(2,1)}, u32[]{:S(2)}, u32[]{:S(2)}) async-start(bf16[64,96,128]{2,1,0:T(8,128)(2,1)} %bitcast.90), calls=%async_computation.3 | async-start | bytes 3145728 | tf_op jit(solution)/shard_map/all_to_all | solution.py:124
  269.9 4.6 %fusion.2 = bf16[1,256,4096]{2,1,0:T(8,128)(2,1)} fusion(bf16[384,256]{1,0:T(8,128)(2,1)S(1)} %get-tuple-element.10, bf16[384,4096]{1,0:T(8,128)(2,1)} %all-gather.6.cloned.1.call-done), kind=kOutput, calls=%fused_computation.6 | convolution fusion | flops 806354944 | bytes 5439488 | tf_op jit(solution)/shard_map/pf,pd->fd/dot_general | solution.py:86
  274.6 2.6 fusion
  277.2 2.6 fusion.1
  279.8 29.5 %all-to-all-done.1 = bf16[64,96,128]{2,1,0:T(8,128)(2,1)} async-done(((bf16[64,96,128]{2,1,0:T(8,128)(2,1)}), bf16[64,96,128]{2,1,0:T(8,128)(2,1)}, u32[]{:S(2)}, u32[]{:S(2)}) %all-to-all-start.1) | async-done | bytes 1572896 | tf_op jit(solution)/shard_map/all_to_all | solution.py:124
  309.3 4.6 %reshape.49 = f32[8,8,2,6,1024]{4,3,2,1,0:T(8,128)} reshape(bf16[64,96,128]{2,1,0:T(8,128)(2,1)} %all-to-all-done.1) | data formatting | bytes 4718592 | tf_op jit(solution)/shard_map/convert_element_type | solution.py:125
  313.8 2.7 reduce_sum.65
  316.7 0.2 fusion.27
  316.9 1.0 fusion.19
  317.9 9.5 %psum.22 = f32[16,2]{0,1:T(2,128)S(1)} all-reduce(f32[16,2]{0,1:T(2,128)S(1)} %pad_maximum_fusion.2), channel_id=1, replica_groups=mesh['section'=4,'ex'=4,'ez'=8,'ec'=2] {'section'}, use_global_device_ids=true, to_apply=%region_9.10 | all-reduce | flops 32 | bytes 256 | tf_op jit(solution)/shard_map/psum | solution.py:139
  327.4 0.1 convolution_bitcast_fusion
  327.5 3.4 psum.23
  331.0 25.0 %all_gather.21 = f32[8,8,1024]{2,1,0:T(8,128)S(1)} all-gather(f32[1,8,1024]{2,1,0:T(8,128)S(1)} %psum.23), channel_id=1, replica_groups=mesh['section'=4,'ex'=4,'ez'=8,'ec'=2] {'ez'}, dimensions={0}, use_global_device_ids=true | all-gather | bytes 294912 | tf_op jit(solution)/shard_map/all_gather | solution.py:155
  355.9 12.0 %all-gather = f32[32,1024]{1,0:T(8,128)S(1)} all-gather(f32[8,1024]{1,0:T(8,128)S(1)} %reduce_sum.68), channel_id=2, replica_groups=mesh['section'=4,'ex'=4,'ez'=8,'ec'=2] {'ex'}, dimensions={0}, use_global_device_ids=true | all-gather | bytes 163840 | tf_op jit(solution)/shard_map/all_gather | solution.py:155
  367.9 0.6 bitcast_reduce_fusion
  368.6 0.2 fusion.29
  368.8 0.2 convolution_add_fusion.2
  369.1 0.8 fusion.11
  (24 shorter events, 0.2 us)
Async XLA Ops:
  7.2 158.0 %copy-start = (bf16[1,4096,256]{2,1,0:T(8,128)(2,1)S(1)}, bf16[1,4096,256]{2,1,0:T(8,128)(2,1)}, u32[]{:S(2)}) copy-start(bf16[1,4096,256]{2,1,0:T(8,128)(2,1)} %param.12) | copy-start | bytes 6291460
  7.2 109.6 %all-gather.4.cloned.1.call-start = ((), (), s32[]{:S(2)}) async-start(), calls=%async_computation.4 | async-start | bytes 3932160 | tf_op jit(solution)/shard_map/all_gather | solution.py:75
  78.2 83.3 %all-gather.6.cloned.1.call-start = ((), (), s32[]{:S(2)}) async-start(), calls=%async_computation.6 | async-start | bytes 3932160 | tf_op jit(solution)/shard_map/all_gather | solution.py:76
  79.5 131.9 %reduce-scatter.5.cloned.1.call-start = ((), (), s32[]{:S(2)}) async-start(), calls=%async_computation.7 | async-start | bytes 3932160 | tf_op jit(solution)/shard_map/reduce_scatter | solution.py:114
  161.5 3.7 copy-start.6
  165.2 1.6 copy-start.1
  170.7 83.7 %reduce-scatter.3.cloned.1.call-start = ((), (), s32[]{:S(2)}) async-start(), calls=%async_computation.5 | async-start | bytes 3932160 | tf_op jit(solution)/shard_map/reduce_scatter | solution.py:108
  259.1 10.8 %copy-start.5 = (s32[16,2]{0,1:T(2,128)S(1)}, s32[16,2]{0,1:T(2,128)}, u32[]{:S(2)}) copy-start(s32[16,2]{0,1:T(2,128)} %param.9) | copy-start | bytes 388
  259.1 50.2 %all-to-all-start.1 = ((bf16[64,96,128]{2,1,0:T(8,128)(2,1)}), bf16[64,96,128]{2,1,0:T(8,128)(2,1)}, u32[]{:S(2)}, u32[]{:S(2)}) async-start(bf16[64,96,128]{2,1,0:T(8,128)(2,1)} %bitcast.90), calls=%async_computation.3 | async-start | bytes 3145728 | tf_op jit(solution)/shard_map/all_to_all | solution.py:124
  269.9 4.6 %copy-start.7 = (bf16[384,4096]{1,0:T(8,128)(2,1)S(1)}, bf16[384,4096]{1,0:T(8,128)(2,1)}, u32[]{:S(2)}) copy-start(bf16[384,4096]{1,0:T(8,128)(2,1)} %all-gather.4.cloned.1.call-done) | copy-start | bytes 9437188
  313.8 3.1 copy-start.2
  316.5 10.9 %copy-start.3 = (bf16[16,1024]{1,0:T(8,128)(2,1)S(1)}, bf16[16,1024]{1,0:T(8,128)(2,1)}, u32[]{:S(2)}) copy-start(bf16[16,1024]{1,0:T(8,128)(2,1)} %param.7) | copy-start | bytes 98308
  316.6 52.5 %copy-start.4 = (bf16[1024,8]{0,1:T(8,128)(2,1)S(1)}, bf16[1024,8]{0,1:T(8,128)(2,1)}, u32[]{:S(2)}) copy-start(bf16[1024,8]{0,1:T(8,128)(2,1)} %param.10) | copy-start | bytes 49156
Sparse Core Ops, SparseCore 0:
  78.3 38.3 all-gather.3
  119.1 42.3 all-gather.5
  170.8 40.5 reduce-scatter.4
  213.8 40.5 reduce-scatter.2

commit v3 on v2

--- a/solution.py
+++ b/solution.py
@@ -82,6 +82,18 @@
     sigmoid_gate = jax.nn.sigmoid(pre_gate)
     activated = pre_gate * sigmoid_gate
     hidden = (activated * pre_up).astype(jnp.bfloat16)
+    hid = gate_local.shape[1]
+    down_blocks = down_local.reshape(hid, n_section, width)
+    gate_blocks = gate_local.reshape(n_section, width, hid)
+    up_blocks = up_local.reshape(n_section, width, hid)
+    out_piece = jnp.einsum("pf,fsd->spd", hidden, down_blocks, preferred_element_type=jnp.float32)
+    out_piece = out_piece.astype(jnp.bfloat16).reshape(n_section * row_total, width)
+    out_piece, dy_rows = lax.optimization_barrier((out_piece, dy_rows))
+    out_red = lax.psum_scatter(out_piece, "section", scatter_dimension=0, tiled=True)
+    n_dev = row_total // capacity
+    out_back = lax.all_to_all(out_red.reshape(n_dev, half, LANES), EXPERT_AXES, 0, 0, tiled=True)
+    out_back = out_back.reshape(experts, groups, capacity, width).astype(jnp.float32)
+    slot_out = jnp.sum(out_back, axis=1).reshape(slot_total, width)
     d_hidden = jnp.einsum("pd,fd->pf", dy_rows, down_local, preferred_element_type=jnp.float32)
     grad_down = jnp.einsum("pf,pd->fd", hidden, dy_rows, preferred_element_type=jnp.float32).astype(
         jnp.bfloat16
@@ -96,36 +108,6 @@
     grad_up = jnp.einsum("pd,pf->df", x_rows, d_pre_up, preferred_element_type=jnp.float32).astype(
         jnp.bfloat16
     )
-    hid = gate_local.shape[1]
-    down_blocks = down_local.reshape(hid, n_section, width)
-    gate_blocks = gate_local.reshape(n_section, width, hid)
-    up_blocks = up_local.reshape(n_section, width, hid)
-    out_piece = jnp.einsum("pf,fsd->spd", hidden, down_blocks, preferred_element_type=jnp.float32)
-    dx_piece = jnp.einsum("pf,sdf->spd", d_pre_gate, gate_blocks, preferred_element_type=jnp.float32)
-    dx_piece = dx_piece + jnp.einsum(
-        "pf,sdf->spd", d_pre_up, up_blocks, preferred_element_type=jnp.float32
-    )
-    out_red = lax.psum_scatter(
-        out_piece.astype(jnp.bfloat16).reshape(n_section * row_total, width),
-        "section",
-        scatter_dimension=0,
-        tiled=True,
-    )
-    dx_red = lax.psum_scatter(
-        dx_piece.astype(jnp.bfloat16).reshape(n_section * row_total, width),
-        "section",
-        scatter_dimension=0,
-        tiled=True,
-    )
-    n_dev = row_total // capacity
-    back = jnp.stack(
-        [out_red.reshape(n_dev, half, LANES), dx_red.reshape(n_dev, half, LANES)], axis=1
-    ).reshape(n_dev, block_rows, LANES)
-    returned = lax.all_to_all(back, EXPERT_AXES, 0, 0, tiled=True)
-    returned = returned.reshape(experts, groups, 2, capacity, width).astype(jnp.float32)
-    folded = jnp.sum(returned, axis=1)
-    slot_out = folded[:, 0].reshape(slot_total, width)
-    slot_dx = folded[:, 1].reshape(slot_total, width)
     first_float = pick_first.astype(jnp.float32)
     second_float = pick_second.astype(jnp.float32)
     out_first = jnp.dot(first_float, slot_out, precision=highest)
@@ -141,6 +123,19 @@
     d_logits = jnp.where(route_hot[:, 0, :], d_first[:, None], zero_f) - jnp.where(
         route_hot[:, 1, :], d_first[:, None], zero_f
     )
+    dx_piece = jnp.einsum("pf,sdf->spd", d_pre_gate, gate_blocks, preferred_element_type=jnp.float32)
+    dx_piece = dx_piece + jnp.einsum(
+        "pf,sdf->spd", d_pre_up, up_blocks, preferred_element_type=jnp.float32
+    )
+    dx_red = lax.psum_scatter(
+        dx_piece.astype(jnp.bfloat16).reshape(n_section * row_total, width),
+        "section",
+        scatter_dimension=0,
+        tiled=True,
+    )
+    dx_back = lax.all_to_all(dx_red.reshape(n_dev, half, LANES), EXPERT_AXES, 0, 0, tiled=True)
+    dx_back = dx_back.reshape(experts, groups, capacity, width).astype(jnp.float32)
+    slot_dx = jnp.sum(dx_back, axis=1).reshape(slot_total, width)
     dx_expert = jnp.dot(first_float, slot_dx, precision=highest)
     dx_expert = dx_expert + jnp.dot(second_float, slot_dx, precision=highest)
     router_float = w_router.astype(jnp.float32)

time: 377 us -> 337 us (0.89)
  waiting for transfers between devices: 181 us -> 127 us
  starting transfers between devices: 11 us -> 21.2 us
    all_to_all x1 -> x2, waiting for transfers between devices: 29.5 us -> 0.01 us  [the longest x1 0.01 us: per_device(): lax.all_to_all(out_red.reshape(n_dev, half, LANES), EXPERT_AXES, 0, 0, ti...]
    all_to_all x1 -> x2, starting transfers between devices: 10.8 us -> 21.1 us  [the longest x1 10.6 us: per_device(): lax.all_to_all(out_red.reshape(n_dev, half, LANES), EXPERT_AXES, 0, 0, ti...]
    reduce_scatter x1, waiting for transfers between devices: 31.2 us -> 22.9 us  [per_device(): lax.psum_scatter(dx_piece.astype(jnp.bfloat16).reshape(n_section * row_to...]
    reduce_scatter x1, waiting for transfers between devices: 41.6 us -> 35.4 us  [per_device(): lax.psum_scatter(out_piece, 'section', scatter_dimension=0, tiled=True)]
    all_gather x1, waiting for transfers between devices: 41.2 us -> 36.1 us  [per_device(): dy_rows = lax.all_gather(dy_recv, 'section', axis=1, tiled=True)]
    all_gather x1, waiting for transfers between devices: 37.2 us -> 32.7 us  [per_device(): x_rows = lax.all_gather(x_recv, 'section', axis=1, tiled=True)]
    reshape x0 -> x4, local copies, waits for them, and re-layouts: none -> 4.36 us  [the longest x1 2.15 us: per_device(): dx_red.reshape(n_dev, half, LANES)]
  transfers between devices with their start and end apart: 5 -> 6, of which waited for: 5 -> 4; matrix products, arithmetic and copies ran while one was open for 7% -> 13% of each run, Pallas kernels for 0% -> 0%
where the time goes in v3:
time: 337 us; the launch traced here: 336 us
  waiting for transfers between devices  127 us (38%)
  blocking collectives  111 us (33%)
  matrix products  34.1 us (10%)
  local copies, waits for them, and re-layouts  21.3 us (6%)
  starting transfers between devices  21.2 us (6%)
  between operations  14 us (4%)
  other arithmetic  6.52 us (2%)
    all_to_all x1, blocking collectives, per_device(): received = lax.all_to_all(sent, EXPERT_AXES, 0, 0, tiled=True)  50 us
    all_gather x2, blocking collectives, per_device(): router_part = jnp.sum(lax.all_gather(router_part, name, axis=0), axis=0)  38.3 us
    all_gather x1, waiting for transfers between devices, per_device(): dy_rows = lax.all_gather(dy_recv, 'section', axis=1, tiled=True)  36.1 us
    reduce_scatter x1, waiting for transfers between devices, per_device(): lax.psum_scatter(out_piece, 'section', scatter_dimension=0, tiled=True)  35.4 us
    all_gather x1, waiting for transfers between devices, per_device(): x_rows = lax.all_gather(x_recv, 'section', axis=1, tiled=True)  32.7 us
    reduce_scatter x1, waiting for transfers between devices, per_device(): lax.psum_scatter(dx_piece.astype(jnp.bfloat16).reshape(n_section * row_to...  22.9 us
    all_to_all x1, starting transfers between devices, per_device(): lax.all_to_all(out_red.reshape(n_dev, half, LANES), EXPERT_AXES, 0, 0, ti...  10.6 us
    all_to_all x1, starting transfers between devices, per_device(): lax.all_to_all(dx_red.reshape(n_dev, half, LANES), EXPERT_AXES, 0, 0, til...  10.4 us
  transfers between devices with their start and end apart: 6, of which 4 were waited for; matrix products, arithmetic and copies ran while one was open for 13% of the time, Pallas kernels for 0%

profile of v3, /device:TPU:8, one launch (start us, length us, event | category | flops | bytes accessed | tf_op | source)
XLA Modules:
  0.0 335.6 jit_solution(261256658480862980)
XLA Ops:
  7.2 0.0 all-gather.4.cloned.1.call-start
  7.2 1.0 fusion.47
  8.3 9.9 %psum.21 = f32[16,8]{0,1:T(8,128)S(1)} all-reduce(f32[16,8]{0,1:T(8,128)S(1)} %fusion.47), channel_id=1, replica_groups=mesh['section'=4,'ex'=4,'ez'=8,'ec'=2] {'section'}, use_global_device_ids=true, to_apply=%region_0.0 | all-reduce | flops 128 | bytes 1024 | tf_op jit(solution)/shard_map/psum | solution.py:29
  18.1 0.8 copy.35
  18.9 0.7 select_reduce_fusion.1
  19.6 0.1 eq.55
  19.7 0.1 fusion.26
  19.8 0.1 reduce_window_sum.11
  19.8 0.2 select_reduce_fusion
  20.0 0.1 reshape.54
  20.1 0.1 copy.36
  20.2 0.7 multiply_add_fusion
  20.9 1.0 convolution_convert_fusion.4
  21.9 0.1 stack_reshape.8
  22.0 1.0 fusion.22
  23.1 1.0 fusion.10
  24.1 0.1 stack_reshape.9
  24.2 0.5 pad_maximum_fusion
  24.6 0.1 broadcast_in_dim.58
  24.8 0.2 broadcast_in_dim.59
  25.0 50.0 %all_to_all.15 = bf16[64,96,128]{2,1,0:T(8,128)(2,1)S(1)} all-to-all(bf16[64,96,128]{2,1,0:T(8,128)(2,1)S(1)} %bitcast.91), channel_id=1, replica_groups=mesh['section'=4,'ex'=4,'ez'=8,'ec'=2] {'ex','ez','ec'}, dimensions={0} | all-to-all | bytes 3145728 | tf_op jit(solution)/shard_map/all_to_all | solution.py:70
  75.0 1.0 fusion.46
  76.0 2.1 reshape.56
  78.2 0.0 all-gather.4.cloned.1.call-update
  78.2 0.0 all-gather.6.cloned.1.call-start
  78.2 1.2 reshape.58
  79.5 0.0 all-gather.6.cloned.1.call-update
  79.5 0.0 reduce-scatter.3.cloned.1.call-start
  79.5 4.5 %reshape_squeeze.9 = bf16[256,4,1024]{2,1,0:T(4,128)(2,1)} reshape(bf16[1,256,4096]{2,1,0:T(8,128)(2,1)} %param.13) | data formatting | bytes 4194304 | tf_op jit(solution)/shard_map/reshape;squeeze | solution.py:86
  84.0 32.7 %all-gather.4.cloned.1.call-done = bf16[384,4096]{1,0:T(8,128)(2,1)} async-done(((bf16[384,1024]{1,0:T(8,128)(2,1)}), bf16[384,4096]{1,0:T(8,128)(2,1)}) %all-gather.4.cloned.1.call-update) | async-done | bytes 3145744 | tf_op jit(solution)/shard_map/all_gather | solution.py:75
  116.7 3.7 %fusion.7 = f32[384,256]{1,0:T(8,128)S(1)} fusion(bf16[384,4096]{1,0:T(8,128)(2,1)} %all-gather.4.cloned.1.call-done, bf16[1,4096,256]{2,1,0:T(8,128)(2,1)} %param.11), kind=kOutput, calls=%fused_computation.12 | convolution fusion | flops 805306368 | bytes 5636096 | tf_op jit(solution)/shard_map/dot_general | solution.py:80
  120.4 1.0 multiply_convert_fusion.2
  121.4 0.6 copy-done.1
  122.0 3.3 convolution_convert_fusion.3
  125.4 36.1 %all-gather.6.cloned.1.call-done = bf16[384,4096]{1,0:T(8,128)(2,1)} async-done(((bf16[384,1024]{1,0:T(8,128)(2,1)}), bf16[384,4096]{1,0:T(8,128)(2,1)}) %all-gather.6.cloned.1.call-update) | async-done | bytes 3145744 | tf_op jit(solution)/shard_map/all_gather | solution.py:76
  161.5 0.0 reduce-scatter.5.cloned.1.call-start
  161.6 3.7 %multiply_convert_fusion = (bf16[384,256]{1,0:T(8,128)(2,1)S(1)}, bf16[384,256]{1,0:T(8,128)(2,1)S(1)}) fusion(f32[384,256]{1,0:T(8,128)S(1)} %fusion.7, f32[384,256]{1,0:T(8,128)S(1)} %get-tuple-element.22, bf16[384,4096]{1,0:T(8,128)(2,1)} %all-gather.6.cloned.1.call-done, bf16[1,256,4096]{2,1,0:T(8,128)(2,1)} %param.13), kind=kOutput, calls=%fused_computation.22 | convolution fusion | flops 806584320 | bytes 6422528 | tf_op jit(solution)/shard_map/pd,fd->pf/dot_general | solution.py:97
  165.3 1.0 fusion.14
  166.3 2.9 add_convert_fusion
  169.2 35.4 %reduce-scatter.3.cloned.1.call-done = bf16[384,1024]{1,0:T(8,128)(2,1)} async-done(((bf16[1536,1024]{1,0:T(8,128)(2,1)}), bf16[384,1024]{1,0:T(8,128)(2,1)}) %reduce-scatter.3.cloned.1.call-update) | async-done | bytes 786448 | tf_op jit(solution)/shard_map/reduce_scatter | solution.py:92
  204.6 2.1 reshape.59
  206.8 10.6 %all-to-all-start.1 = ((bf16[64,48,128]{2,1,0:T(8,128)(2,1)}), bf16[64,48,128]{2,1,0:T(8,128)(2,1)S(1)}, u32[]{:S(2)}, u32[]{:S(2)}) async-start(bf16[64,48,128]{2,1,0:T(8,128)(2,1)} %reshape.59), calls=%async_computation.2 | async-start | bytes 1572864 | tf_op jit(solution)/shard_map/all_to_all | solution.py:94
  217.4 4.7 %fusion.2 = bf16[1,256,4096]{2,1,0:T(8,128)(2,1)} fusion(bf16[384,256]{1,0:T(8,128)(2,1)S(1)} %get-tuple-element.21, bf16[384,4096]{1,0:T(8,128)(2,1)} %all-gather.6.cloned.1.call-done), kind=kOutput, calls=%fused_computation.6 | convolution fusion | flops 806354944 | bytes 5439488 | tf_op jit(solution)/shard_map/pf,pd->fd/dot_general | solution.py:98
  222.1 2.6 fusion.1
  224.7 22.9 %reduce-scatter.5.cloned.1.call-done = bf16[384,1024]{1,0:T(8,128)(2,1)} async-done(((bf16[1536,1024]{1,0:T(8,128)(2,1)}), bf16[384,1024]{1,0:T(8,128)(2,1)}) %reduce-scatter.5.cloned.1.call-update) | async-done | bytes 786448 | tf_op jit(solution)/shard_map/reduce_scatter | solution.py:130
  247.6 2.2 reshape.62
  249.8 0.9 copy-done.2
  250.7 10.4 %all-to-all-start.2 = ((bf16[64,48,128]{2,1,0:T(8,128)(2,1)}), bf16[64,48,128]{2,1,0:T(8,128)(2,1)S(1)}, u32[]{:S(2)}, u32[]{:S(2)}) async-start(bf16[64,48,128]{2,1,0:T(8,128)(2,1)} %reshape.62), calls=%async_computation.4 | async-start | bytes 1572864 | tf_op jit(solution)/shard_map/all_to_all | solution.py:136
  261.1 4.5 %fusion = bf16[1,4096,256]{2,1,0:T(8,128)(2,1)} fusion(bf16[384,4096]{1,0:T(8,128)(2,1)} %all-gather.4.cloned.1.call-done, bf16[384,256]{1,0:T(8,128)(2,1)S(1)} %get-tuple-element.15), kind=kOutput, calls=%fused_computation.4 | convolution fusion | flops 806354944 | bytes 5439488 | tf_op jit(solution)/shard_map/pd,pf->df/dot_general | solution.py:105
  265.6 2.9 reshape.64
  268.5 1.8 reduce_sum.74
  270.4 0.2 fusion.27
  270.6 1.0 fusion.19
  271.6 9.5 %psum.22 = f32[16,2]{0,1:T(2,128)S(1)} all-reduce(f32[16,2]{0,1:T(2,128)S(1)} %pad_maximum_fusion.1), channel_id=1, replica_groups=mesh['section'=4,'ex'=4,'ez'=8,'ec'=2] {'section'}, use_global_device_ids=true, to_apply=%region_10.11 | all-reduce | flops 32 | bytes 256 | tf_op jit(solution)/shard_map/psum | solution.py:121
  281.2 0.1 convolution_bitcast_fusion
  281.3 3.4 %psum.23 = f32[1,8,1024]{2,1,0:T(8,128)S(1)} all-reduce(f32[1,8,1024]{2,1,0:T(8,128)S(1)} %convolution_bitcast_fusion), channel_id=1, replica_groups=mesh['section'=4,'ex'=4,'ez'=8,'ec'=2] {'ec'}, use_global_device_ids=true, to_apply=%region_11.12 | all-reduce | flops 8192 | bytes 65536 | tf_op jit(solution)/shard_map/psum | solution.py:148
  284.7 25.9 %all_gather.21 = f32[8,8,1024]{2,1,0:T(8,128)S(1)} all-gather(f32[1,8,1024]{2,1,0:T(8,128)S(1)} %psum.23), channel_id=1, replica_groups=mesh['section'=4,'ex'=4,'ez'=8,'ec'=2] {'ez'}, dimensions={0}, use_global_device_ids=true | all-gather | bytes 294912 | tf_op jit(solution)/shard_map/all_gather | solution.py:150
  310.6 12.4 %all-gather = f32[32,1024]{1,0:T(8,128)S(1)} all-gather(f32[8,1024]{1,0:T(8,128)S(1)} %reduce_sum.78), channel_id=2, replica_groups=mesh['section'=4,'ex'=4,'ez'=8,'ec'=2] {'ex'}, dimensions={0}, use_global_device_ids=true | all-gather | bytes 163840 | tf_op jit(solution)/shard_map/all_gather | solution.py:150
  323.0 0.6 bitcast_reduce_fusion
  323.7 2.2 reshape.65
  325.8 1.8 reduce_sum.75
  327.7 0.2 fusion.29
  327.9 0.2 convolution_add_fusion.2
  328.2 0.8 fusion.11
  (30 shorter events, 0.2 us)
Async XLA Ops:
  7.2 113.2 %copy-start = (bf16[1,4096,256]{2,1,0:T(8,128)(2,1)S(1)}, bf16[1,4096,256]{2,1,0:T(8,128)(2,1)}, u32[]{:S(2)}) copy-start(bf16[1,4096,256]{2,1,0:T(8,128)(2,1)} %param.12) | copy-start | bytes 6291460
  7.2 109.6 %all-gather.4.cloned.1.call-start = ((), (), s32[]{:S(2)}) async-start(), calls=%async_computation.5 | async-start | bytes 3932160 | tf_op jit(solution)/shard_map/all_gather | solution.py:75
  78.2 83.3 %all-gather.6.cloned.1.call-start = ((), (), s32[]{:S(2)}) async-start(), calls=%async_computation.6 | async-start | bytes 3932160 | tf_op jit(solution)/shard_map/all_gather | solution.py:76
  79.5 125.2 %reduce-scatter.3.cloned.1.call-start = ((), (), s32[]{:S(2)}) async-start(), calls=%async_computation.7 | async-start | bytes 3932160 | tf_op jit(solution)/shard_map/reduce_scatter | solution.py:92
  116.7 3.7 %copy-start.8 = (bf16[384,4096]{1,0:T(8,128)(2,1)S(1)}, bf16[384,4096]{1,0:T(8,128)(2,1)}, u32[]{:S(2)}) copy-start(bf16[384,4096]{1,0:T(8,128)(2,1)} %all-gather.4.cloned.1.call-done) | copy-start | bytes 9437188
  120.4 1.6 copy-start.1
  161.5 86.2 %reduce-scatter.5.cloned.1.call-start = ((), (), s32[]{:S(2)}) async-start(), calls=%async_computation.8 | async-start | bytes 3932160 | tf_op jit(solution)/shard_map/reduce_scatter | solution.py:130
  161.5 3.7 %copy-start.3 = (bf16[1,4096,256]{2,1,0:T(8,128)(2,1)S(1)}, bf16[1,4096,256]{2,1,0:T(8,128)(2,1)}, u32[]{:S(2)}) copy-start(bf16[1,4096,256]{2,1,0:T(8,128)(2,1)} %param.11) | copy-start | bytes 6291460
  169.2 48.2 %copy-start.7 = (s32[16,2]{0,1:T(2,128)S(1)}, s32[16,2]{0,1:T(2,128)}, u32[]{:S(2)}) copy-start(s32[16,2]{0,1:T(2,128)} %param.9) | copy-start | bytes 388
  206.8 43.0 %all-to-all-start.1 = ((bf16[64,48,128]{2,1,0:T(8,128)(2,1)}), bf16[64,48,128]{2,1,0:T(8,128)(2,1)S(1)}, u32[]{:S(2)}, u32[]{:S(2)}) async-start(bf16[64,48,128]{2,1,0:T(8,128)(2,1)} %reshape.59), calls=%async_computation.2 | async-start | bytes 1572864 | tf_op jit(solution)/shard_map/all_to_all | solution.py:94
  217.4 4.7 %copy-start.9 = (bf16[384,4096]{1,0:T(8,128)(2,1)S(1)}, bf16[384,4096]{1,0:T(8,128)(2,1)}, u32[]{:S(2)}) copy-start(bf16[384,4096]{1,0:T(8,128)(2,1)} %all-gather.4.cloned.1.call-done) | copy-start | bytes 9437188
  249.8 0.9 copy-start.2
  250.7 73.0 %all-to-all-start.2 = ((bf16[64,48,128]{2,1,0:T(8,128)(2,1)}), bf16[64,48,128]{2,1,0:T(8,128)(2,1)S(1)}, u32[]{:S(2)}, u32[]{:S(2)}) async-start(bf16[64,48,128]{2,1,0:T(8,128)(2,1)} %reshape.62), calls=%async_computation.4 | async-start | bytes 1572864 | tf_op jit(solution)/shard_map/all_to_all | solution.py:136
  268.5 2.1 copy-start.4
  268.5 12.6 %copy-start.5 = (bf16[16,1024]{1,0:T(8,128)(2,1)S(1)}, bf16[16,1024]{1,0:T(8,128)(2,1)}, u32[]{:S(2)}) copy-start(bf16[16,1024]{1,0:T(8,128)(2,1)} %param.7) | copy-start | bytes 98308
  325.8 2.3 copy-start.6
Sparse Core Ops, SparseCore 0:
  78.3 38.3 all-gather.3
  119.1 42.3 all-gather.5
  164.0 40.5 reduce-scatter.2
  207.0 40.5 reduce-scatter.4

commit v4 on v3

--- a/solution.py
+++ b/solution.py
@@ -118,11 +118,6 @@
     local_inner = jnp.stack(
         [jnp.sum(cot_float * out_first, axis=1), jnp.sum(cot_float * out_second, axis=1)], axis=1
     )
-    gate_inner = lax.psum(local_inner, "section")
-    d_first = gate_first * gate_second * (gate_inner[:, 0] - gate_inner[:, 1])
-    d_logits = jnp.where(route_hot[:, 0, :], d_first[:, None], zero_f) - jnp.where(
-        route_hot[:, 1, :], d_first[:, None], zero_f
-    )
     dx_piece = jnp.einsum("pf,sdf->spd", d_pre_gate, gate_blocks, preferred_element_type=jnp.float32)
     dx_piece = dx_piece + jnp.einsum(
         "pf,sdf->spd", d_pre_up, up_blocks, preferred_element_type=jnp.float32
@@ -133,7 +128,13 @@
         scatter_dimension=0,
         tiled=True,
     )
+    gate_inner = lax.psum(local_inner, "section")
+    gate_inner, dx_red = lax.optimization_barrier((gate_inner, dx_red))
     dx_back = lax.all_to_all(dx_red.reshape(n_dev, half, LANES), EXPERT_AXES, 0, 0, tiled=True)
+    d_first = gate_first * gate_second * (gate_inner[:, 0] - gate_inner[:, 1])
+    d_logits = jnp.where(route_hot[:, 0, :], d_first[:, None], zero_f) - jnp.where(
+        route_hot[:, 1, :], d_first[:, None], zero_f
+    )
     dx_back = dx_back.reshape(experts, groups, capacity, width).astype(jnp.float32)
     slot_dx = jnp.sum(dx_back, axis=1).reshape(slot_total, width)
     dx_expert = jnp.dot(first_float, slot_dx, precision=highest)

time: 337 us -> 329 us (0.976)
  starting transfers between devices: 21.2 us -> 17 us
    reduce_scatter x1, waiting for transfers between devices: 22.9 us -> 0.01 us  [per_device(): lax.psum_scatter(dx_piece.astype(jnp.bfloat16).reshape(n_section * row_to...]
    all_to_all x1, waiting for transfers between devices: 0.01 us -> 22.7 us  [per_device(): lax.all_to_all(out_red.reshape(n_dev, half, LANES), EXPERT_AXES, 0, 0, ti...]
    all_to_all x1, starting transfers between devices: 10.4 us -> 6.23 us  [per_device(): lax.all_to_all(dx_red.reshape(n_dev, half, LANES), EXPERT_AXES, 0, 0, til...]
  transfers between devices with their start and end apart: 6 -> 6, of which waited for: 4 -> 4; matrix products, arithmetic and copies ran while one was open for 13% -> 12% of each run, Pallas kernels for 0% -> 0%
where the time goes in v4:
time: 329 us; the launch traced here: 328 us
  waiting for transfers between devices  127 us (39%)
  blocking collectives  111 us (34%)
  matrix products  32.2 us (10%)
  local copies, waits for them, and re-layouts  19.7 us (6%)
  starting transfers between devices  17 us (5%)
  between operations  14 us (4%)
  other arithmetic  6.53 us (2%)
    all_to_all x1, blocking collectives, per_device(): received = lax.all_to_all(sent, EXPERT_AXES, 0, 0, tiled=True)  50 us
    all_gather x2, blocking collectives, per_device(): router_part = jnp.sum(lax.all_gather(router_part, name, axis=0), axis=0)  38.6 us
    all_gather x1, waiting for transfers between devices, per_device(): dy_rows = lax.all_gather(dy_recv, 'section', axis=1, tiled=True)  36 us
    reduce_scatter x1, waiting for transfers between devices, per_device(): lax.psum_scatter(out_piece, 'section', scatter_dimension=0, tiled=True)  35.5 us
    all_gather x1, waiting for transfers between devices, per_device(): x_rows = lax.all_gather(x_recv, 'section', axis=1, tiled=True)  32.7 us
    all_to_all x1, waiting for transfers between devices, per_device(): lax.all_to_all(out_red.reshape(n_dev, half, LANES), EXPERT_AXES, 0, 0, ti...  22.7 us
    all_to_all x1, starting transfers between devices, per_device(): lax.all_to_all(out_red.reshape(n_dev, half, LANES), EXPERT_AXES, 0, 0, ti...  10.6 us
    psum x1, blocking collectives, per_device(): logits = lax.psum(partial_logits, 'section')  9.88 us
  transfers between devices with their start and end apart: 6, of which 4 were waited for; matrix products, arithmetic and copies ran while one was open for 12% of the time, Pallas kernels for 0%

profile of v4, /device:TPU:8, one launch (start us, length us, event | category | flops | bytes accessed | tf_op | source)
XLA Modules:
  0.0 328.0 jit_solution(17537535246226794366)
XLA Ops:
  7.2 0.0 all-gather.4.cloned.1.call-start
  7.2 1.0 fusion.47
  8.2 9.9 %psum.21 = f32[16,8]{0,1:T(8,128)S(1)} all-reduce(f32[16,8]{0,1:T(8,128)S(1)} %fusion.47), channel_id=1, replica_groups=mesh['section'=4,'ex'=4,'ez'=8,'ec'=2] {'section'}, use_global_device_ids=true, to_apply=%region_0.0 | all-reduce | flops 128 | bytes 1024 | tf_op jit(solution)/shard_map/psum | solution.py:29
  18.1 0.8 copy.35
  18.9 0.7 select_reduce_fusion.1
  19.6 0.1 eq.55
  19.7 0.1 fusion.26
  19.8 0.1 reduce_window_sum.11
  19.8 0.2 select_reduce_fusion
  20.0 0.1 reshape.54
  20.1 0.1 copy.36
  20.2 0.7 multiply_add_fusion
  20.9 1.0 convolution_convert_fusion.4
  21.9 0.1 stack_reshape.8
  22.0 1.0 fusion.22
  23.1 1.0 fusion.10
  24.1 0.1 stack_reshape.9
  24.2 0.5 pad_maximum_fusion
  24.6 0.1 broadcast_in_dim.58
  24.8 0.2 broadcast_in_dim.59
  25.0 50.0 %all_to_all.15 = bf16[64,96,128]{2,1,0:T(8,128)(2,1)S(1)} all-to-all(bf16[64,96,128]{2,1,0:T(8,128)(2,1)S(1)} %bitcast.91), channel_id=1, replica_groups=mesh['section'=4,'ex'=4,'ez'=8,'ec'=2] {'ex','ez','ec'}, dimensions={0} | all-to-all | bytes 3145728 | tf_op jit(solution)/shard_map/all_to_all | solution.py:70
  75.0 1.0 fusion.46
  76.0 2.1 reshape.56
  78.2 0.0 all-gather.4.cloned.1.call-update
  78.2 0.0 all-gather.6.cloned.1.call-start
  78.2 1.2 reshape.58
  79.5 0.0 all-gather.6.cloned.1.call-update
  79.5 0.0 reduce-scatter.3.cloned.1.call-start
  79.5 4.5 %reshape_squeeze.9 = bf16[256,4,1024]{2,1,0:T(4,128)(2,1)} reshape(bf16[1,256,4096]{2,1,0:T(8,128)(2,1)} %param.13) | data formatting | bytes 4194304 | tf_op jit(solution)/shard_map/reshape;squeeze | solution.py:86
  84.0 32.7 %all-gather.4.cloned.1.call-done = bf16[384,4096]{1,0:T(8,128)(2,1)} async-done(((bf16[384,1024]{1,0:T(8,128)(2,1)}), bf16[384,4096]{1,0:T(8,128)(2,1)}) %all-gather.4.cloned.1.call-update) | async-done | bytes 3145744 | tf_op jit(solution)/shard_map/all_gather | solution.py:75
  116.7 3.7 %fusion.7 = f32[384,256]{1,0:T(8,128)S(1)} fusion(bf16[384,4096]{1,0:T(8,128)(2,1)} %all-gather.4.cloned.1.call-done, bf16[1,4096,256]{2,1,0:T(8,128)(2,1)} %param.11), kind=kOutput, calls=%fused_computation.12 | convolution fusion | flops 805306368 | bytes 5636096 | tf_op jit(solution)/shard_map/dot_general | solution.py:80
  120.4 1.0 multiply_convert_fusion.2
  121.4 0.6 copy-done.1
  122.0 3.4 %convolution_convert_fusion.3 = bf16[384,4,1024]{2,0,1:T(8,128)(2,1)} fusion(bf16[256,4,1024]{2,1,0:T(4,128)(2,1)S(1)} %copy-done.1, bf16[384,256]{1,0:T(8,128)(2,1)S(1)} %get-tuple-element.25), kind=kOutput, calls=%fused_computation.7 | convolution fusion | flops 806879232 | bytes 5439488 | tf_op jit(solution)/shard_map/pf,fsd->spd/dot_general | solution.py:89
  125.4 36.0 %all-gather.6.cloned.1.call-done = bf16[384,4096]{1,0:T(8,128)(2,1)} async-done(((bf16[384,1024]{1,0:T(8,128)(2,1)}), bf16[384,4096]{1,0:T(8,128)(2,1)}) %all-gather.6.cloned.1.call-update) | async-done | bytes 3145744 | tf_op jit(solution)/shard_map/all_gather | solution.py:76
  161.5 0.0 reduce-scatter.3.cloned.1.call-update
  161.5 0.0 reduce-scatter.5.cloned.1.call-start
  161.6 3.7 %multiply_convert_fusion = (bf16[384,256]{1,0:T(8,128)(2,1)S(1)}, bf16[384,256]{1,0:T(8,128)(2,1)S(1)}) fusion(f32[384,256]{1,0:T(8,128)S(1)} %fusion.7, f32[384,256]{1,0:T(8,128)S(1)} %get-tuple-element.26, bf16[384,4096]{1,0:T(8,128)(2,1)} %all-gather.6.cloned.1.call-done, bf16[1,256,4096]{2,1,0:T(8,128)(2,1)} %param.13), kind=kOutput, calls=%fused_computation.22 | convolution fusion | flops 806584320 | bytes 6422528 | tf_op jit(solution)/shard_map/pd,fd->pf/dot_general | solution.py:97
  165.3 1.0 fusion.14
  166.3 2.8 add_convert_fusion
  169.1 35.5 %reduce-scatter.3.cloned.1.call-done = bf16[384,1024]{1,0:T(8,128)(2,1)} async-done(((bf16[1536,1024]{1,0:T(8,128)(2,1)}), bf16[384,1024]{1,0:T(8,128)(2,1)}) %reduce-scatter.3.cloned.1.call-update) | async-done | bytes 786448 | tf_op jit(solution)/shard_map/reduce_scatter | solution.py:92
  204.6 2.1 reshape.59
  206.8 10.6 %all-to-all-start.1 = ((bf16[64,48,128]{2,1,0:T(8,128)(2,1)}), bf16[64,48,128]{2,1,0:T(8,128)(2,1)S(1)}, u32[]{:S(2)}, u32[]{:S(2)}) async-start(bf16[64,48,128]{2,1,0:T(8,128)(2,1)} %reshape.59), calls=%async_computation.2 | async-start | bytes 1572864 | tf_op jit(solution)/shard_map/all_to_all | solution.py:94
  217.4 22.7 %all-to-all-done.1 = bf16[64,48,128]{2,1,0:T(8,128)(2,1)S(1)} async-done(((bf16[64,48,128]{2,1,0:T(8,128)(2,1)}), bf16[64,48,128]{2,1,0:T(8,128)(2,1)S(1)}, u32[]{:S(2)}, u32[]{:S(2)}) %all-to-all-start.1) | async-done | bytes 786464 | tf_op jit(solution)/shard_map/all_to_all | solution.py:94
  240.2 2.1 reshape.64
  242.3 1.9 reduce_sum.74
  244.2 0.2 fusion.27
  244.4 1.0 fusion.19
  245.4 9.6 %psum.22 = f32[16,2]{0,1:T(2,128)S(1)} all-reduce(f32[16,2]{0,1:T(2,128)S(1)} %pad_maximum_fusion.1), channel_id=1, replica_groups=mesh['section'=4,'ex'=4,'ez'=8,'ec'=2] {'section'}, use_global_device_ids=true, to_apply=%region_8.9 | all-reduce | flops 32 | bytes 256 | tf_op jit(solution)/shard_map/psum | solution.py:131
  255.0 2.2 reshape.62
  257.1 6.2 %all-to-all-start.2 = ((bf16[64,48,128]{2,1,0:T(8,128)(2,1)}), bf16[64,48,128]{2,1,0:T(8,128)(2,1)S(1)}, u32[]{:S(2)}, u32[]{:S(2)}) async-start(bf16[64,48,128]{2,1,0:T(8,128)(2,1)} %reshape.62), calls=%async_computation.4 | async-start | bytes 1572864 | tf_op jit(solution)/shard_map/all_to_all | solution.py:133
  263.4 4.6 %fusion.2 = bf16[1,256,4096]{2,1,0:T(8,128)(2,1)} fusion(bf16[384,256]{1,0:T(8,128)(2,1)S(1)} %get-tuple-element.25, bf16[384,4096]{1,0:T(8,128)(2,1)} %all-gather.6.cloned.1.call-done), kind=kOutput, calls=%fused_computation.6 | convolution fusion | flops 806354944 | bytes 5439488 | tf_op jit(solution)/shard_map/pf,pd->fd/dot_general | solution.py:98
  268.0 2.6 fusion.1
  270.6 2.6 fusion
  273.3 0.1 convolution_bitcast_fusion
  273.4 3.4 %psum.23 = f32[1,8,1024]{2,1,0:T(8,128)S(1)} all-reduce(f32[1,8,1024]{2,1,0:T(8,128)S(1)} %convolution_bitcast_fusion), channel_id=1, replica_groups=mesh['section'=4,'ex'=4,'ez'=8,'ec'=2] {'ec'}, use_global_device_ids=true, to_apply=%region_11.12 | all-reduce | flops 8192 | bytes 65536 | tf_op jit(solution)/shard_map/psum | solution.py:149
  276.8 26.2 %all_gather.21 = f32[8,8,1024]{2,1,0:T(8,128)S(1)} all-gather(f32[1,8,1024]{2,1,0:T(8,128)S(1)} %psum.23), channel_id=1, replica_groups=mesh['section'=4,'ex'=4,'ez'=8,'ec'=2] {'ez'}, dimensions={0}, use_global_device_ids=true | all-gather | bytes 294912 | tf_op jit(solution)/shard_map/all_gather | solution.py:151
  303.0 12.4 %all-gather = f32[32,1024]{1,0:T(8,128)S(1)} all-gather(f32[8,1024]{1,0:T(8,128)S(1)} %reduce_sum.78), channel_id=2, replica_groups=mesh['section'=4,'ex'=4,'ez'=8,'ec'=2] {'ex'}, dimensions={0}, use_global_device_ids=true | all-gather | bytes 163840 | tf_op jit(solution)/shard_map/all_gather | solution.py:151
  315.5 0.6 bitcast_reduce_fusion
  316.1 2.2 reshape.65
  318.3 1.8 reduce_sum.77
  320.1 0.2 fusion.29
  320.4 0.2 convolution_add_fusion.2
  320.6 0.8 fusion.11
  (28 shorter events, 0.2 us)
Async XLA Ops:
  7.2 113.2 %copy-start = (bf16[1,4096,256]{2,1,0:T(8,128)(2,1)S(1)}, bf16[1,4096,256]{2,1,0:T(8,128)(2,1)}, u32[]{:S(2)}) copy-start(bf16[1,4096,256]{2,1,0:T(8,128)(2,1)} %param.12) | copy-start | bytes 6291460
  7.2 109.6 %all-gather.4.cloned.1.call-start = ((), (), s32[]{:S(2)}) async-start(), calls=%async_computation.5 | async-start | bytes 3932160 | tf_op jit(solution)/shard_map/all_gather | solution.py:75
  78.2 83.3 %all-gather.6.cloned.1.call-start = ((), (), s32[]{:S(2)}) async-start(), calls=%async_computation.6 | async-start | bytes 3932160 | tf_op jit(solution)/shard_map/all_gather | solution.py:76
  79.5 125.2 %reduce-scatter.3.cloned.1.call-start = ((), (), s32[]{:S(2)}) async-start(), calls=%async_computation.7 | async-start | bytes 3932160 | tf_op jit(solution)/shard_map/reduce_scatter | solution.py:92
  116.7 3.7 %copy-start.7 = (bf16[384,4096]{1,0:T(8,128)(2,1)S(1)}, bf16[384,4096]{1,0:T(8,128)(2,1)}, u32[]{:S(2)}) copy-start(bf16[384,4096]{1,0:T(8,128)(2,1)} %all-gather.4.cloned.1.call-done) | copy-start | bytes 9437188
  120.4 1.6 copy-start.1
  161.5 93.5 %reduce-scatter.5.cloned.1.call-start = ((), (), s32[]{:S(2)}) async-start(), calls=%async_computation.8 | async-start | bytes 3932160 | tf_op jit(solution)/shard_map/reduce_scatter | solution.py:125
  161.5 3.7 %copy-start.2 = (bf16[1,4096,256]{2,1,0:T(8,128)(2,1)S(1)}, bf16[1,4096,256]{2,1,0:T(8,128)(2,1)}, u32[]{:S(2)}) copy-start(bf16[1,4096,256]{2,1,0:T(8,128)(2,1)} %param.11) | copy-start | bytes 6291460
  169.1 48.3 %copy-start.6 = (s32[16,2]{0,1:T(2,128)S(1)}, s32[16,2]{0,1:T(2,128)}, u32[]{:S(2)}) copy-start(s32[16,2]{0,1:T(2,128)} %param.9) | copy-start | bytes 388
  206.8 33.4 %all-to-all-start.1 = ((bf16[64,48,128]{2,1,0:T(8,128)(2,1)}), bf16[64,48,128]{2,1,0:T(8,128)(2,1)S(1)}, u32[]{:S(2)}, u32[]{:S(2)}) async-start(bf16[64,48,128]{2,1,0:T(8,128)(2,1)} %reshape.59), calls=%async_computation.2 | async-start | bytes 1572864 | tf_op jit(solution)/shard_map/all_to_all | solution.py:94
  242.3 2.1 copy-start.3
  257.1 59.0 %all-to-all-start.2 = ((bf16[64,48,128]{2,1,0:T(8,128)(2,1)}), bf16[64,48,128]{2,1,0:T(8,128)(2,1)S(1)}, u32[]{:S(2)}, u32[]{:S(2)}) async-start(bf16[64,48,128]{2,1,0:T(8,128)(2,1)} %reshape.62), calls=%async_computation.4 | async-start | bytes 1572864 | tf_op jit(solution)/shard_map/all_to_all | solution.py:133
  263.4 4.6 %copy-start.8 = (bf16[384,4096]{1,0:T(8,128)(2,1)S(1)}, bf16[384,4096]{1,0:T(8,128)(2,1)}, u32[]{:S(2)}) copy-start(bf16[384,4096]{1,0:T(8,128)(2,1)} %all-gather.4.cloned.1.call-done) | copy-start | bytes 9437188
  270.6 2.6 copy-start.4
  318.3 2.3 copy-start.5
Sparse Core Ops, SparseCore 0:
  78.3 38.3 all-gather.3
  119.1 42.3 all-gather.5
  164.0 40.5 reduce-scatter.2
  207.0 40.5 reduce-scatter.4

commit v5 on v4

--- a/solution.py
+++ b/solution.py
@@ -73,7 +73,6 @@
     x_recv = received[:, :half].reshape(row_total, width)
     dy_recv = received[:, half:].reshape(row_total, width)
     x_rows = lax.all_gather(x_recv, "section", axis=1, tiled=True)
-    dy_rows = lax.all_gather(dy_recv, "section", axis=1, tiled=True)
     gate_local = w_gate[0]
     up_local = w_up[0]
     down_local = w_down[0]
@@ -88,8 +87,9 @@
     up_blocks = up_local.reshape(n_section, width, hid)
     out_piece = jnp.einsum("pf,fsd->spd", hidden, down_blocks, preferred_element_type=jnp.float32)
     out_piece = out_piece.astype(jnp.bfloat16).reshape(n_section * row_total, width)
-    out_piece, dy_rows = lax.optimization_barrier((out_piece, dy_rows))
     out_red = lax.psum_scatter(out_piece, "section", scatter_dimension=0, tiled=True)
+    out_red, dy_recv = lax.optimization_barrier((out_red, dy_recv))
+    dy_rows = lax.all_gather(dy_recv, "section", axis=1, tiled=True)
     n_dev = row_total // capacity
     out_back = lax.all_to_all(out_red.reshape(n_dev, half, LANES), EXPERT_AXES, 0, 0, tiled=True)
     out_back = out_back.reshape(experts, groups, capacity, width).astype(jnp.float32)
@@ -122,19 +122,22 @@
     dx_piece = dx_piece + jnp.einsum(
         "pf,sdf->spd", d_pre_up, up_blocks, preferred_element_type=jnp.float32
     )
-    dx_red = lax.psum_scatter(
-        dx_piece.astype(jnp.bfloat16).reshape(n_section * row_total, width),
-        "section",
-        scatter_dimension=0,
-        tiled=True,
-    )
     gate_inner = lax.psum(local_inner, "section")
-    gate_inner, dx_red = lax.optimization_barrier((gate_inner, dx_red))
-    dx_back = lax.all_to_all(dx_red.reshape(n_dev, half, LANES), EXPERT_AXES, 0, 0, tiled=True)
     d_first = gate_first * gate_second * (gate_inner[:, 0] - gate_inner[:, 1])
     d_logits = jnp.where(route_hot[:, 0, :], d_first[:, None], zero_f) - jnp.where(
         route_hot[:, 1, :], d_first[:, None], zero_f
     )
+    dx_piece = dx_piece.astype(jnp.bfloat16).reshape(n_section * row_total, width)
+    d_logits, dx_piece = lax.optimization_barrier((d_logits, dx_piece))
+    dx_red = lax.psum_scatter(dx_piece, "section", scatter_dimension=0, tiled=True)
+    router_part = jnp.einsum(
+        "te,tf->ef", d_logits, tokens.astype(jnp.float32), precision=highest
+    )
+    router_part = lax.psum(router_part, EXPERT_AXES[2])
+    for name in (EXPERT_AXES[1], EXPERT_AXES[0]):
+        router_part = jnp.sum(lax.all_gather(router_part, name, axis=0), axis=0)
+    router_part, dx_red = lax.optimization_barrier((router_part, dx_red))
+    dx_back = lax.all_to_all(dx_red.reshape(n_dev, half, LANES), EXPERT_AXES, 0, 0, tiled=True)
     dx_back = dx_back.reshape(experts, groups, capacity, width).astype(jnp.float32)
     slot_dx = jnp.sum(dx_back, axis=1).reshape(slot_total, width)
     dx_expert = jnp.dot(first_float, slot_dx, precision=highest)
@@ -143,12 +146,6 @@
     grad_tokens = (dx_expert + jnp.dot(d_logits, router_float.T, precision=highest)).astype(
         jnp.bfloat16
     )
-    router_part = jnp.einsum(
-        "te,tf->ef", d_logits, tokens.astype(jnp.float32), precision=highest
-    )
-    router_part = lax.psum(router_part, EXPERT_AXES[2])
-    for name in (EXPERT_AXES[1], EXPERT_AXES[0]):
-        router_part = jnp.sum(lax.all_gather(router_part, name, axis=0), axis=0)
     grad_router = router_part.T
     return (mixed, grad_tokens, grad_router, grad_gate[None], grad_up[None], grad_down[None])
 

time: 329 us -> 312 us (0.948)
  waiting for transfers between devices: 127 us -> 109 us
    all_gather x1, waiting for transfers between devices: 36 us -> 0.02 us  [per_device(): dy_rows = lax.all_gather(dy_recv, 'section', axis=1, tiled=True)]
    all_to_all x1, waiting for transfers between devices: 0.01 us -> 13 us  [per_device(): lax.all_to_all(dx_red.reshape(n_dev, half, LANES), EXPERT_AXES, 0, 0, til...]
    reduce_scatter x1, waiting for transfers between devices: 35.5 us -> 39.5 us  [per_device(): lax.psum_scatter(out_piece, 'section', scatter_dimension=0, tiled=True)]
  transfers between devices with their start and end apart: 6 -> 6, of which waited for: 4 -> 4; matrix products, arithmetic and copies ran while one was open for 12% -> 8% of each run, Pallas kernels for 0% -> 0%
where the time goes in v5:
time: 312 us; the launch traced here: 310 us
  blocking collectives  110 us (35%)
  waiting for transfers between devices  109 us (35%)
  matrix products  33.2 us (11%)
  local copies, waits for them, and re-layouts  19.8 us (6%)
  starting transfers between devices  16.7 us (5%)
  between operations  14 us (4%)
  other arithmetic  6.52 us (2%)
    all_to_all x1, blocking collectives, per_device(): received = lax.all_to_all(sent, EXPERT_AXES, 0, 0, tiled=True)  50 us
    reduce_scatter x1, waiting for transfers between devices, per_device(): lax.psum_scatter(out_piece, 'section', scatter_dimension=0, tiled=True)  39.5 us
    all_gather x2, blocking collectives, per_device(): router_part = jnp.sum(lax.all_gather(router_part, name, axis=0), axis=0)  36.9 us
    all_gather x1, waiting for transfers between devices, per_device(): x_rows = lax.all_gather(x_recv, 'section', axis=1, tiled=True)  34 us
    all_to_all x1, waiting for transfers between devices, per_device(): lax.all_to_all(out_red.reshape(n_dev, half, LANES), EXPERT_AXES, 0, 0, ti...  22.9 us
    all_to_all x1, waiting for transfers between devices, per_device(): lax.all_to_all(dx_red.reshape(n_dev, half, LANES), EXPERT_AXES, 0, 0, til...  13 us
    all_to_all x1, starting transfers between devices, per_device(): lax.all_to_all(out_red.reshape(n_dev, half, LANES), EXPERT_AXES, 0, 0, ti...  10.4 us
    psum x1, blocking collectives, per_device(): logits = lax.psum(partial_logits, 'section')  9.88 us
  transfers between devices with their start and end apart: 6, of which 4 were waited for; matrix products, arithmetic and copies ran while one was open for 8% of the time, Pallas kernels for 0%

profile of v5, /device:TPU:8, one launch (start us, length us, event | category | flops | bytes accessed | tf_op | source)
XLA Modules:
  0.0 309.6 jit_solution(4701261076263927448)
XLA Ops:
  7.2 0.0 all-gather.4.cloned.1.call-start
  7.2 1.0 fusion.41
  8.2 9.9 %psum.21 = f32[16,8]{0,1:T(8,128)S(1)} all-reduce(f32[16,8]{0,1:T(8,128)S(1)} %fusion.41), channel_id=1, replica_groups=mesh['section'=4,'ex'=4,'ez'=8,'ec'=2] {'section'}, use_global_device_ids=true, to_apply=%region_0.0 | all-reduce | flops 128 | bytes 1024 | tf_op jit(solution)/shard_map/psum | solution.py:29
  18.1 0.8 copy.35
  18.9 0.7 select_reduce_fusion.1
  19.6 0.1 eq.55
  19.7 0.1 fusion.26
  19.8 0.1 reduce_window_sum.11
  19.8 0.2 select_reduce_fusion
  20.0 0.1 reshape.54
  20.1 0.1 copy.36
  20.2 0.7 multiply_add_fusion
  20.9 1.0 convolution_convert_fusion.4
  21.9 0.1 stack_reshape.8
  22.0 1.0 fusion.22
  23.1 1.0 fusion.10
  24.1 0.1 stack_reshape.9
  24.2 0.5 pad_maximum_fusion
  24.6 0.1 broadcast_in_dim.58
  24.8 0.2 broadcast_in_dim.59
  25.0 50.0 %all_to_all.15 = bf16[64,96,128]{2,1,0:T(8,128)(2,1)S(1)} all-to-all(bf16[64,96,128]{2,1,0:T(8,128)(2,1)S(1)} %bitcast.85), channel_id=1, replica_groups=mesh['section'=4,'ex'=4,'ez'=8,'ec'=2] {'ex','ez','ec'}, dimensions={0} | all-to-all | bytes 3145728 | tf_op jit(solution)/shard_map/all_to_all | solution.py:70
  75.0 1.0 fusion.40
  76.0 2.1 reshape.56
  78.2 0.0 all-gather.4.cloned.1.call-update
  78.2 0.0 reduce-scatter.3.cloned.1.call-start
  78.2 4.5 %reshape_squeeze.9 = bf16[256,4,1024]{2,1,0:T(4,128)(2,1)} reshape(bf16[1,256,4096]{2,1,0:T(8,128)(2,1)} %param.13) | data formatting | bytes 4194304 | tf_op jit(solution)/shard_map/reshape;squeeze | solution.py:85
  82.7 34.0 %all-gather.4.cloned.1.call-done = bf16[384,4096]{1,0:T(8,128)(2,1)} async-done(((bf16[384,1024]{1,0:T(8,128)(2,1)}), bf16[384,4096]{1,0:T(8,128)(2,1)}) %all-gather.4.cloned.1.call-update) | async-done | bytes 3145744 | tf_op jit(solution)/shard_map/all_gather | solution.py:75
  116.7 3.7 %fusion.7 = f32[384,256]{1,0:T(8,128)S(1)} fusion(bf16[384,4096]{1,0:T(8,128)(2,1)} %all-gather.4.cloned.1.call-done, bf16[1,4096,256]{2,1,0:T(8,128)(2,1)} %param.11), kind=kOutput, calls=%fused_computation.12 | convolution fusion | flops 805306368 | bytes 5636096 | tf_op jit(solution)/shard_map/dot_general | solution.py:79
  120.5 1.7 multiply_convert_fusion.2
  122.2 3.4 %convolution_convert_fusion.3 = bf16[384,4,1024]{2,0,1:T(8,128)(2,1)} fusion(bf16[256,4,1024]{2,1,0:T(4,128)(2,1)S(1)} %copy-done.1, bf16[384,256]{1,0:T(8,128)(2,1)S(1)} %get-tuple-element.29), kind=kOutput, calls=%fused_computation.7 | convolution fusion | flops 806879232 | bytes 5439488 | tf_op jit(solution)/shard_map/pf,fsd->spd/dot_general | solution.py:88
  125.6 0.0 all-gather.6.cloned.1.call-start
  125.7 1.2 reshape.58
  126.9 39.5 %reduce-scatter.3.cloned.1.call-done = bf16[384,1024]{1,0:T(8,128)(2,1)} async-done(((bf16[1536,1024]{1,0:T(8,128)(2,1)}), bf16[384,1024]{1,0:T(8,128)(2,1)}) %reduce-scatter.3.cloned.1.call-update) | async-done | bytes 786448 | tf_op jit(solution)/shard_map/reduce_scatter | solution.py:90
  166.4 0.0 all-gather.6.cloned.1.call-update
  166.4 2.2 reshape.59
  168.5 10.4 %all-to-all-start.1 = ((bf16[64,48,128]{2,1,0:T(8,128)(2,1)}), bf16[64,48,128]{2,1,0:T(8,128)(2,1)S(1)}, u32[]{:S(2)}, u32[]{:S(2)}) async-start(bf16[64,48,128]{2,1,0:T(8,128)(2,1)} %reshape.59), calls=%async_computation.2 | async-start | bytes 1572864 | tf_op jit(solution)/shard_map/all_to_all | solution.py:94
  179.0 0.0 reduce-scatter.5.cloned.1.call-start
  179.1 22.9 %all-to-all-done.1 = bf16[64,48,128]{2,1,0:T(8,128)(2,1)S(1)} async-done(((bf16[64,48,128]{2,1,0:T(8,128)(2,1)}), bf16[64,48,128]{2,1,0:T(8,128)(2,1)S(1)}, u32[]{:S(2)}, u32[]{:S(2)}) %all-to-all-start.1) | async-done | bytes 786464 | tf_op jit(solution)/shard_map/all_to_all | solution.py:94
  201.9 2.1 reshape.64
  204.0 1.8 reduce_sum.74
  205.9 0.2 fusion.27
  206.2 1.0 fusion.19
  207.1 9.7 %psum.22 = f32[16,2]{0,1:T(2,128)S(1)} all-reduce(f32[16,2]{0,1:T(2,128)S(1)} %pad_maximum_fusion.1), channel_id=1, replica_groups=mesh['section'=4,'ex'=4,'ez'=8,'ec'=2] {'section'}, use_global_device_ids=true, to_apply=%region_8.9 | all-reduce | flops 32 | bytes 256 | tf_op jit(solution)/shard_map/psum | solution.py:125
  216.8 0.0 all-gather.6.cloned.1.call-done
  216.9 3.9 %multiply_convert_fusion = (bf16[384,256]{1,0:T(8,128)(2,1)S(1)}, bf16[384,256]{1,0:T(8,128)(2,1)S(1)}) fusion(f32[384,256]{1,0:T(8,128)} %copy-done.9, f32[384,256]{1,0:T(8,128)} %get-tuple-element.30, bf16[384,4096]{1,0:T(8,128)(2,1)} %all-gather.6.cloned.1.call-done, bf16[1,256,4096]{2,1,0:T(8,128)(2,1)} %param.13), kind=kOutput, calls=%fused_computation.22 | convolution fusion | flops 806584320 | bytes 6422528 | tf_op jit(solution)/shard_map/pd,fd->pf/dot_general | solution.py:97
  220.7 1.0 fusion.14
  221.8 2.9 add_convert_fusion
  224.6 0.7 copy-done.4
  225.4 0.1 convolution_bitcast_fusion
  225.5 3.4 %psum.23 = f32[1,8,1024]{2,1,0:T(8,128)S(1)} all-reduce(f32[1,8,1024]{2,1,0:T(8,128)S(1)} %convolution_bitcast_fusion), channel_id=1, replica_groups=mesh['section'=4,'ex'=4,'ez'=8,'ec'=2] {'ec'}, use_global_device_ids=true, to_apply=%region_9.10 | all-reduce | flops 8192 | bytes 65536 | tf_op jit(solution)/shard_map/psum | solution.py:136
  228.9 24.9 %all_gather.21 = f32[8,8,1024]{2,1,0:T(8,128)S(1)} all-gather(f32[1,8,1024]{2,1,0:T(8,128)S(1)} %psum.23), channel_id=1, replica_groups=mesh['section'=4,'ex'=4,'ez'=8,'ec'=2] {'ez'}, dimensions={0}, use_global_device_ids=true | all-gather | bytes 294912 | tf_op jit(solution)/shard_map/all_gather | solution.py:138
  253.9 12.0 %all-gather = f32[32,1024]{1,0:T(8,128)S(1)} all-gather(f32[8,1024]{1,0:T(8,128)S(1)} %reduce_sum.77), channel_id=2, replica_groups=mesh['section'=4,'ex'=4,'ez'=8,'ec'=2] {'ex'}, dimensions={0}, use_global_device_ids=true | all-gather | bytes 163840 | tf_op jit(solution)/shard_map/all_gather | solution.py:138
  265.9 0.6 bitcast_reduce_fusion
  266.5 2.2 reshape.62
  268.7 6.1 %all-to-all-start.2 = ((bf16[64,48,128]{2,1,0:T(8,128)(2,1)}), bf16[64,48,128]{2,1,0:T(8,128)(2,1)S(1)}, u32[]{:S(2)}, u32[]{:S(2)}) async-start(bf16[64,48,128]{2,1,0:T(8,128)(2,1)} %reshape.62), calls=%async_computation.4 | async-start | bytes 1572864 | tf_op jit(solution)/shard_map/all_to_all | solution.py:140
  274.8 4.6 %fusion.2 = bf16[1,256,4096]{2,1,0:T(8,128)(2,1)} fusion(bf16[384,256]{1,0:T(8,128)(2,1)S(1)} %get-tuple-element.29, bf16[384,4096]{1,0:T(8,128)(2,1)} %all-gather.6.cloned.1.call-done), kind=kOutput, calls=%fused_computation.6 | convolution fusion | flops 806354944 | bytes 5439488 | tf_op jit(solution)/shard_map/pf,pd->fd/dot_general | solution.py:98
  279.4 2.6 fusion.1
  282.1 2.6 fusion
  284.7 13.0 %all-to-all-done.2 = bf16[64,48,128]{2,1,0:T(8,128)(2,1)S(1)} async-done(((bf16[64,48,128]{2,1,0:T(8,128)(2,1)}), bf16[64,48,128]{2,1,0:T(8,128)(2,1)S(1)}, u32[]{:S(2)}, u32[]{:S(2)}) %all-to-all-start.2) | async-done | bytes 786464 | tf_op jit(solution)/shard_map/all_to_all | solution.py:140
  297.7 2.2 reshape.65
  299.9 1.8 reduce_sum.79
  301.7 0.2 fusion.29
  302.0 0.2 convolution_add_fusion.2
  302.2 0.8 fusion.11
  (31 shorter events, 0.2 us)
Async XLA Ops:
  7.2 113.2 %copy-start = (bf16[1,4096,256]{2,1,0:T(8,128)(2,1)S(1)}, bf16[1,4096,256]{2,1,0:T(8,128)(2,1)}, u32[]{:S(2)}) copy-start(bf16[1,4096,256]{2,1,0:T(8,128)(2,1)} %param.12) | copy-start | bytes 6291460
  7.2 109.6 %all-gather.4.cloned.1.call-start = ((), (), s32[]{:S(2)}) async-start(), calls=%async_computation.5 | async-start | bytes 3932160 | tf_op jit(solution)/shard_map/all_gather | solution.py:75
  78.2 88.2 %reduce-scatter.3.cloned.1.call-start = ((), (), s32[]{:S(2)}) async-start(), calls=%async_computation.6 | async-start | bytes 3932160 | tf_op jit(solution)/shard_map/reduce_scatter | solution.py:90
  116.7 3.7 %copy-start.7 = (bf16[384,4096]{1,0:T(8,128)(2,1)S(1)}, bf16[384,4096]{1,0:T(8,128)(2,1)}, u32[]{:S(2)}) copy-start(bf16[384,4096]{1,0:T(8,128)(2,1)} %all-gather.4.cloned.1.call-done) | copy-start | bytes 9437188
  120.4 1.8 copy-start.9
  120.4 1.8 copy-start.1
  125.6 91.2 %all-gather.6.cloned.1.call-start = ((), (), s32[]{:S(2)}) async-start(), calls=%async_computation.7 | async-start | bytes 3932160 | tf_op jit(solution)/shard_map/all_gather | solution.py:92
  126.9 52.1 %copy-start.6 = (s32[16,2]{0,1:T(2,128)S(1)}, s32[16,2]{0,1:T(2,128)}, u32[]{:S(2)}) copy-start(s32[16,2]{0,1:T(2,128)} %param.9) | copy-start | bytes 388
  168.5 33.4 %all-to-all-start.1 = ((bf16[64,48,128]{2,1,0:T(8,128)(2,1)}), bf16[64,48,128]{2,1,0:T(8,128)(2,1)S(1)}, u32[]{:S(2)}, u32[]{:S(2)}) async-start(bf16[64,48,128]{2,1,0:T(8,128)(2,1)} %reshape.59), calls=%async_computation.2 | async-start | bytes 1572864 | tf_op jit(solution)/shard_map/all_to_all | solution.py:94
  179.0 87.5 %reduce-scatter.5.cloned.1.call-start = ((), (), s32[]{:S(2)}) async-start(), calls=%async_computation.8 | async-start | bytes 3932160 | tf_op jit(solution)/shard_map/reduce_scatter | solution.py:132
  204.0 2.1 copy-start.3
  216.9 3.9 %copy-start.2 = (bf16[1,4096,256]{2,1,0:T(8,128)(2,1)S(1)}, bf16[1,4096,256]{2,1,0:T(8,128)(2,1)}, u32[]{:S(2)}) copy-start(bf16[1,4096,256]{2,1,0:T(8,128)(2,1)} %param.11) | copy-start | bytes 6291460
  224.6 0.8 copy-start.4
  268.7 29.0 %all-to-all-start.2 = ((bf16[64,48,128]{2,1,0:T(8,128)(2,1)}), bf16[64,48,128]{2,1,0:T(8,128)(2,1)S(1)}, u32[]{:S(2)}, u32[]{:S(2)}) async-start(bf16[64,48,128]{2,1,0:T(8,128)(2,1)} %reshape.62), calls=%async_computation.4 | async-start | bytes 1572864 | tf_op jit(solution)/shard_map/all_to_all | solution.py:140
  274.8 4.6 %copy-start.8 = (bf16[384,4096]{1,0:T(8,128)(2,1)S(1)}, bf16[384,4096]{1,0:T(8,128)(2,1)}, u32[]{:S(2)}) copy-start(bf16[384,4096]{1,0:T(8,128)(2,1)} %all-gather.4.cloned.1.call-done) | copy-start | bytes 9437188
  299.9 2.3 copy-start.5
Sparse Core Ops, SparseCore 0:
  78.3 38.3 all-gather.3
  125.8 40.5 reduce-scatter.2
  168.7 42.3 all-gather.5
  224.8 35.1 reduce-scatter.4

commit v6 on v5

--- a/solution.py
+++ b/solution.py
@@ -40,25 +40,20 @@
     pick_first = slot_row[:, 0:1] == slot_ids
     pick_second = slot_row[:, 1:2] == slot_ids
     pick_both = (pick_first | pick_second).astype(jnp.bfloat16)
-    x_source = jnp.einsum(
-        "ts,td->sd", pick_both, tokens, preferred_element_type=jnp.float32
+    both_rows = jnp.concatenate([tokens, cotangent], axis=1)
+    selected = jnp.einsum(
+        "ts,td->sd", pick_both, both_rows, preferred_element_type=jnp.float32
     ).astype(jnp.bfloat16)
+    x_source = selected[:, :width]
+    cot_source = selected[:, width:].astype(jnp.float32)
     cot_float = cotangent.astype(jnp.float32)
-    scaled_first = (gate_first[:, None] * cot_float).astype(jnp.bfloat16)
-    scaled_second = (gate_second[:, None] * cot_float).astype(jnp.bfloat16)
-    dy_source = jnp.einsum(
-        "ts,td->sd",
-        pick_first.astype(jnp.bfloat16),
-        scaled_first,
-        preferred_element_type=jnp.float32,
+    zero_gate = jnp.zeros((), jnp.float32)
+    gate_slot = jnp.sum(
+        jnp.where(pick_first, gate_first[:, None], zero_gate)
+        + jnp.where(pick_second, gate_second[:, None], zero_gate),
+        axis=0,
     )
-    dy_source = dy_source + jnp.einsum(
-        "ts,td->sd",
-        pick_second.astype(jnp.bfloat16),
-        scaled_second,
-        preferred_element_type=jnp.float32,
-    )
-    dy_source = dy_source.astype(jnp.bfloat16)
+    dy_source = (gate_slot[:, None] * cot_source).astype(jnp.bfloat16)
     both_source = jnp.stack(
         [x_source.reshape(experts, capacity * width), dy_source.reshape(experts, capacity * width)],
         axis=1,
@@ -92,7 +87,7 @@
     dy_rows = lax.all_gather(dy_recv, "section", axis=1, tiled=True)
     n_dev = row_total // capacity
     out_back = lax.all_to_all(out_red.reshape(n_dev, half, LANES), EXPERT_AXES, 0, 0, tiled=True)
-    out_back = out_back.reshape(experts, groups, capacity, width).astype(jnp.float32)
+    out_back = out_back.reshape(experts, groups, half, LANES).astype(jnp.float32)
     slot_out = jnp.sum(out_back, axis=1).reshape(slot_total, width)
     d_hidden = jnp.einsum("pd,fd->pf", dy_rows, down_local, preferred_element_type=jnp.float32)
     grad_down = jnp.einsum("pf,pd->fd", hidden, dy_rows, preferred_element_type=jnp.float32).astype(
@@ -138,7 +133,7 @@
         router_part = jnp.sum(lax.all_gather(router_part, name, axis=0), axis=0)
     router_part, dx_red = lax.optimization_barrier((router_part, dx_red))
     dx_back = lax.all_to_all(dx_red.reshape(n_dev, half, LANES), EXPERT_AXES, 0, 0, tiled=True)
-    dx_back = dx_back.reshape(experts, groups, capacity, width).astype(jnp.float32)
+    dx_back = dx_back.reshape(experts, groups, half, LANES).astype(jnp.float32)
     slot_dx = jnp.sum(dx_back, axis=1).reshape(slot_total, width)
     dx_expert = jnp.dot(first_float, slot_dx, precision=highest)
     dx_expert = dx_expert + jnp.dot(second_float, slot_dx, precision=highest)

time: 312 us -> 305 us (0.978)
  local copies, waits for them, and re-layouts: 19.8 us -> 15.5 us
  other arithmetic: 6.52 us -> 3.23 us
    convert_element_type x2 -> x0, local copies, waits for them, and re-layouts: 4.3 us -> none  [the longest x1 2.17 us: per_device(): dx_back.reshape(experts, groups, capacity, width).astype(jnp.float32)]
  transfers between devices with their start and end apart: 6 -> 6, of which waited for: 4 -> 4; matrix products, arithmetic and copies ran while one was open for 8% -> 7% of each run, Pallas kernels for 0% -> 0%
where the time goes in v6:
time: 305 us; the launch traced here: 302 us
  blocking collectives  110 us (36%)
  waiting for transfers between devices  109 us (36%)
  matrix products  31.2 us (10%)
  starting transfers between devices  18.8 us (6%)
  local copies, waits for them, and re-layouts  15.5 us (5%)
  between operations  14.1 us (5%)
  other arithmetic  3.23 us (1%)
    all_to_all x1, blocking collectives, per_device(): received = lax.all_to_all(sent, EXPERT_AXES, 0, 0, tiled=True)  50 us
    reduce_scatter x1, waiting for transfers between devices, per_device(): lax.psum_scatter(out_piece, 'section', scatter_dimension=0, tiled=True)  39.4 us
    all_gather x2, blocking collectives, per_device(): router_part = jnp.sum(lax.all_gather(router_part, name, axis=0), axis=0)  36.9 us
    all_gather x1, waiting for transfers between devices, per_device(): x_rows = lax.all_gather(x_recv, 'section', axis=1, tiled=True)  34 us
    all_to_all x1, waiting for transfers between devices, per_device(): lax.all_to_all(out_red.reshape(n_dev, half, LANES), EXPERT_AXES, 0, 0, ti...  22.9 us
    all_to_all x1, waiting for transfers between devices, per_device(): lax.all_to_all(dx_red.reshape(n_dev, half, LANES), EXPERT_AXES, 0, 0, til...  13 us
    all_to_all x1, starting transfers between devices, per_device(): lax.all_to_all(out_red.reshape(n_dev, half, LANES), EXPERT_AXES, 0, 0, ti...  10.5 us
    psum x1, blocking collectives, per_device(): logits = lax.psum(partial_logits, 'section')  9.88 us
  transfers between devices with their start and end apart: 6, of which 4 were waited for; matrix products, arithmetic and copies ran while one was open for 7% of the time, Pallas kernels for 0%

profile of v6, /device:TPU:8, one launch (start us, length us, event | category | flops | bytes accessed | tf_op | source)
XLA Modules:
  0.0 302.1 jit_solution(8580359435437574383)
XLA Ops:
  7.2 0.0 all-gather.4.cloned.1.call-start
  7.2 1.0 fusion.35
  8.2 9.9 %psum.21 = f32[16,8]{0,1:T(8,128)S(1)} all-reduce(f32[16,8]{0,1:T(8,128)S(1)} %fusion.35), channel_id=1, replica_groups=mesh['section'=4,'ex'=4,'ez'=8,'ec'=2] {'section'}, use_global_device_ids=true, to_apply=%region_0.0 | all-reduce | flops 128 | bytes 1024 | tf_op jit(solution)/shard_map/psum | solution.py:29
  18.1 0.8 copy.35
  18.9 0.7 select_reduce_fusion.1
  19.6 0.1 eq.55
  19.7 0.1 fusion.21
  19.8 0.1 reduce_window_sum.11
  19.8 0.2 select_reduce_fusion
  20.0 0.1 reshape.55
  20.1 0.1 copy.36
  20.2 0.7 multiply_add_fusion
  20.9 1.1 convolution_convert_fusion.4
  22.0 0.1 add_reduce_fusion
  22.1 0.1 multiply_convert_fusion.3
  22.2 0.1 stack_reshape.8
  22.3 0.1 stack_reshape.9
  22.4 0.5 pad_maximum_fusion
  22.8 0.1 broadcast_in_dim.83
  22.9 0.2 broadcast_in_dim.84
  23.2 50.0 %all_to_all.15 = bf16[64,96,128]{2,1,0:T(8,128)(2,1)S(1)} all-to-all(bf16[64,96,128]{2,1,0:T(8,128)(2,1)S(1)} %bitcast.90), channel_id=1, replica_groups=mesh['section'=4,'ex'=4,'ez'=8,'ec'=2] {'ex','ez','ec'}, dimensions={0} | all-to-all | bytes 3145728 | tf_op jit(solution)/shard_map/all_to_all | solution.py:65
  73.2 1.0 fusion.34
  74.2 2.1 reshape.57
  76.3 0.0 all-gather.4.cloned.1.call-update
  76.4 0.0 reduce-scatter.3.cloned.1.call-start
  76.4 4.5 %reshape_squeeze.9 = bf16[256,4,1024]{2,1,0:T(4,128)(2,1)} reshape(bf16[1,256,4096]{2,1,0:T(8,128)(2,1)} %param.13) | data formatting | bytes 4194304 | tf_op jit(solution)/shard_map/reshape;squeeze | solution.py:80
  80.9 34.0 %all-gather.4.cloned.1.call-done = bf16[384,4096]{1,0:T(8,128)(2,1)} async-done(((bf16[384,1024]{1,0:T(8,128)(2,1)}), bf16[384,4096]{1,0:T(8,128)(2,1)}) %all-gather.4.cloned.1.call-update) | async-done | bytes 3145744 | tf_op jit(solution)/shard_map/all_gather | solution.py:70
  114.9 3.7 %fusion.7 = f32[384,256]{1,0:T(8,128)S(1)} fusion(bf16[384,4096]{1,0:T(8,128)(2,1)} %all-gather.4.cloned.1.call-done, bf16[1,4096,256]{2,1,0:T(8,128)(2,1)} %param.11), kind=kOutput, calls=%fused_computation.13 | convolution fusion | flops 805306368 | bytes 5636096 | tf_op jit(solution)/shard_map/dot_general | solution.py:74
  118.6 1.7 multiply_convert_fusion.2
  120.4 3.4 %convolution_convert_fusion.3 = bf16[384,4,1024]{2,0,1:T(8,128)(2,1)} fusion(bf16[256,4,1024]{2,1,0:T(4,128)(2,1)S(1)} %copy-done.1, bf16[384,256]{1,0:T(8,128)(2,1)S(1)} %get-tuple-element.29), kind=kOutput, calls=%fused_computation.7 | convolution fusion | flops 806879232 | bytes 5439488 | tf_op jit(solution)/shard_map/pf,fsd->spd/dot_general | solution.py:83
  123.8 0.0 reduce-scatter.3.cloned.1.call-update
  123.8 0.0 all-gather.6.cloned.1.call-start
  123.9 1.2 reshape.59
  125.1 39.4 %reduce-scatter.3.cloned.1.call-done = bf16[384,1024]{1,0:T(8,128)(2,1)} async-done(((bf16[1536,1024]{1,0:T(8,128)(2,1)}), bf16[384,1024]{1,0:T(8,128)(2,1)}) %reduce-scatter.3.cloned.1.call-update) | async-done | bytes 786448 | tf_op jit(solution)/shard_map/reduce_scatter | solution.py:85
  164.5 0.0 all-gather.6.cloned.1.call-update
  164.5 2.2 reshape.60
  166.7 10.5 %all-to-all-start.1 = ((bf16[64,48,128]{2,1,0:T(8,128)(2,1)}), bf16[64,48,128]{2,1,0:T(8,128)(2,1)S(1)}, u32[]{:S(2)}, u32[]{:S(2)}) async-start(bf16[64,48,128]{2,1,0:T(8,128)(2,1)} %reshape.60), calls=%async_computation.2 | async-start | bytes 1572864 | tf_op jit(solution)/shard_map/all_to_all | solution.py:89
  177.2 0.0 reduce-scatter.5.cloned.1.call-start
  177.2 22.9 %all-to-all-done.1 = bf16[64,48,128]{2,1,0:T(8,128)(2,1)S(1)} async-done(((bf16[64,48,128]{2,1,0:T(8,128)(2,1)}), bf16[64,48,128]{2,1,0:T(8,128)(2,1)S(1)}, u32[]{:S(2)}, u32[]{:S(2)}) %all-to-all-start.1) | async-done | bytes 786464 | tf_op jit(solution)/shard_map/all_to_all | solution.py:89
  200.1 0.1 convert_reduce_fusion.1
  200.2 0.2 fusion.22
  200.5 1.0 fusion.16
  201.4 9.7 %psum.22 = f32[16,2]{0,1:T(2,128)S(1)} all-reduce(f32[16,2]{0,1:T(2,128)S(1)} %pad_maximum_fusion.1), channel_id=1, replica_groups=mesh['section'=4,'ex'=4,'ez'=8,'ec'=2] {'section'}, use_global_device_ids=true, to_apply=%region_9.10 | all-reduce | flops 32 | bytes 256 | tf_op jit(solution)/shard_map/psum | solution.py:120
  211.2 0.0 all-gather.6.cloned.1.call-done
  211.2 3.9 %multiply_convert_fusion = (bf16[384,256]{1,0:T(8,128)(2,1)S(1)}, bf16[384,256]{1,0:T(8,128)(2,1)S(1)}) fusion(f32[384,256]{1,0:T(8,128)} %copy-done.9, f32[384,256]{1,0:T(8,128)} %get-tuple-element.30, bf16[384,4096]{1,0:T(8,128)(2,1)} %all-gather.6.cloned.1.call-done, bf16[1,256,4096]{2,1,0:T(8,128)(2,1)} %param.13), kind=kOutput, calls=%fused_computation.22 | convolution fusion | flops 806584320 | bytes 6422528 | tf_op jit(solution)/shard_map/pd,fd->pf/dot_general | solution.py:92
  215.1 1.0 fusion.13
  216.1 2.9 add_convert_fusion
  219.0 0.0 reduce-scatter.5.cloned.1.call-update
  219.0 0.7 copy-done.3
  219.8 0.1 convolution_bitcast_fusion
  219.9 3.4 %psum.23 = f32[1,8,1024]{2,1,0:T(8,128)S(1)} all-reduce(f32[1,8,1024]{2,1,0:T(8,128)S(1)} %convolution_bitcast_fusion), channel_id=1, replica_groups=mesh['section'=4,'ex'=4,'ez'=8,'ec'=2] {'ec'}, use_global_device_ids=true, to_apply=%region_10.11 | all-reduce | flops 8192 | bytes 65536 | tf_op jit(solution)/shard_map/psum | solution.py:131
  223.3 24.9 %all_gather.21 = f32[8,8,1024]{2,1,0:T(8,128)S(1)} all-gather(f32[1,8,1024]{2,1,0:T(8,128)S(1)} %psum.23), channel_id=1, replica_groups=mesh['section'=4,'ex'=4,'ez'=8,'ec'=2] {'ez'}, dimensions={0}, use_global_device_ids=true | all-gather | bytes 294912 | tf_op jit(solution)/shard_map/all_gather | solution.py:133
  248.2 12.0 %all-gather = f32[32,1024]{1,0:T(8,128)S(1)} all-gather(f32[8,1024]{1,0:T(8,128)S(1)} %reduce_sum.87), channel_id=2, replica_groups=mesh['section'=4,'ex'=4,'ez'=8,'ec'=2] {'ex'}, dimensions={0}, use_global_device_ids=true | all-gather | bytes 163840 | tf_op jit(solution)/shard_map/all_gather | solution.py:133
  260.2 0.6 bitcast_reduce_fusion
  260.8 2.2 reshape.63
  263.0 8.2 %all-to-all-start.2 = ((bf16[64,48,128]{2,1,0:T(8,128)(2,1)}), bf16[64,48,128]{2,1,0:T(8,128)(2,1)S(1)}, u32[]{:S(2)}, u32[]{:S(2)}) async-start(bf16[64,48,128]{2,1,0:T(8,128)(2,1)} %reshape.63), calls=%async_computation.4 | async-start | bytes 1572864 | tf_op jit(solution)/shard_map/all_to_all | solution.py:135
  271.2 4.6 %fusion.2 = bf16[1,256,4096]{2,1,0:T(8,128)(2,1)} fusion(bf16[384,256]{1,0:T(8,128)(2,1)S(1)} %get-tuple-element.29, bf16[384,4096]{1,0:T(8,128)(2,1)} %all-gather.6.cloned.1.call-done), kind=kOutput, calls=%fused_computation.6 | convolution fusion | flops 806354944 | bytes 5439488 | tf_op jit(solution)/shard_map/pf,pd->fd/dot_general | solution.py:93
  275.9 2.6 fusion.1
  278.5 2.6 fusion
  281.1 13.0 %all-to-all-done.2 = bf16[64,48,128]{2,1,0:T(8,128)(2,1)S(1)} async-done(((bf16[64,48,128]{2,1,0:T(8,128)(2,1)}), bf16[64,48,128]{2,1,0:T(8,128)(2,1)S(1)}, u32[]{:S(2)}, u32[]{:S(2)}) %all-to-all-start.2) | async-done | bytes 786464 | tf_op jit(solution)/shard_map/all_to_all | solution.py:135
  294.1 0.1 convert_reduce_fusion
  294.3 0.2 fusion.24
  294.5 0.2 convolution_add_fusion.1
  294.8 0.8 fusion.10
  (30 shorter events, 0.2 us)
Async XLA Ops:
  7.2 111.4 %copy-start = (bf16[1,4096,256]{2,1,0:T(8,128)(2,1)S(1)}, bf16[1,4096,256]{2,1,0:T(8,128)(2,1)}, u32[]{:S(2)}) copy-start(bf16[1,4096,256]{2,1,0:T(8,128)(2,1)} %param.12) | copy-start | bytes 6291460
  7.2 107.7 %all-gather.4.cloned.1.call-start = ((), (), s32[]{:S(2)}) async-start(), calls=%async_computation.5 | async-start | bytes 3932160 | tf_op jit(solution)/shard_map/all_gather | solution.py:70
  76.4 88.1 %reduce-scatter.3.cloned.1.call-start = ((), (), s32[]{:S(2)}) async-start(), calls=%async_computation.6 | async-start | bytes 3932160 | tf_op jit(solution)/shard_map/reduce_scatter | solution.py:85
  114.9 3.7 %copy-start.7 = (bf16[384,4096]{1,0:T(8,128)(2,1)S(1)}, bf16[384,4096]{1,0:T(8,128)(2,1)}, u32[]{:S(2)}) copy-start(bf16[384,4096]{1,0:T(8,128)(2,1)} %all-gather.4.cloned.1.call-done) | copy-start | bytes 9437188
  118.6 1.8 copy-start.9
  118.6 1.8 copy-start.1
  123.8 87.4 %all-gather.6.cloned.1.call-start = ((), (), s32[]{:S(2)}) async-start(), calls=%async_computation.7 | async-start | bytes 3932160 | tf_op jit(solution)/shard_map/all_gather | solution.py:87
  125.1 52.1 %copy-start.6 = (s32[16,2]{0,1:T(2,128)S(1)}, s32[16,2]{0,1:T(2,128)}, u32[]{:S(2)}) copy-start(s32[16,2]{0,1:T(2,128)} %param.9) | copy-start | bytes 388
  164.5 35.9 %copy-start.4 = (bf16[16,1024]{1,0:T(8,128)(2,1)S(1)}, bf16[16,1024]{1,0:T(8,128)(2,1)}, u32[]{:S(2)}) copy-start(bf16[16,1024]{1,0:T(8,128)(2,1)} %param.8) | copy-start | bytes 98308
  166.7 33.4 %all-to-all-start.1 = ((bf16[64,48,128]{2,1,0:T(8,128)(2,1)}), bf16[64,48,128]{2,1,0:T(8,128)(2,1)S(1)}, u32[]{:S(2)}, u32[]{:S(2)}) async-start(bf16[64,48,128]{2,1,0:T(8,128)(2,1)} %reshape.60), calls=%async_computation.2 | async-start | bytes 1572864 | tf_op jit(solution)/shard_map/all_to_all | solution.py:89
  177.2 83.7 %reduce-scatter.5.cloned.1.call-start = ((), (), s32[]{:S(2)}) async-start(), calls=%async_computation.8 | async-start | bytes 3932160 | tf_op jit(solution)/shard_map/reduce_scatter | solution.py:127
  211.2 3.9 %copy-start.2 = (bf16[1,4096,256]{2,1,0:T(8,128)(2,1)S(1)}, bf16[1,4096,256]{2,1,0:T(8,128)(2,1)}, u32[]{:S(2)}) copy-start(bf16[1,4096,256]{2,1,0:T(8,128)(2,1)} %param.11) | copy-start | bytes 6291460
  219.0 0.8 copy-start.3
  263.0 31.1 %all-to-all-start.2 = ((bf16[64,48,128]{2,1,0:T(8,128)(2,1)}), bf16[64,48,128]{2,1,0:T(8,128)(2,1)S(1)}, u32[]{:S(2)}, u32[]{:S(2)}) async-start(bf16[64,48,128]{2,1,0:T(8,128)(2,1)} %reshape.63), calls=%async_computation.4 | async-start | bytes 1572864 | tf_op jit(solution)/shard_map/all_to_all | solution.py:135
  271.2 4.6 %copy-start.8 = (bf16[384,4096]{1,0:T(8,128)(2,1)S(1)}, bf16[384,4096]{1,0:T(8,128)(2,1)}, u32[]{:S(2)}) copy-start(bf16[384,4096]{1,0:T(8,128)(2,1)} %all-gather.4.cloned.1.call-done) | copy-start | bytes 9437188
  278.5 16.3 %copy-start.5 = (bf16[1024,8]{0,1:T(8,128)(2,1)S(1)}, bf16[1024,8]{0,1:T(8,128)(2,1)}, u32[]{:S(2)}) copy-start(bf16[1024,8]{0,1:T(8,128)(2,1)} %param.10) | copy-start | bytes 49156
Sparse Core Ops, SparseCore 0:
  76.5 38.3 all-gather.3
  123.9 40.5 reduce-scatter.2
  166.9 42.4 all-gather.5
  219.1 38.6 reduce-scatter.4

commit v7 on v6

--- a/solution.py
+++ b/solution.py
@@ -25,13 +25,8 @@
     tok_count, width = tokens.shape
     n_section = lax.axis_size("section")
     slot_total = experts * capacity
-    partial_logits = jnp.dot(tokens, w_router, preferred_element_type=jnp.float32)
-    logits = lax.psum(partial_logits, "section")
     route_hot = routes[:, :, None] == jnp.arange(experts, dtype=jnp.int32)[None, None, :]
     zero_f = jnp.zeros((), jnp.float32)
-    chosen = jnp.sum(jnp.where(route_hot, logits[:, None, :], zero_f), axis=2)
-    gate_first = 1.0 / (1.0 + jnp.exp(chosen[:, 1] - chosen[:, 0]))
-    gate_second = 1.0 / (1.0 + jnp.exp(chosen[:, 0] - chosen[:, 1]))
     counts_flat = route_hot.astype(jnp.int32).reshape(2 * tok_count, experts)
     earlier = jnp.cumsum(counts_flat, axis=0) - counts_flat
     position = jnp.sum(earlier * counts_flat, axis=1).reshape(tok_count, 2)
@@ -44,30 +39,47 @@
     selected = jnp.einsum(
         "ts,td->sd", pick_both, both_rows, preferred_element_type=jnp.float32
     ).astype(jnp.bfloat16)
-    x_source = selected[:, :width]
-    cot_source = selected[:, width:].astype(jnp.float32)
-    cot_float = cotangent.astype(jnp.float32)
-    zero_gate = jnp.zeros((), jnp.float32)
-    gate_slot = jnp.sum(
-        jnp.where(pick_first, gate_first[:, None], zero_gate)
-        + jnp.where(pick_second, gate_second[:, None], zero_gate),
+    zero_i = jnp.zeros((), jnp.int32)
+    other_slot = jnp.sum(
+        jnp.where(pick_first, routes[:, 1:2], zero_i) + jnp.where(pick_second, routes[:, 0:1], zero_i),
         axis=0,
     )
-    dy_source = (gate_slot[:, None] * cot_source).astype(jnp.bfloat16)
-    both_source = jnp.stack(
-        [x_source.reshape(experts, capacity * width), dy_source.reshape(experts, capacity * width)],
+    half = capacity * width // LANES
+    meta = jnp.zeros((experts, 16, LANES), jnp.bfloat16)
+    meta = meta.at[:, 0, :capacity].set(other_slot.reshape(experts, capacity).astype(jnp.bfloat16))
+    both_source = jnp.concatenate(
+        [
+            selected[:, :width].reshape(experts, half, LANES),
+            selected[:, width:].reshape(experts, half, LANES),
+            meta,
+        ],
         axis=1,
     )
-    block_rows = 2 * capacity * width // LANES
+    block_rows = both_source.shape[1]
     sent = jnp.broadcast_to(
-        both_source.reshape(experts, 1, block_rows, LANES), (experts, groups, block_rows, LANES)
+        both_source[:, None], (experts, groups, block_rows, LANES)
     ).reshape(experts * groups, block_rows, LANES)
     received = lax.all_to_all(sent, EXPERT_AXES, 0, 0, tiled=True)
     row_total = received.shape[0] * capacity
-    half = block_rows // 2
     x_recv = received[:, :half].reshape(row_total, width)
-    dy_recv = received[:, half:].reshape(row_total, width)
     x_rows = lax.all_gather(x_recv, "section", axis=1, tiled=True)
+    cot_recv = received[:, half : 2 * half].reshape(row_total, width)
+    other_recv = received[:, 2 * half, :capacity].astype(jnp.int32).reshape(row_total)
+    w_router, x_recv = lax.optimization_barrier((w_router, x_recv))
+    partial_logits = jnp.dot(tokens, w_router, preferred_element_type=jnp.float32)
+    logits = lax.psum(partial_logits, "section")
+    chosen = jnp.sum(jnp.where(route_hot, logits[:, None, :], zero_f), axis=2)
+    gate_first = 1.0 / (1.0 + jnp.exp(chosen[:, 1] - chosen[:, 0]))
+    gate_second = 1.0 / (1.0 + jnp.exp(chosen[:, 0] - chosen[:, 1]))
+    cot_float = cotangent.astype(jnp.float32)
+    row_logits = lax.psum(
+        jnp.dot(x_recv, w_router, preferred_element_type=jnp.float32), "section"
+    )
+    own = lax.axis_index(EXPERT_AXES) // groups
+    expert_ids = jnp.arange(experts, dtype=jnp.int32)[None, :]
+    own_logit = jnp.sum(jnp.where(expert_ids == own, row_logits, zero_f), axis=1)
+    other_logit = jnp.sum(jnp.where(expert_ids == other_recv[:, None], row_logits, zero_f), axis=1)
+    row_gate = 1.0 / (1.0 + jnp.exp(other_logit - own_logit))
     gate_local = w_gate[0]
     up_local = w_up[0]
     down_local = w_down[0]
@@ -83,8 +95,9 @@
     out_piece = jnp.einsum("pf,fsd->spd", hidden, down_blocks, preferred_element_type=jnp.float32)
     out_piece = out_piece.astype(jnp.bfloat16).reshape(n_section * row_total, width)
     out_red = lax.psum_scatter(out_piece, "section", scatter_dimension=0, tiled=True)
-    out_red, dy_recv = lax.optimization_barrier((out_red, dy_recv))
-    dy_rows = lax.all_gather(dy_recv, "section", axis=1, tiled=True)
+    out_red, cot_recv = lax.optimization_barrier((out_red, cot_recv))
+    cot_rows = lax.all_gather(cot_recv, "section", axis=1, tiled=True)
+    dy_rows = (row_gate[:, None] * cot_rows.astype(jnp.float32)).astype(jnp.bfloat16)
     n_dev = row_total // capacity
     out_back = lax.all_to_all(out_red.reshape(n_dev, half, LANES), EXPERT_AXES, 0, 0, tiled=True)
     out_back = out_back.reshape(experts, groups, half, LANES).astype(jnp.float32)

time: 305 us -> 305 us (level)
    psum x1 -> x0, blocking collectives: 9.74 us -> none  [per_device(): gate_inner = lax.psum(local_inner, 'section')]
    all_to_all x1, blocking collectives: 50 us -> 57.1 us  [per_device(): received = lax.all_to_all(sent, EXPERT_AXES, 0, 0, tiled=True)]
    psum x1, blocking collectives: 9.88 us -> 14.9 us  [per_device(): logits = lax.psum(partial_logits, 'section')]
  transfers between devices with their start and end apart: 6 -> 6, of which waited for: 4 -> 4; matrix products, arithmetic and copies ran while one was open for 7% -> 8% of each run, Pallas kernels for 0% -> 0%
where the time goes in v7:
time: 305 us; the launch traced here: 301 us
  blocking collectives  112 us (37%)
  waiting for transfers between devices  106 us (35%)
  matrix products  30.2 us (10%)
  local copies, waits for them, and re-layouts  17.1 us (6%)
  starting transfers between devices  16.9 us (6%)
  between operations  14.1 us (5%)
  other arithmetic  5 us (2%)
    all_to_all x1, blocking collectives, per_device(): received = lax.all_to_all(sent, EXPERT_AXES, 0, 0, tiled=True)  57.1 us
    reduce_scatter x1, waiting for transfers between devices, per_device(): lax.psum_scatter(out_piece, 'section', scatter_dimension=0, tiled=True)  38.4 us
    all_gather x2, blocking collectives, per_device(): router_part = jnp.sum(lax.all_gather(router_part, name, axis=0), axis=0)  37 us
    all_gather x1, waiting for transfers between devices, per_device(): x_rows = lax.all_gather(x_recv, 'section', axis=1, tiled=True)  34 us
    all_to_all x1, waiting for transfers between devices, per_device(): lax.all_to_all(out_red.reshape(n_dev, half, LANES), EXPERT_AXES, 0, 0, ti...  21.1 us
    psum x1, blocking collectives, per_device(): logits = lax.psum(partial_logits, 'section')  14.9 us
    all_to_all x1, waiting for transfers between devices, per_device(): lax.all_to_all(dx_red.reshape(n_dev, half, LANES), EXPERT_AXES, 0, 0, til...  12.1 us
    all_to_all x1, starting transfers between devices, per_device(): lax.all_to_all(out_red.reshape(n_dev, half, LANES), EXPERT_AXES, 0, 0, ti...  10.7 us
  transfers between devices with their start and end apart: 6, of which 4 were waited for; matrix products, arithmetic and copies ran while one was open for 8% of the time, Pallas kernels for 0%

profile of v7, /device:TPU:8, one launch (start us, length us, event | category | flops | bytes accessed | tf_op | source)
XLA Modules:
  0.0 301.4 jit_solution(9110043773544213287)
XLA Ops:
  7.2 0.0 all-gather.4.cloned.1.call-start
  7.2 0.9 copy.42
  8.1 0.1 eq.79
  8.2 0.1 fusion.24
  8.3 0.1 reduce_window_sum.11
  8.3 0.2 select_reduce_fusion
  8.5 0.1 reshape.124
  8.6 0.1 copy.43
  8.7 0.7 multiply_add_fusion
  9.4 0.8 slice_bitcast_fusion.3
  10.2 0.1 add_reduce_fusion
  10.3 0.1 convert_element_type.118
  10.3 1.1 convolution_convert_fusion.4
  11.6 0.2 broadcast_in_dim.97
  11.9 57.1 %all_to_all.15 = bf16[64,112,128]{2,1,0:T(8,128)(2,1)S(1)} all-to-all(bf16[64,112,128]{2,1,0:T(8,128)(2,1)S(1)} %bitcast.96), channel_id=1, replica_groups=mesh['section'=4,'ex'=4,'ez'=8,'ec'=2] {'ex','ez','ec'}, dimensions={0} | all-to-all | bytes 3670016 | tf_op jit(solution)/shard_map/all_to_all | solution.py:62
  68.9 1.2 copy-done.3
  70.2 1.0 fusion.37
  71.1 1.2 reshape.128
  72.4 0.0 all-gather.4.cloned.1.call-update
  72.4 0.0 reduce-scatter.3.cloned.1.call-start
  72.4 4.5 %reshape_squeeze.9 = bf16[256,4,1024]{2,1,0:T(4,128)(2,1)} reshape(bf16[1,256,4096]{2,1,0:T(8,128)(2,1)} %param.15) | data formatting | bytes 4194304 | tf_op jit(solution)/shard_map/reshape;squeeze | solution.py:92
  76.9 34.0 %all-gather.4.cloned.1.call-done = bf16[384,4096]{1,0:T(8,128)(2,1)} async-done(((bf16[384,1024]{1,0:T(8,128)(2,1)}), bf16[384,4096]{1,0:T(8,128)(2,1)}) %all-gather.4.cloned.1.call-update) | async-done | bytes 3145744 | tf_op jit(solution)/shard_map/all_gather | solution.py:65
  111.0 3.7 %fusion.7 = f32[384,256]{1,0:T(8,128)S(1)} fusion(bf16[384,4096]{1,0:T(8,128)(2,1)} %all-gather.4.cloned.1.call-done, bf16[1,4096,256]{2,1,0:T(8,128)(2,1)} %param.13), kind=kOutput, calls=%fused_computation.14 | convolution fusion | flops 805306368 | bytes 5636096 | tf_op jit(solution)/shard_map/dot_general | solution.py:86
  114.7 1.8 multiply_convert_fusion.5
  116.4 3.4 %convolution_convert_fusion.3 = bf16[384,4,1024]{2,0,1:T(8,128)(2,1)} fusion(bf16[256,4,1024]{2,1,0:T(4,128)(2,1)S(1)} %copy-done.1, bf16[384,256]{1,0:T(8,128)(2,1)S(1)} %get-tuple-element.54), kind=kOutput, calls=%fused_computation.8 | convolution fusion | flops 806879232 | bytes 5439488 | tf_op jit(solution)/shard_map/pf,fsd->spd/dot_general | solution.py:95
  119.8 0.0 reduce-scatter.3.cloned.1.call-update
  119.9 0.0 all-gather.6.cloned.1.call-start
  120.0 2.2 reshape.130
  122.2 38.4 %reduce-scatter.3.cloned.1.call-done = bf16[384,1024]{1,0:T(8,128)(2,1)} async-done(((bf16[1536,1024]{1,0:T(8,128)(2,1)}), bf16[384,1024]{1,0:T(8,128)(2,1)}) %reduce-scatter.3.cloned.1.call-update) | async-done | bytes 786448 | tf_op jit(solution)/shard_map/reduce_scatter | solution.py:97
  160.6 0.0 all-gather.6.cloned.1.call-update
  160.6 2.2 reshape.131
  162.8 10.7 %all-to-all-start.1 = ((bf16[64,48,128]{2,1,0:T(8,128)(2,1)}), bf16[64,48,128]{2,1,0:T(8,128)(2,1)}, u32[]{:S(2)}, u32[]{:S(2)}) async-start(bf16[64,48,128]{2,1,0:T(8,128)(2,1)} %reshape.131), calls=%async_computation.2 | async-start | bytes 1572864 | tf_op jit(solution)/shard_map/all_to_all | solution.py:102
  173.4 0.0 reduce-scatter.5.cloned.1.call-start
  173.5 1.0 fusion.23
  174.6 0.1 reshape.137
  174.7 0.1 convolution_bitcast_fusion.1
  174.8 0.3 fusion.39
  175.1 21.1 %all-to-all-done.1 = bf16[64,48,128]{2,1,0:T(8,128)(2,1)} async-done(((bf16[64,48,128]{2,1,0:T(8,128)(2,1)}), bf16[64,48,128]{2,1,0:T(8,128)(2,1)}, u32[]{:S(2)}, u32[]{:S(2)}) %all-to-all-start.1) | async-done | bytes 786464 | tf_op jit(solution)/shard_map/all_to_all | solution.py:102
  196.2 1.3 convert_reduce_fusion.1
  197.5 0.2 fusion.25
  197.8 0.3 fusion.18
  198.1 14.9 %all-reduce.1 = (f32[16,8]{0,1:T(8,128)S(1)}, f32[16,2]{0,1:T(2,128)S(1)}, f32[384,8]{0,1:T(8,128)S(1)}) all-reduce(f32[16,8]{0,1:T(8,128)S(1)} %convolution_bitcast_fusion.1, f32[16,2]{0,1:T(2,128)S(1)} %pad_maximum_fusion, f32[384,8]{0,1:T(8,128)S(1)} %fusion.39), channel_id=1, replica_groups=mesh['section'=4,'ex'=4,'ez'=8,'ec'=2] {'section'}, use_global_device_ids=true, to_apply=%region_3.4 | all-reduce | flops 3232 | bytes 25856 | tf_op jit(solution)/shard_map/psum | solution.py:70
  213.1 0.1 select_reduce_fusion.1
  213.2 0.0 all-gather.6.cloned.1.call-done
  213.2 3.9 %multiply_convert_fusion.3 = (bf16[384,256]{1,0:T(8,128)(2,1)S(1)}, bf16[384,256]{1,0:T(8,128)(2,1)S(1)}) fusion(f32[384,256]{1,0:T(8,128)} %copy-done.13, f32[384,256]{1,0:T(8,128)} %get-tuple-element.55, bf16[1,256,4096]{2,1,0:T(8,128)(2,1)} %param.15, bf16[384,4096]{1,0:T(8,128)(2,1)} %all-gather.6.cloned.1.call-done, f32[384]{0:T(512)S(1)} %add_divide_fusion.1), kind=kOutput, calls=%fused_computation.26 | convolution fusion | flops 811302912 | bytes 6424064 | tf_op jit(solution)/shard_map/pd,fd->pf/dot_general | solution.py:105
  217.2 1.0 fusion.15
  218.2 2.9 add_convert_fusion
  221.0 0.0 reduce-scatter.5.cloned.1.call-update
  221.1 0.1 convolution_bitcast_fusion
  221.2 3.4 %psum.31 = f32[1,8,1024]{2,1,0:T(8,128)S(1)} all-reduce(f32[1,8,1024]{2,1,0:T(8,128)S(1)} %convolution_bitcast_fusion), channel_id=1, replica_groups=mesh['section'=4,'ex'=4,'ez'=8,'ec'=2] {'ec'}, use_global_device_ids=true, to_apply=%region_13.14 | all-reduce | flops 8192 | bytes 65536 | tf_op jit(solution)/shard_map/psum | solution.py:144
  224.6 25.0 %all_gather.21 = f32[8,8,1024]{2,1,0:T(8,128)S(1)} all-gather(f32[1,8,1024]{2,1,0:T(8,128)S(1)} %psum.31), channel_id=1, replica_groups=mesh['section'=4,'ex'=4,'ez'=8,'ec'=2] {'ez'}, dimensions={0}, use_global_device_ids=true | all-gather | bytes 294912 | tf_op jit(solution)/shard_map/all_gather | solution.py:146
  249.6 12.0 %all-gather = f32[32,1024]{1,0:T(8,128)S(1)} all-gather(f32[8,1024]{1,0:T(8,128)S(1)} %reduce_sum.107), channel_id=2, replica_groups=mesh['section'=4,'ex'=4,'ez'=8,'ec'=2] {'ex'}, dimensions={0}, use_global_device_ids=true | all-gather | bytes 163840 | tf_op jit(solution)/shard_map/all_gather | solution.py:146
  261.6 0.6 bitcast_reduce_fusion
  262.3 2.2 reshape.134
  264.4 6.1 %all-to-all-start.2 = ((bf16[64,48,128]{2,1,0:T(8,128)(2,1)}), bf16[64,48,128]{2,1,0:T(8,128)(2,1)S(1)}, u32[]{:S(2)}, u32[]{:S(2)}) async-start(bf16[64,48,128]{2,1,0:T(8,128)(2,1)} %reshape.134), calls=%async_computation.4 | async-start | bytes 1572864 | tf_op jit(solution)/shard_map/all_to_all | solution.py:148
  270.6 0.7 add_convert_fusion.1
  271.3 4.9 %fusion.2 = bf16[1,256,4096]{2,1,0:T(8,128)(2,1)} fusion(bf16[384,256]{1,0:T(8,128)(2,1)S(1)} %get-tuple-element.54, bf16[384,4096]{1,0:T(8,128)(2,1)} %all-gather.6.cloned.1.call-done, f32[384]{0:T(512)S(1)} %add_divide_fusion.1), kind=kOutput, calls=%fused_computation.7 | convolution fusion | flops 811073536 | bytes 5441024 | tf_op jit(solution)/shard_map/pf,pd->fd/dot_general | solution.py:106
  276.2 2.6 fusion
  278.8 2.6 fusion.1
  281.4 12.1 %all-to-all-done.2 = bf16[64,48,128]{2,1,0:T(8,128)(2,1)S(1)} async-done(((bf16[64,48,128]{2,1,0:T(8,128)(2,1)}), bf16[64,48,128]{2,1,0:T(8,128)(2,1)S(1)}, u32[]{:S(2)}, u32[]{:S(2)}) %all-to-all-start.2) | async-done | bytes 786464 | tf_op jit(solution)/shard_map/all_to_all | solution.py:148
  293.5 0.1 convert_reduce_fusion
  293.6 0.2 fusion.27
  293.8 0.2 convolution_add_fusion.1
  294.1 0.8 fusion.10
  (43 shorter events, 0.4 us)
Async XLA Ops:
  7.2 107.5 %copy-start = (bf16[1,4096,256]{2,1,0:T(8,128)(2,1)S(1)}, bf16[1,4096,256]{2,1,0:T(8,128)(2,1)}, u32[]{:S(2)}) copy-start(bf16[1,4096,256]{2,1,0:T(8,128)(2,1)} %param.14) | copy-start | bytes 6291460
  7.2 103.8 %all-gather.4.cloned.1.call-start = ((), (), s32[]{:S(2)}) async-start(), calls=%async_computation.5 | async-start | bytes 3932160 | tf_op jit(solution)/shard_map/all_gather | solution.py:65
  68.9 1.2 copy-start.3
  72.4 88.2 %reduce-scatter.3.cloned.1.call-start = ((), (), s32[]{:S(2)}) async-start(), calls=%async_computation.6 | async-start | bytes 3932160 | tf_op jit(solution)/shard_map/reduce_scatter | solution.py:97
  111.0 3.7 %copy-start.11 = (bf16[384,4096]{1,0:T(8,128)(2,1)S(1)}, bf16[384,4096]{1,0:T(8,128)(2,1)}, u32[]{:S(2)}) copy-start(bf16[384,4096]{1,0:T(8,128)(2,1)} %all-gather.4.cloned.1.call-done) | copy-start | bytes 9437188
  114.7 1.8 copy-start.13
  114.7 1.8 copy-start.1
  119.9 53.7 %copy-start.10 = (s32[16,2]{0,1:T(2,128)S(1)}, s32[16,2]{0,1:T(2,128)}, u32[]{:S(2)}) copy-start(s32[16,2]{0,1:T(2,128)} %param.11) | copy-start | bytes 388
  119.9 54.8 %copy-start.5 = (bf16[16,1024]{1,0:T(8,128)(2,1)S(1)}, bf16[16,1024]{1,0:T(8,128)(2,1)}, u32[]{:S(2)}) copy-start(bf16[16,1024]{1,0:T(8,128)(2,1)} %param.9) | copy-start | bytes 98308
  119.9 54.8 %copy-start.8 = (bf16[1024,8]{0,1:T(8,128)(2,1)S(1)}, bf16[1024,8]{0,1:T(8,128)(2,1)}, u32[]{:S(2)}) copy-start(bf16[1024,8]{0,1:T(8,128)(2,1)} %param.12) | copy-start | bytes 49156
  119.9 54.9 %copy-start.2 = (bf16[384,1024]{1,0:T(8,128)(2,1)S(1)}, bf16[384,1024]{1,0:T(8,128)(2,1)}, u32[]{:S(2)}) copy-start(bf16[384,1024]{1,0:T(8,128)(2,1)} %reshape.128) | copy-start | bytes 2359300
  119.9 93.3 %all-gather.6.cloned.1.call-start = ((), (), s32[]{:S(2)}) async-start(), calls=%async_computation.7 | async-start | bytes 3932160 | tf_op jit(solution)/shard_map/all_gather | solution.py:99
  122.2 75.6 %copy-start.9 = (bf16[16,1024]{1,0:T(8,128)(2,1)S(1)}, bf16[16,1024]{1,0:T(8,128)(2,1)}, u32[]{:S(2)}) copy-start(bf16[16,1024]{1,0:T(8,128)(2,1)} %param.10) | copy-start | bytes 98308
  162.8 33.5 %all-to-all-start.1 = ((bf16[64,48,128]{2,1,0:T(8,128)(2,1)}), bf16[64,48,128]{2,1,0:T(8,128)(2,1)}, u32[]{:S(2)}, u32[]{:S(2)}) async-start(bf16[64,48,128]{2,1,0:T(8,128)(2,1)} %reshape.131), calls=%async_computation.2 | async-start | bytes 1572864 | tf_op jit(solution)/shard_map/all_to_all | solution.py:102
  173.4 88.8 %reduce-scatter.5.cloned.1.call-start = ((), (), s32[]{:S(2)}) async-start(), calls=%async_computation.8 | async-start | bytes 3932160 | tf_op jit(solution)/shard_map/reduce_scatter | solution.py:140
  213.2 3.9 %copy-start.4 = (bf16[1,4096,256]{2,1,0:T(8,128)(2,1)S(1)}, bf16[1,4096,256]{2,1,0:T(8,128)(2,1)}, u32[]{:S(2)}) copy-start(bf16[1,4096,256]{2,1,0:T(8,128)(2,1)} %param.13) | copy-start | bytes 6291460
  217.1 1.0 copy-start.6
  264.4 29.0 %all-to-all-start.2 = ((bf16[64,48,128]{2,1,0:T(8,128)(2,1)}), bf16[64,48,128]{2,1,0:T(8,128)(2,1)S(1)}, u32[]{:S(2)}, u32[]{:S(2)}) async-start(bf16[64,48,128]{2,1,0:T(8,128)(2,1)} %reshape.134), calls=%async_computation.4 | async-start | bytes 1572864 | tf_op jit(solution)/shard_map/all_to_all | solution.py:148
  270.5 5.6 %copy-start.7 = (bf16[384,256]{1,0:T(8,128)(2,1)S(1)}, bf16[384,256]{1,0:T(8,128)(2,1)}, u32[]{:S(2)}) copy-start(bf16[384,256]{1,0:T(8,128)(2,1)} %copy-done.6) | copy-start | bytes 589828
  270.5 5.6 %copy-start.12 = (bf16[384,4096]{1,0:T(8,128)(2,1)S(1)}, bf16[384,4096]{1,0:T(8,128)(2,1)}, u32[]{:S(2)}) copy-start(bf16[384,4096]{1,0:T(8,128)(2,1)} %all-gather.4.cloned.1.call-done) | copy-start | bytes 9437188
Sparse Core Ops, SparseCore 0:
  72.5 38.4 all-gather.3
  120.0 40.5 reduce-scatter.2
  162.4 42.4 all-gather.5
  221.2 36.6 reduce-scatter.4

commit v8 on v7

--- a/solution.py
+++ b/solution.py
@@ -80,6 +80,9 @@
     own_logit = jnp.sum(jnp.where(expert_ids == own, row_logits, zero_f), axis=1)
     other_logit = jnp.sum(jnp.where(expert_ids == other_recv[:, None], row_logits, zero_f), axis=1)
     row_gate = 1.0 / (1.0 + jnp.exp(other_logit - own_logit))
+    row_gate, gate_first, gate_second, x_rows = lax.optimization_barrier(
+        (row_gate, gate_first, gate_second, x_rows)
+    )
     gate_local = w_gate[0]
     up_local = w_up[0]
     down_local = w_down[0]

time: 305 us -> 301 us (0.987)
  waiting for transfers between devices: 106 us -> 93.3 us
  blocking collectives: 112 us -> 121 us
    all_gather x1, waiting for transfers between devices: 34 us -> 18 us  [per_device(): x_rows = lax.all_gather(x_recv, 'section', axis=1, tiled=True)]
    psum x1 -> x2, blocking collectives: 14.9 us -> 24 us  [the longest x1 14.3 us: per_device(): lax.psum(jnp.dot(x_recv, w_router, preferred_element_type=jnp.float32), '...]
  transfers between devices with their start and end apart: 6 -> 6, of which waited for: 4 -> 4; matrix products, arithmetic and copies ran while one was open for 8% -> 7% of each run, Pallas kernels for 0% -> 0%
where the time goes in v8:
time: 301 us; the launch traced here: 297 us
  blocking collectives  121 us (40%)
  waiting for transfers between devices  93.3 us (31%)
  matrix products  30.7 us (10%)
  starting transfers between devices  18.8 us (6%)
  local copies, waits for them, and re-layouts  16.1 us (5%)
  between operations  14.1 us (5%)
  other arithmetic  3.15 us (1%)
    all_to_all x1, blocking collectives, per_device(): received = lax.all_to_all(sent, EXPERT_AXES, 0, 0, tiled=True)  57.1 us
    reduce_scatter x1, waiting for transfers between devices, per_device(): lax.psum_scatter(out_piece, 'section', scatter_dimension=0, tiled=True)  39.4 us
    all_gather x2, blocking collectives, per_device(): router_part = jnp.sum(lax.all_gather(router_part, name, axis=0), axis=0)  36.9 us
    all_to_all x1, waiting for transfers between devices, per_device(): lax.all_to_all(out_red.reshape(n_dev, half, LANES), EXPERT_AXES, 0, 0, ti...  22.9 us
    all_gather x1, waiting for transfers between devices, per_device(): x_rows = lax.all_gather(x_recv, 'section', axis=1, tiled=True)  18 us
    psum x1, blocking collectives, per_device(): lax.psum(jnp.dot(x_recv, w_router, preferred_element_type=jnp.float32), '...  14.3 us
    all_to_all x1, waiting for transfers between devices, per_device(): lax.all_to_all(dx_red.reshape(n_dev, half, LANES), EXPERT_AXES, 0, 0, til...  13 us
    all_to_all x1, starting transfers between devices, per_device(): lax.all_to_all(out_red.reshape(n_dev, half, LANES), EXPERT_AXES, 0, 0, ti...  10.4 us
  transfers between devices with their start and end apart: 6, of which 4 were waited for; matrix products, arithmetic and copies ran while one was open for 7% of the time, Pallas kernels for 0%

profile of v8, /device:TPU:8, one launch (start us, length us, event | category | flops | bytes accessed | tf_op | source)
XLA Modules:
  0.0 297.5 jit_solution(242263460282261895)
XLA Ops:
  7.2 0.0 all-gather.4.cloned.1.call-start
  7.2 0.9 copy.39
  8.1 0.1 eq.77
  8.2 0.1 fusion.24
  8.3 0.1 reduce_window_sum.11
  8.3 0.2 select_reduce_fusion
  8.5 0.1 reshape.134
  8.6 0.1 copy.40
  8.7 0.7 multiply_add_fusion
  9.4 0.8 slice_bitcast_fusion.3
  10.2 0.1 add_reduce_fusion
  10.3 0.1 convert_element_type.118
  10.3 1.1 convolution_convert_fusion.4
  11.6 0.2 broadcast_in_dim.95
  11.9 57.1 %all_to_all.15 = bf16[64,112,128]{2,1,0:T(8,128)(2,1)S(1)} all-to-all(bf16[64,112,128]{2,1,0:T(8,128)(2,1)S(1)} %bitcast.98), channel_id=1, replica_groups=mesh['section'=4,'ex'=4,'ez'=8,'ec'=2] {'ex','ez','ec'}, dimensions={0} | all-to-all | bytes 3670016 | tf_op jit(solution)/shard_map/all_to_all | solution.py:62
  68.9 1.2 copy-done.3
  70.2 1.0 fusion.37
  71.1 1.2 reshape.138
  72.4 0.0 all-gather.4.cloned.1.call-update
  72.4 0.0 reduce-scatter.3.cloned.1.call-start
  72.5 4.5 %reshape_squeeze.9 = bf16[256,4,1024]{2,1,0:T(4,128)(2,1)} reshape(bf16[1,256,4096]{2,1,0:T(8,128)(2,1)} %param.15) | data formatting | bytes 4194304 | tf_op jit(solution)/shard_map/reshape;squeeze | solution.py:95
  77.0 1.0 fusion.23
  78.0 0.1 reshape.146
  78.2 0.1 convolution_bitcast_fusion.1
  78.3 0.3 fusion.39
  78.6 14.3 %all-reduce.1 = (f32[384,8]{0,1:T(8,128)S(1)}, f32[16,8]{0,1:T(8,128)S(1)}) all-reduce(f32[384,8]{0,1:T(8,128)S(1)} %fusion.39, f32[16,8]{0,1:T(8,128)S(1)} %convolution_bitcast_fusion.1), channel_id=1, replica_groups=mesh['section'=4,'ex'=4,'ez'=8,'ec'=2] {'section'}, use_global_device_ids=true, to_apply=%region_3.4 | all-reduce | flops 3200 | bytes 25600 | tf_op jit(solution)/shard_map/psum | solution.py:75
  92.9 0.1 select_reduce_fusion.1
  93.0 18.0 %all-gather.4.cloned.1.call-done = bf16[384,4096]{1,0:T(8,128)(2,1)} async-done(((bf16[384,1024]{1,0:T(8,128)(2,1)}), bf16[384,4096]{1,0:T(8,128)(2,1)}) %all-gather.4.cloned.1.call-update) | async-done | bytes 3145744 | tf_op jit(solution)/shard_map/all_gather | solution.py:65
  111.0 3.7 %fusion.7 = f32[384,256]{1,0:T(8,128)S(1)} fusion(bf16[384,4096]{1,0:T(8,128)(2,1)} %all-gather.4.cloned.1.call-done, bf16[1,4096,256]{2,1,0:T(8,128)(2,1)} %param.13), kind=kOutput, calls=%fused_computation.14 | convolution fusion | flops 805306368 | bytes 5636096 | tf_op jit(solution)/shard_map/dot_general | solution.py:89
  114.8 1.8 multiply_convert_fusion.5
  116.5 3.4 %convolution_convert_fusion.3 = bf16[384,4,1024]{2,0,1:T(8,128)(2,1)} fusion(bf16[256,4,1024]{2,1,0:T(4,128)(2,1)S(1)} %copy-done.1, bf16[384,256]{1,0:T(8,128)(2,1)S(1)} %get-tuple-element.61), kind=kOutput, calls=%fused_computation.8 | convolution fusion | flops 806879232 | bytes 5439488 | tf_op jit(solution)/shard_map/pf,fsd->spd/dot_general | solution.py:98
  119.9 0.0 reduce-scatter.3.cloned.1.call-update
  119.9 0.0 all-gather.6.cloned.1.call-start
  120.0 1.2 reshape.140
  121.2 39.4 %reduce-scatter.3.cloned.1.call-done = bf16[384,1024]{1,0:T(8,128)(2,1)} async-done(((bf16[1536,1024]{1,0:T(8,128)(2,1)}), bf16[384,1024]{1,0:T(8,128)(2,1)}) %reduce-scatter.3.cloned.1.call-update) | async-done | bytes 786448 | tf_op jit(solution)/shard_map/reduce_scatter | solution.py:100
  160.6 0.0 all-gather.6.cloned.1.call-update
  160.6 2.2 reshape.141
  162.8 10.4 %all-to-all-start.1 = ((bf16[64,48,128]{2,1,0:T(8,128)(2,1)}), bf16[64,48,128]{2,1,0:T(8,128)(2,1)S(1)}, u32[]{:S(2)}, u32[]{:S(2)}) async-start(bf16[64,48,128]{2,1,0:T(8,128)(2,1)} %reshape.141), calls=%async_computation.2 | async-start | bytes 1572864 | tf_op jit(solution)/shard_map/all_to_all | solution.py:105
  173.2 0.0 reduce-scatter.5.cloned.1.call-start
  173.3 22.9 %all-to-all-done.1 = bf16[64,48,128]{2,1,0:T(8,128)(2,1)S(1)} async-done(((bf16[64,48,128]{2,1,0:T(8,128)(2,1)}), bf16[64,48,128]{2,1,0:T(8,128)(2,1)S(1)}, u32[]{:S(2)}, u32[]{:S(2)}) %all-to-all-start.1) | async-done | bytes 786464 | tf_op jit(solution)/shard_map/all_to_all | solution.py:105
  196.1 0.1 convert_reduce_fusion.1
  196.3 0.2 fusion.25
  196.5 1.0 fusion.18
  197.5 9.8 %psum.30 = f32[16,2]{0,1:T(2,128)S(1)} all-reduce(f32[16,2]{0,1:T(2,128)S(1)} %pad_maximum_fusion), channel_id=1, replica_groups=mesh['section'=4,'ex'=4,'ez'=8,'ec'=2] {'section'}, use_global_device_ids=true, to_apply=%region_12.13 | all-reduce | flops 32 | bytes 256 | tf_op jit(solution)/shard_map/psum | solution.py:136
  207.3 0.0 all-gather.6.cloned.1.call-done
  207.3 3.9 %multiply_convert_fusion.3 = (bf16[384,256]{1,0:T(8,128)(2,1)S(1)}, bf16[384,256]{1,0:T(8,128)(2,1)S(1)}) fusion(f32[384,256]{1,0:T(8,128)} %copy-done.12, f32[384,256]{1,0:T(8,128)} %get-tuple-element.62, bf16[1,256,4096]{2,1,0:T(8,128)(2,1)} %param.15, bf16[384,4096]{1,0:T(8,128)(2,1)} %all-gather.6.cloned.1.call-done, f32[384]{0:T(512)S(1)} %add_divide_fusion.1), kind=kOutput, calls=%fused_computation.26 | convolution fusion | flops 811302912 | bytes 6424064 | tf_op jit(solution)/shard_map/pd,fd->pf/dot_general | solution.py:108
  211.2 1.0 fusion.15
  212.2 2.9 add_convert_fusion
  215.1 0.0 reduce-scatter.5.cloned.1.call-update
  215.1 0.1 convolution_bitcast_fusion
  215.2 3.4 %psum.31 = f32[1,8,1024]{2,1,0:T(8,128)S(1)} all-reduce(f32[1,8,1024]{2,1,0:T(8,128)S(1)} %convolution_bitcast_fusion), channel_id=1, replica_groups=mesh['section'=4,'ex'=4,'ez'=8,'ec'=2] {'ec'}, use_global_device_ids=true, to_apply=%region_13.14 | all-reduce | flops 8192 | bytes 65536 | tf_op jit(solution)/shard_map/psum | solution.py:147
  218.7 24.9 %all_gather.21 = f32[8,8,1024]{2,1,0:T(8,128)S(1)} all-gather(f32[1,8,1024]{2,1,0:T(8,128)S(1)} %psum.31), channel_id=1, replica_groups=mesh['section'=4,'ex'=4,'ez'=8,'ec'=2] {'ez'}, dimensions={0}, use_global_device_ids=true | all-gather | bytes 294912 | tf_op jit(solution)/shard_map/all_gather | solution.py:149
  243.6 12.0 %all-gather = f32[32,1024]{1,0:T(8,128)S(1)} all-gather(f32[8,1024]{1,0:T(8,128)S(1)} %reduce_sum.107), channel_id=2, replica_groups=mesh['section'=4,'ex'=4,'ez'=8,'ec'=2] {'ex'}, dimensions={0}, use_global_device_ids=true | all-gather | bytes 163840 | tf_op jit(solution)/shard_map/all_gather | solution.py:149
  255.6 0.6 bitcast_reduce_fusion
  256.2 2.2 reshape.144
  258.4 8.2 %all-to-all-start.2 = ((bf16[64,48,128]{2,1,0:T(8,128)(2,1)}), bf16[64,48,128]{2,1,0:T(8,128)(2,1)S(1)}, u32[]{:S(2)}, u32[]{:S(2)}) async-start(bf16[64,48,128]{2,1,0:T(8,128)(2,1)} %reshape.144), calls=%async_computation.4 | async-start | bytes 1572864 | tf_op jit(solution)/shard_map/all_to_all | solution.py:151
  266.6 4.7 %fusion.2 = bf16[1,256,4096]{2,1,0:T(8,128)(2,1)} fusion(bf16[384,256]{1,0:T(8,128)(2,1)S(1)} %get-tuple-element.61, bf16[384,4096]{1,0:T(8,128)(2,1)} %all-gather.6.cloned.1.call-done, f32[384]{0:T(512)S(1)} %add_divide_fusion.1), kind=kOutput, calls=%fused_computation.7 | convolution fusion | flops 811073536 | bytes 5441024 | tf_op jit(solution)/shard_map/pf,pd->fd/dot_general | solution.py:109
  271.3 2.6 fusion
  273.9 2.6 fusion.1
  276.5 13.0 %all-to-all-done.2 = bf16[64,48,128]{2,1,0:T(8,128)(2,1)S(1)} async-done(((bf16[64,48,128]{2,1,0:T(8,128)(2,1)}), bf16[64,48,128]{2,1,0:T(8,128)(2,1)S(1)}, u32[]{:S(2)}, u32[]{:S(2)}) %all-to-all-start.2) | async-done | bytes 786464 | tf_op jit(solution)/shard_map/all_to_all | solution.py:151
  289.5 0.1 convert_reduce_fusion
  289.6 0.2 fusion.27
  289.9 0.2 convolution_add_fusion.1
  290.1 0.8 fusion.10
  (42 shorter events, 0.4 us)
Async XLA Ops:
  7.2 107.6 %copy-start = (bf16[1,4096,256]{2,1,0:T(8,128)(2,1)S(1)}, bf16[1,4096,256]{2,1,0:T(8,128)(2,1)}, u32[]{:S(2)}) copy-start(bf16[1,4096,256]{2,1,0:T(8,128)(2,1)} %param.14) | copy-start | bytes 6291460
  7.2 103.9 %all-gather.4.cloned.1.call-start = ((), (), s32[]{:S(2)}) async-start(), calls=%async_computation.5 | async-start | bytes 3932160 | tf_op jit(solution)/shard_map/all_gather | solution.py:65
  68.9 1.2 copy-start.3
  71.1 7.0 %copy-start.6 = (bf16[16,1024]{1,0:T(8,128)(2,1)S(1)}, bf16[16,1024]{1,0:T(8,128)(2,1)}, u32[]{:S(2)}) copy-start(bf16[16,1024]{1,0:T(8,128)(2,1)} %param.9) | copy-start | bytes 98308
  71.1 7.0 %copy-start.7 = (bf16[1024,8]{0,1:T(8,128)(2,1)S(1)}, bf16[1024,8]{0,1:T(8,128)(2,1)}, u32[]{:S(2)}) copy-start(bf16[1024,8]{0,1:T(8,128)(2,1)} %param.12) | copy-start | bytes 49156
  72.4 5.9 %copy-start.2 = (bf16[384,1024]{1,0:T(8,128)(2,1)S(1)}, bf16[384,1024]{1,0:T(8,128)(2,1)}, u32[]{:S(2)}) copy-start(bf16[384,1024]{1,0:T(8,128)(2,1)} %reshape.138) | copy-start | bytes 2359300
  72.4 20.5 %copy-start.9 = (s32[16,2]{0,1:T(2,128)S(1)}, s32[16,2]{0,1:T(2,128)}, u32[]{:S(2)}) copy-start(s32[16,2]{0,1:T(2,128)} %param.11) | copy-start | bytes 388
  72.4 88.2 %reduce-scatter.3.cloned.1.call-start = ((), (), s32[]{:S(2)}) async-start(), calls=%async_computation.6 | async-start | bytes 3932160 | tf_op jit(solution)/shard_map/reduce_scatter | solution.py:100
  111.0 3.7 %copy-start.10 = (bf16[384,4096]{1,0:T(8,128)(2,1)S(1)}, bf16[384,4096]{1,0:T(8,128)(2,1)}, u32[]{:S(2)}) copy-start(bf16[384,4096]{1,0:T(8,128)(2,1)} %all-gather.4.cloned.1.call-done) | copy-start | bytes 9437188
  114.7 1.8 copy-start.12
  114.7 1.8 copy-start.1
  116.5 3.5 %copy-start.4 = (bf16[64,48,128]{2,1,0:T(8,128)(2,1)S(1)}, bf16[64,48,128]{2,1,0:T(8,128)(2,1)}, u32[]{:S(2)}) copy-start(bf16[64,48,128]{2,1,0:T(8,128)(2,1)} %get-tuple-element.48) | copy-start | bytes 2359300
  119.9 87.3 %all-gather.6.cloned.1.call-start = ((), (), s32[]{:S(2)}) async-start(), calls=%async_computation.7 | async-start | bytes 3932160 | tf_op jit(solution)/shard_map/all_gather | solution.py:102
  121.2 75.3 %copy-start.8 = (bf16[16,1024]{1,0:T(8,128)(2,1)S(1)}, bf16[16,1024]{1,0:T(8,128)(2,1)}, u32[]{:S(2)}) copy-start(bf16[16,1024]{1,0:T(8,128)(2,1)} %param.10) | copy-start | bytes 98308
  162.8 33.4 %all-to-all-start.1 = ((bf16[64,48,128]{2,1,0:T(8,128)(2,1)}), bf16[64,48,128]{2,1,0:T(8,128)(2,1)S(1)}, u32[]{:S(2)}, u32[]{:S(2)}) async-start(bf16[64,48,128]{2,1,0:T(8,128)(2,1)} %reshape.141), calls=%async_computation.2 | async-start | bytes 1572864 | tf_op jit(solution)/shard_map/all_to_all | solution.py:105
  173.2 83.0 %reduce-scatter.5.cloned.1.call-start = ((), (), s32[]{:S(2)}) async-start(), calls=%async_computation.8 | async-start | bytes 3932160 | tf_op jit(solution)/shard_map/reduce_scatter | solution.py:143
  207.3 3.9 %copy-start.5 = (bf16[1,4096,256]{2,1,0:T(8,128)(2,1)S(1)}, bf16[1,4096,256]{2,1,0:T(8,128)(2,1)}, u32[]{:S(2)}) copy-start(bf16[1,4096,256]{2,1,0:T(8,128)(2,1)} %param.13) | copy-start | bytes 6291460
  258.4 31.1 %all-to-all-start.2 = ((bf16[64,48,128]{2,1,0:T(8,128)(2,1)}), bf16[64,48,128]{2,1,0:T(8,128)(2,1)S(1)}, u32[]{:S(2)}, u32[]{:S(2)}) async-start(bf16[64,48,128]{2,1,0:T(8,128)(2,1)} %reshape.144), calls=%async_computation.4 | async-start | bytes 1572864 | tf_op jit(solution)/shard_map/all_to_all | solution.py:151
  266.6 4.7 %copy-start.11 = (bf16[384,4096]{1,0:T(8,128)(2,1)S(1)}, bf16[384,4096]{1,0:T(8,128)(2,1)}, u32[]{:S(2)}) copy-start(bf16[384,4096]{1,0:T(8,128)(2,1)} %all-gather.4.cloned.1.call-done) | copy-start | bytes 9437188
Sparse Core Ops, SparseCore 0:
  72.5 38.4 all-gather.3
  120.1 40.4 reduce-scatter.2
  163.0 42.3 all-gather.5
  215.2 38.6 reduce-scatter.4

commit v9 on v8

--- a/solution.py
+++ b/solution.py
@@ -91,13 +91,8 @@
     sigmoid_gate = jax.nn.sigmoid(pre_gate)
     activated = pre_gate * sigmoid_gate
     hidden = (activated * pre_up).astype(jnp.bfloat16)
-    hid = gate_local.shape[1]
-    down_blocks = down_local.reshape(hid, n_section, width)
-    gate_blocks = gate_local.reshape(n_section, width, hid)
-    up_blocks = up_local.reshape(n_section, width, hid)
-    out_piece = jnp.einsum("pf,fsd->spd", hidden, down_blocks, preferred_element_type=jnp.float32)
-    out_piece = out_piece.astype(jnp.bfloat16).reshape(n_section * row_total, width)
-    out_red = lax.psum_scatter(out_piece, "section", scatter_dimension=0, tiled=True)
+    out_piece = jnp.dot(hidden, down_local, preferred_element_type=jnp.float32).astype(jnp.bfloat16)
+    out_red = lax.psum_scatter(out_piece, "section", scatter_dimension=1, tiled=True)
     out_red, cot_recv = lax.optimization_barrier((out_red, cot_recv))
     cot_rows = lax.all_gather(cot_recv, "section", axis=1, tiled=True)
     dy_rows = (row_gate[:, None] * cot_rows.astype(jnp.float32)).astype(jnp.bfloat16)
@@ -129,18 +124,18 @@
     local_inner = jnp.stack(
         [jnp.sum(cot_float * out_first, axis=1), jnp.sum(cot_float * out_second, axis=1)], axis=1
     )
-    dx_piece = jnp.einsum("pf,sdf->spd", d_pre_gate, gate_blocks, preferred_element_type=jnp.float32)
+    dx_piece = jnp.einsum("pf,df->pd", d_pre_gate, gate_local, preferred_element_type=jnp.float32)
     dx_piece = dx_piece + jnp.einsum(
-        "pf,sdf->spd", d_pre_up, up_blocks, preferred_element_type=jnp.float32
+        "pf,df->pd", d_pre_up, up_local, preferred_element_type=jnp.float32
     )
     gate_inner = lax.psum(local_inner, "section")
     d_first = gate_first * gate_second * (gate_inner[:, 0] - gate_inner[:, 1])
     d_logits = jnp.where(route_hot[:, 0, :], d_first[:, None], zero_f) - jnp.where(
         route_hot[:, 1, :], d_first[:, None], zero_f
     )
-    dx_piece = dx_piece.astype(jnp.bfloat16).reshape(n_section * row_total, width)
+    dx_piece = dx_piece.astype(jnp.bfloat16)
     d_logits, dx_piece = lax.optimization_barrier((d_logits, dx_piece))
-    dx_red = lax.psum_scatter(dx_piece, "section", scatter_dimension=0, tiled=True)
+    dx_red = lax.psum_scatter(dx_piece, "section", scatter_dimension=1, tiled=True)
     router_part = jnp.einsum(
         "te,tf->ef", d_logits, tokens.astype(jnp.float32), precision=highest
     )

time: 301 us -> 301 us (level)
  waiting for transfers between devices: 93.3 us -> 96.8 us
    another operation x1 -> x0, local copies, waits for them, and re-layouts: 4.54 us -> none  [per_device(): down_blocks = down_local.reshape(hid, n_section, width)]
    all_gather x1, waiting for transfers between devices: 18 us -> 21.5 us  [per_device(): x_rows = lax.all_gather(x_recv, 'section', axis=1, tiled=True)]
  transfers between devices with their start and end apart: 6 -> 6, of which waited for: 4 -> 4; matrix products, arithmetic and copies ran while one was open for 7% -> 6% of each run, Pallas kernels for 0% -> 0%
where the time goes in v9:
time: 301 us; the launch traced here: 298 us
  blocking collectives  121 us (40%)
  waiting for transfers between devices  96.8 us (32%)
  matrix products  30.4 us (10%)
  starting transfers between devices  19 us (6%)
  between operations  14.1 us (5%)
  local copies, waits for them, and re-layouts  13.5 us (4%)
  other arithmetic  3.15 us (1%)
    all_to_all x1, blocking collectives, per_device(): received = lax.all_to_all(sent, EXPERT_AXES, 0, 0, tiled=True)  57.1 us
    reduce_scatter x1, waiting for transfers between devices, per_device(): lax.psum_scatter(out_piece, 'section', scatter_dimension=1, tiled=True)  39.4 us
    all_gather x2, blocking collectives, per_device(): router_part = jnp.sum(lax.all_gather(router_part, name, axis=0), axis=0)  37.1 us
    all_to_all x1, waiting for transfers between devices, per_device(): lax.all_to_all(out_red.reshape(n_dev, half, LANES), EXPERT_AXES, 0, 0, ti...  22.9 us
    all_gather x1, waiting for transfers between devices, per_device(): x_rows = lax.all_gather(x_recv, 'section', axis=1, tiled=True)  21.5 us
    psum x1, blocking collectives, per_device(): lax.psum(jnp.dot(x_recv, w_router, preferred_element_type=jnp.float32), '...  14.2 us
    all_to_all x1, waiting for transfers between devices, per_device(): lax.all_to_all(dx_red.reshape(n_dev, half, LANES), EXPERT_AXES, 0, 0, til...  13 us
    all_to_all x1, starting transfers between devices, per_device(): lax.all_to_all(out_red.reshape(n_dev, half, LANES), EXPERT_AXES, 0, 0, ti...  10.4 us
  transfers between devices with their start and end apart: 6, of which 4 were waited for; matrix products, arithmetic and copies ran while one was open for 6% of the time, Pallas kernels for 0%

profile of v9, /device:TPU:8, one launch (start us, length us, event | category | flops | bytes accessed | tf_op | source)
XLA Modules:
  0.0 298.1 jit_solution(1303704272062600097)
XLA Ops:
  7.2 0.0 all-gather.4.cloned.1.call-start
  7.2 0.9 copy.34
  8.1 0.1 eq.77
  8.2 0.1 fusion.23
  8.3 0.1 reduce_window_sum.11
  8.3 0.2 select_reduce_fusion
  8.5 0.1 reshape.128
  8.6 0.1 copy.35
  8.7 0.7 multiply_add_fusion
  9.4 0.8 slice_bitcast_fusion.3
  10.2 0.1 add_reduce_fusion
  10.3 0.1 convert_element_type.110
  10.3 1.1 convolution_convert_fusion.4
  11.6 0.2 broadcast_in_dim.95
  11.9 57.1 %all_to_all.15 = bf16[64,112,128]{2,1,0:T(8,128)(2,1)S(1)} all-to-all(bf16[64,112,128]{2,1,0:T(8,128)(2,1)S(1)} %bitcast.85), channel_id=1, replica_groups=mesh['section'=4,'ex'=4,'ez'=8,'ec'=2] {'ex','ez','ec'}, dimensions={0} | all-to-all | bytes 3670016 | tf_op jit(solution)/shard_map/all_to_all | solution.py:62
  68.9 1.2 copy-done.1
  70.2 1.0 fusion.36
  71.1 2.1 reshape.132
  73.3 0.0 all-gather.4.cloned.1.call-update
  73.3 0.0 reduce-scatter.3.cloned.1.call-start
  73.4 1.0 fusion.22
  74.4 0.1 reshape.138
  74.6 0.1 convolution_bitcast_fusion.1
  74.7 1.4 fusion.38
  76.1 14.2 %all-reduce.1 = (f32[384,8]{0,1:T(8,128)S(1)}, f32[16,8]{0,1:T(8,128)S(1)}) all-reduce(f32[384,8]{0,1:T(8,128)S(1)} %fusion.38, f32[16,8]{0,1:T(8,128)S(1)} %convolution_bitcast_fusion.1), channel_id=1, replica_groups=mesh['section'=4,'ex'=4,'ez'=8,'ec'=2] {'section'}, use_global_device_ids=true, to_apply=%region_3.4 | all-reduce | flops 3200 | bytes 25600 | tf_op jit(solution)/shard_map/psum | solution.py:75
  90.4 0.1 select_reduce_fusion.1
  90.5 21.5 %all-gather.4.cloned.1.call-done = bf16[384,4096]{1,0:T(8,128)(2,1)} async-done(((bf16[384,1024]{1,0:T(8,128)(2,1)}), bf16[384,4096]{1,0:T(8,128)(2,1)}) %all-gather.4.cloned.1.call-update) | async-done | bytes 3145744 | tf_op jit(solution)/shard_map/all_gather | solution.py:65
  111.9 3.7 %fusion.11 = f32[384,256]{1,0:T(8,128)S(1)} fusion(bf16[384,4096]{1,0:T(8,128)(2,1)} %all-gather.4.cloned.1.call-done, bf16[1,4096,256]{2,1,0:T(8,128)(2,1)} %param.13), kind=kOutput, calls=%fused_computation.18 | convolution fusion | flops 805306368 | bytes 5636096 | tf_op jit(solution)/shard_map/dot_general | solution.py:89
  115.6 0.4 copy-done.9
  116.0 1.7 multiply_convert_fusion.5
  117.8 2.7 convolution_convert_fusion
  120.4 0.0 reduce-scatter.3.cloned.1.call-update
  120.5 0.0 all-gather.6.cloned.1.call-start
  120.5 1.2 reshape.133
  121.7 39.4 %reduce-scatter.3.cloned.1.call-done = bf16[384,1024]{1,0:T(8,128)(2,1)} async-done(((bf16[384,4096]{1,0:T(8,128)(2,1)}), bf16[384,1024]{1,0:T(8,128)(2,1)}) %reduce-scatter.3.cloned.1.call-update) | async-done | bytes 786448 | tf_op jit(solution)/shard_map/reduce_scatter | solution.py:95
  161.1 0.0 all-gather.6.cloned.1.call-update
  161.2 2.2 reshape.134
  163.3 10.4 %all-to-all-start.1 = ((bf16[64,48,128]{2,1,0:T(8,128)(2,1)}), bf16[64,48,128]{2,1,0:T(8,128)(2,1)S(1)}, u32[]{:S(2)}, u32[]{:S(2)}) async-start(bf16[64,48,128]{2,1,0:T(8,128)(2,1)} %reshape.134), calls=%async_computation.2 | async-start | bytes 1572864 | tf_op jit(solution)/shard_map/all_to_all | solution.py:100
  173.8 0.0 reduce-scatter.5.cloned.1.call-start
  173.8 22.9 %all-to-all-done.1 = bf16[64,48,128]{2,1,0:T(8,128)(2,1)S(1)} async-done(((bf16[64,48,128]{2,1,0:T(8,128)(2,1)}), bf16[64,48,128]{2,1,0:T(8,128)(2,1)S(1)}, u32[]{:S(2)}, u32[]{:S(2)}) %all-to-all-start.1) | async-done | bytes 786464 | tf_op jit(solution)/shard_map/all_to_all | solution.py:100
  196.7 0.1 convert_reduce_fusion.1
  196.8 0.2 fusion.24
  197.1 1.0 fusion.17
  198.1 9.6 %psum.30 = f32[16,2]{0,1:T(2,128)S(1)} all-reduce(f32[16,2]{0,1:T(2,128)S(1)} %pad_maximum_fusion), channel_id=1, replica_groups=mesh['section'=4,'ex'=4,'ez'=8,'ec'=2] {'section'}, use_global_device_ids=true, to_apply=%region_12.13 | all-reduce | flops 32 | bytes 256 | tf_op jit(solution)/shard_map/psum | solution.py:131
  207.6 0.0 all-gather.6.cloned.1.call-done
  207.7 3.3 %multiply_convert_fusion.3 = (bf16[384,256]{1,0:T(8,128)(2,1)S(1)}, bf16[384,256]{1,0:T(8,128)(2,1)S(1)}) fusion(f32[384,256]{1,0:T(8,128)} %copy-done.11, f32[384,256]{1,0:T(8,128)} %get-tuple-element.62, bf16[1,256,4096]{2,1,0:T(8,128)(2,1)S(1)} %copy-done, bf16[384,4096]{1,0:T(8,128)(2,1)} %all-gather.6.cloned.1.call-done, f32[384]{0:T(512)S(1)} %add_divide_fusion.1), kind=kOutput, calls=%fused_computation.29 | convolution fusion | flops 811302912 | bytes 6424064 | tf_op jit(solution)/shard_map/pd,fd->pf/dot_general | solution.py:103
  211.0 1.0 fusion.9
  212.0 0.6 copy-done.4
  212.6 2.8 add_convert_fusion
  215.4 0.1 convolution_bitcast_fusion
  215.5 3.4 %psum.31 = f32[1,8,1024]{2,1,0:T(8,128)S(1)} all-reduce(f32[1,8,1024]{2,1,0:T(8,128)S(1)} %convolution_bitcast_fusion), channel_id=1, replica_groups=mesh['section'=4,'ex'=4,'ez'=8,'ec'=2] {'ec'}, use_global_device_ids=true, to_apply=%region_13.14 | all-reduce | flops 8192 | bytes 65536 | tf_op jit(solution)/shard_map/psum | solution.py:142
  218.9 24.9 %all_gather.21 = f32[8,8,1024]{2,1,0:T(8,128)S(1)} all-gather(f32[1,8,1024]{2,1,0:T(8,128)S(1)} %psum.31), channel_id=1, replica_groups=mesh['section'=4,'ex'=4,'ez'=8,'ec'=2] {'ez'}, dimensions={0}, use_global_device_ids=true | all-gather | bytes 294912 | tf_op jit(solution)/shard_map/all_gather | solution.py:144
  243.9 12.2 %all-gather = f32[32,1024]{1,0:T(8,128)S(1)} all-gather(f32[8,1024]{1,0:T(8,128)S(1)} %reduce_sum.107), channel_id=2, replica_groups=mesh['section'=4,'ex'=4,'ez'=8,'ec'=2] {'ex'}, dimensions={0}, use_global_device_ids=true | all-gather | bytes 163840 | tf_op jit(solution)/shard_map/all_gather | solution.py:144
  256.1 0.6 bitcast_reduce_fusion
  256.7 2.2 reshape.136
  258.8 8.4 %all-to-all-start.2 = ((bf16[64,48,128]{2,1,0:T(8,128)(2,1)}), bf16[64,48,128]{2,1,0:T(8,128)(2,1)S(1)}, u32[]{:S(2)}, u32[]{:S(2)}) async-start(bf16[64,48,128]{2,1,0:T(8,128)(2,1)} %reshape.136), calls=%async_computation.4 | async-start | bytes 1572864 | tf_op jit(solution)/shard_map/all_to_all | solution.py:146
  267.2 4.7 %fusion.2 = bf16[1,256,4096]{2,1,0:T(8,128)(2,1)} fusion(bf16[384,256]{1,0:T(8,128)(2,1)S(1)} %get-tuple-element.61, bf16[384,4096]{1,0:T(8,128)(2,1)} %all-gather.6.cloned.1.call-done, f32[384]{0:T(512)S(1)} %add_divide_fusion.1), kind=kOutput, calls=%fused_computation.8 | convolution fusion | flops 811073536 | bytes 5441024 | tf_op jit(solution)/shard_map/pf,pd->fd/dot_general | solution.py:104
  271.9 2.6 fusion
  274.6 2.6 fusion.1
  277.2 13.0 %all-to-all-done.2 = bf16[64,48,128]{2,1,0:T(8,128)(2,1)S(1)} async-done(((bf16[64,48,128]{2,1,0:T(8,128)(2,1)}), bf16[64,48,128]{2,1,0:T(8,128)(2,1)S(1)}, u32[]{:S(2)}, u32[]{:S(2)}) %all-to-all-start.2) | async-done | bytes 786464 | tf_op jit(solution)/shard_map/all_to_all | solution.py:146
  290.1 0.1 convert_reduce_fusion
  290.3 0.2 fusion.26
  290.5 0.2 convolution_add_fusion.1
  290.7 0.8 fusion.13
  (39 shorter events, 0.4 us)
Async XLA Ops:
  7.2 110.6 %copy-start = (bf16[1,256,4096]{2,1,0:T(8,128)(2,1)S(1)}, bf16[1,256,4096]{2,1,0:T(8,128)(2,1)}, u32[]{:S(2)}) copy-start(bf16[1,256,4096]{2,1,0:T(8,128)(2,1)} %param.15) | copy-start | bytes 6291460
  7.2 104.7 %all-gather.4.cloned.1.call-start = ((), (), s32[]{:S(2)}) async-start(), calls=%async_computation.5 | async-start | bytes 3932160 | tf_op jit(solution)/shard_map/all_gather | solution.py:65
  68.9 1.2 copy-start.1
  70.2 4.4 %copy-start.5 = (bf16[16,1024]{1,0:T(8,128)(2,1)S(1)}, bf16[16,1024]{1,0:T(8,128)(2,1)}, u32[]{:S(2)}) copy-start(bf16[16,1024]{1,0:T(8,128)(2,1)} %param.9) | copy-start | bytes 98308
  70.2 4.4 %copy-start.6 = (bf16[1024,8]{0,1:T(8,128)(2,1)S(1)}, bf16[1024,8]{0,1:T(8,128)(2,1)}, u32[]{:S(2)}) copy-start(bf16[1024,8]{0,1:T(8,128)(2,1)} %param.12) | copy-start | bytes 49156
  70.2 20.2 %copy-start.8 = (s32[16,2]{0,1:T(2,128)S(1)}, s32[16,2]{0,1:T(2,128)}, u32[]{:S(2)}) copy-start(s32[16,2]{0,1:T(2,128)} %param.11) | copy-start | bytes 388
  73.3 87.8 %reduce-scatter.3.cloned.1.call-start = ((), (), s32[]{:S(2)}) async-start(), calls=%async_computation.6 | async-start | bytes 3932160 | tf_op jit(solution)/shard_map/reduce_scatter | solution.py:95
  111.9 3.7 %copy-start.3 = (bf16[1,4096,256]{2,1,0:T(8,128)(2,1)S(1)}, bf16[1,4096,256]{2,1,0:T(8,128)(2,1)}, u32[]{:S(2)}) copy-start(bf16[1,4096,256]{2,1,0:T(8,128)(2,1)} %param.14) | copy-start | bytes 6291460
  111.9 4.1 %copy-start.9 = (bf16[384,4096]{1,0:T(8,128)(2,1)S(1)}, bf16[384,4096]{1,0:T(8,128)(2,1)}, u32[]{:S(2)}) copy-start(bf16[384,4096]{1,0:T(8,128)(2,1)} %all-gather.4.cloned.1.call-done) | copy-start | bytes 9437188
  116.0 1.7 copy-start.11
  120.5 87.2 %all-gather.6.cloned.1.call-start = ((), (), s32[]{:S(2)}) async-start(), calls=%async_computation.7 | async-start | bytes 3932160 | tf_op jit(solution)/shard_map/all_gather | solution.py:97
  121.7 75.3 %copy-start.7 = (bf16[16,1024]{1,0:T(8,128)(2,1)S(1)}, bf16[16,1024]{1,0:T(8,128)(2,1)}, u32[]{:S(2)}) copy-start(bf16[16,1024]{1,0:T(8,128)(2,1)} %param.10) | copy-start | bytes 98308
  163.3 33.4 %all-to-all-start.1 = ((bf16[64,48,128]{2,1,0:T(8,128)(2,1)}), bf16[64,48,128]{2,1,0:T(8,128)(2,1)S(1)}, u32[]{:S(2)}, u32[]{:S(2)}) async-start(bf16[64,48,128]{2,1,0:T(8,128)(2,1)} %reshape.134), calls=%async_computation.2 | async-start | bytes 1572864 | tf_op jit(solution)/shard_map/all_to_all | solution.py:100
  173.8 82.9 %reduce-scatter.5.cloned.1.call-start = ((), (), s32[]{:S(2)}) async-start(), calls=%async_computation.8 | async-start | bytes 3932160 | tf_op jit(solution)/shard_map/reduce_scatter | solution.py:138
  207.7 3.3 %copy-start.2 = (bf16[1,4096,256]{2,1,0:T(8,128)(2,1)S(1)}, bf16[1,4096,256]{2,1,0:T(8,128)(2,1)}, u32[]{:S(2)}) copy-start(bf16[1,4096,256]{2,1,0:T(8,128)(2,1)} %param.13) | copy-start | bytes 6291460
  211.0 1.6 copy-start.4
  258.8 31.3 %all-to-all-start.2 = ((bf16[64,48,128]{2,1,0:T(8,128)(2,1)}), bf16[64,48,128]{2,1,0:T(8,128)(2,1)S(1)}, u32[]{:S(2)}, u32[]{:S(2)}) async-start(bf16[64,48,128]{2,1,0:T(8,128)(2,1)} %reshape.136), calls=%async_computation.4 | async-start | bytes 1572864 | tf_op jit(solution)/shard_map/all_to_all | solution.py:146
  267.2 4.7 %copy-start.10 = (bf16[384,4096]{1,0:T(8,128)(2,1)S(1)}, bf16[384,4096]{1,0:T(8,128)(2,1)}, u32[]{:S(2)}) copy-start(bf16[384,4096]{1,0:T(8,128)(2,1)} %all-gather.4.cloned.1.call-done) | copy-start | bytes 9437188
Sparse Core Ops, SparseCore 0:
  73.4 38.4 all-gather.3
  120.6 40.5 reduce-scatter.2
  163.5 42.4 all-gather.5
  215.5 38.8 reduce-scatter.4

commit v10 on v7

--- a/solution.py
+++ b/solution.py
@@ -47,24 +47,22 @@
     half = capacity * width // LANES
     meta = jnp.zeros((experts, 16, LANES), jnp.bfloat16)
     meta = meta.at[:, 0, :capacity].set(other_slot.reshape(experts, capacity).astype(jnp.bfloat16))
-    both_source = jnp.concatenate(
-        [
-            selected[:, :width].reshape(experts, half, LANES),
-            selected[:, width:].reshape(experts, half, LANES),
-            meta,
-        ],
-        axis=1,
-    )
-    block_rows = both_source.shape[1]
-    sent = jnp.broadcast_to(
-        both_source[:, None], (experts, groups, block_rows, LANES)
-    ).reshape(experts * groups, block_rows, LANES)
-    received = lax.all_to_all(sent, EXPERT_AXES, 0, 0, tiled=True)
-    row_total = received.shape[0] * capacity
-    x_recv = received[:, :half].reshape(row_total, width)
+    def spread(block):
+        rows = block.shape[1]
+        return jnp.broadcast_to(block[:, None], (experts, groups, rows, LANES)).reshape(
+            experts * groups, rows, LANES
+        )
+
+    x_block = selected[:, :width].reshape(experts, half, LANES)
+    c_block = jnp.concatenate([selected[:, width:].reshape(experts, half, LANES), meta], axis=1)
+    x_recv = lax.all_to_all(spread(x_block), EXPERT_AXES, 0, 0, tiled=True)
+    row_total = x_recv.shape[0] * capacity
+    x_recv = x_recv.reshape(row_total, width)
     x_rows = lax.all_gather(x_recv, "section", axis=1, tiled=True)
-    cot_recv = received[:, half : 2 * half].reshape(row_total, width)
-    other_recv = received[:, 2 * half, :capacity].astype(jnp.int32).reshape(row_total)
+    c_block, x_recv = lax.optimization_barrier((c_block, x_recv))
+    c_recv = lax.all_to_all(spread(c_block), EXPERT_AXES, 0, 0, tiled=True)
+    cot_recv = c_recv[:, :half].reshape(row_total, width)
+    other_recv = c_recv[:, half, :capacity].astype(jnp.int32).reshape(row_total)
     w_router, x_recv = lax.optimization_barrier((w_router, x_recv))
     partial_logits = jnp.dot(tokens, w_router, preferred_element_type=jnp.float32)
     logits = lax.psum(partial_logits, "section")
@@ -95,7 +93,9 @@
     out_piece = jnp.einsum("pf,fsd->spd", hidden, down_blocks, preferred_element_type=jnp.float32)
     out_piece = out_piece.astype(jnp.bfloat16).reshape(n_section * row_total, width)
     out_red = lax.psum_scatter(out_piece, "section", scatter_dimension=0, tiled=True)
-    out_red, cot_recv = lax.optimization_barrier((out_red, cot_recv))
+    out_red, cot_recv, row_gate, gate_first, gate_second = lax.optimization_barrier(
+        (out_red, cot_recv, row_gate, gate_first, gate_second)
+    )
     cot_rows = lax.all_gather(cot_recv, "section", axis=1, tiled=True)
     dy_rows = (row_gate[:, None] * cot_rows.astype(jnp.float32)).astype(jnp.bfloat16)
     n_dev = row_total // capacity

time: 305 us -> 276 us (0.905)
  waiting for transfers between devices: 106 us -> 82.6 us
  blocking collectives: 112 us -> 99.8 us
  starting transfers between devices: 16.9 us -> 26.3 us
    reduce_scatter x1, waiting for transfers between devices: 38.4 us -> 0.01 us  [per_device(): lax.psum_scatter(out_piece, 'section', scatter_dimension=0, tiled=True)]
    all_to_all x1, blocking collectives: 57.1 us -> 34.7 us  [per_device(): x_recv = lax.all_to_all(spread(x_block), EXPERT_AXES, 0, 0, tiled=True)]
    all_to_all x0 -> x1, waiting for transfers between devices: none -> 12.5 us  [per_device(): c_recv = lax.all_to_all(spread(c_block), EXPERT_AXES, 0, 0, tiled=True)]
    all_to_all x0 -> x1, starting transfers between devices: none -> 10.7 us  [per_device(): c_recv = lax.all_to_all(spread(c_block), EXPERT_AXES, 0, 0, tiled=True)]
    psum x1 -> x2, blocking collectives: 14.9 us -> 24.9 us  [the longest x1 15 us: per_device(): lax.psum(jnp.dot(x_recv, w_router, preferred_element_type=jnp.float32), '...]
    all_to_all x1, starting transfers between devices: 10.7 us -> 7.42 us  [per_device(): lax.all_to_all(out_red.reshape(n_dev, half, LANES), EXPERT_AXES, 0, 0, ti...]
  transfers between devices with their start and end apart: 6 -> 7, of which waited for: 4 -> 4; matrix products, arithmetic and copies ran while one was open for 8% -> 9% of each run, Pallas kernels for 0% -> 0%
where the time goes in v10:
time: 276 us; the launch traced here: 273 us
  blocking collectives  99.8 us (36%)
  waiting for transfers between devices  82.6 us (30%)
  matrix products  30.6 us (11%)
  starting transfers between devices  26.3 us (10%)
  local copies, waits for them, and re-layouts  16.1 us (6%)
  between operations  14.1 us (5%)
  other arithmetic  3.15 us (1%)
    all_gather x2, blocking collectives, per_device(): router_part = jnp.sum(lax.all_gather(router_part, name, axis=0), axis=0)  36.9 us
    all_to_all x1, blocking collectives, per_device(): x_recv = lax.all_to_all(spread(x_block), EXPERT_AXES, 0, 0, tiled=True)  34.7 us
    all_gather x1, waiting for transfers between devices, per_device(): x_rows = lax.all_gather(x_recv, 'section', axis=1, tiled=True)  34.1 us
    all_to_all x1, waiting for transfers between devices, per_device(): lax.all_to_all(out_red.reshape(n_dev, half, LANES), EXPERT_AXES, 0, 0, ti...  22.9 us
    psum x1, blocking collectives, per_device(): lax.psum(jnp.dot(x_recv, w_router, preferred_element_type=jnp.float32), '...  15 us
    all_to_all x1, waiting for transfers between devices, per_device(): lax.all_to_all(dx_red.reshape(n_dev, half, LANES), EXPERT_AXES, 0, 0, til...  13 us
    all_to_all x1, waiting for transfers between devices, per_device(): c_recv = lax.all_to_all(spread(c_block), EXPERT_AXES, 0, 0, tiled=True)  12.5 us
    all_to_all x1, starting transfers between devices, per_device(): c_recv = lax.all_to_all(spread(c_block), EXPERT_AXES, 0, 0, tiled=True)  10.7 us
  transfers between devices with their start and end apart: 7, of which 4 were waited for; matrix products, arithmetic and copies ran while one was open for 9% of the time, Pallas kernels for 0%

profile of v10, /device:TPU:8, one launch (start us, length us, event | category | flops | bytes accessed | tf_op | source)
XLA Modules:
  0.0 272.7 jit_solution(3072837394174638950)
XLA Ops:
  7.2 0.0 all-gather.4.cloned.1.call-start
  7.2 0.9 copy.41
  8.1 0.1 eq.76
  8.2 0.1 fusion.24
  8.3 0.1 reduce_window_sum.11
  8.3 0.2 select_reduce_fusion
  8.5 0.1 reshape.135
  8.6 0.1 copy.42
  8.7 0.7 multiply_add_fusion
  9.4 0.8 slice_bitcast_fusion.3
  10.2 1.1 convolution_convert_fusion.4
  11.3 0.1 broadcast_in_dim.98
  11.4 34.7 %all_to_all.20 = bf16[64,48,128]{2,1,0:T(8,128)(2,1)S(1)} all-to-all(bf16[64,48,128]{2,1,0:T(8,128)(2,1)S(1)} %bitcast.100), channel_id=1, replica_groups=mesh['section'=4,'ex'=4,'ez'=8,'ec'=2] {'ex','ez','ec'}, dimensions={0} | all-to-all | bytes 1572864 | tf_op jit(solution)/shard_map/all_to_all | solution.py:58
  46.1 1.2 reshape.137
  47.3 0.0 all-gather.4.cloned.1.call-update
  47.3 0.0 reduce-scatter.3.cloned.1.call-start
  47.4 4.5 %reshape_squeeze.9 = bf16[256,4,1024]{2,1,0:T(4,128)(2,1)} reshape(bf16[1,256,4096]{2,1,0:T(8,128)(2,1)} %param.15) | data formatting | bytes 4194304 | tf_op jit(solution)/shard_map/reshape;squeeze | solution.py:90
  51.9 34.1 %all-gather.4.cloned.1.call-done = bf16[384,4096]{1,0:T(8,128)(2,1)} async-done(((bf16[384,1024]{1,0:T(8,128)(2,1)}), bf16[384,4096]{1,0:T(8,128)(2,1)}) %all-gather.4.cloned.1.call-update) | async-done | bytes 3145744 | tf_op jit(solution)/shard_map/all_gather | solution.py:61
  86.0 3.7 %fusion.7 = f32[384,256]{1,0:T(8,128)S(1)} fusion(bf16[384,4096]{1,0:T(8,128)(2,1)} %all-gather.4.cloned.1.call-done, bf16[1,4096,256]{2,1,0:T(8,128)(2,1)} %param.13), kind=kOutput, calls=%fused_computation.14 | convolution fusion | flops 805306368 | bytes 5636096 | tf_op jit(solution)/shard_map/dot_general | solution.py:84
  89.7 1.8 multiply_convert_fusion.5
  91.5 3.4 %convolution_convert_fusion.3 = bf16[384,4,1024]{2,0,1:T(8,128)(2,1)} fusion(bf16[256,4,1024]{2,1,0:T(4,128)(2,1)S(1)} %copy-done.1, bf16[384,256]{1,0:T(8,128)(2,1)S(1)} %get-tuple-element.61), kind=kOutput, calls=%fused_computation.8 | convolution fusion | flops 806879232 | bytes 5439488 | tf_op jit(solution)/shard_map/pf,fsd->spd/dot_general | solution.py:93
  94.9 0.0 reduce-scatter.3.cloned.1.call-update
  94.9 0.1 add_reduce_fusion
  95.0 0.1 convert_element_type.118
  95.2 1.2 broadcast_in_dim.104
  96.4 10.7 %all-to-all-start.1 = ((bf16[64,64,128]{2,1,0:T(8,128)(2,1)}), bf16[64,64,128]{2,1,0:T(8,128)(2,1)}, u32[]{:S(2)}, u32[]{:S(2)}) async-start(bf16[64,64,128]{2,1,0:T(8,128)(2,1)} %bitcast.99), calls=%async_computation.2 | async-start | bytes 2097152 | tf_op jit(solution)/shard_map/all_to_all | solution.py:63
  107.1 0.0 all-gather.6.cloned.1.call-start
  107.2 0.1 convolution_bitcast_fusion.1
  107.3 0.3 fusion.38
  107.6 15.0 %all-reduce.1 = (f32[384,8]{0,1:T(8,128)S(1)}, f32[16,8]{0,1:T(8,128)S(1)}) all-reduce(f32[384,8]{0,1:T(8,128)S(1)} %fusion.38, f32[16,8]{0,1:T(8,128)S(1)} %convolution_bitcast_fusion.1), channel_id=1, replica_groups=mesh['section'=4,'ex'=4,'ez'=8,'ec'=2] {'section'}, use_global_device_ids=true, to_apply=%region_4.5 | all-reduce | flops 3200 | bytes 25600 | tf_op jit(solution)/shard_map/psum | solution.py:73
  122.6 12.5 %all-to-all-done.1 = bf16[64,64,128]{2,1,0:T(8,128)(2,1)} async-done(((bf16[64,64,128]{2,1,0:T(8,128)(2,1)}), bf16[64,64,128]{2,1,0:T(8,128)(2,1)}, u32[]{:S(2)}, u32[]{:S(2)}) %all-to-all-start.1) | async-done | bytes 1048608 | tf_op jit(solution)/shard_map/all_to_all | solution.py:63
  135.1 1.0 fusion.23
  136.2 0.1 reshape.147
  136.3 1.2 slice.83
  137.5 1.2 reshape.141
  138.7 0.1 select_reduce_fusion.1
  138.8 0.0 all-gather.6.cloned.1.call-update
  138.9 2.2 reshape.142
  141.0 7.4 %all-to-all-start.2 = ((bf16[64,48,128]{2,1,0:T(8,128)(2,1)}), bf16[64,48,128]{2,1,0:T(8,128)(2,1)S(1)}, u32[]{:S(2)}, u32[]{:S(2)}) async-start(bf16[64,48,128]{2,1,0:T(8,128)(2,1)} %reshape.142), calls=%async_computation.3 | async-start | bytes 1572864 | tf_op jit(solution)/shard_map/all_to_all | solution.py:102
  148.4 0.0 reduce-scatter.5.cloned.1.call-start
  148.5 22.9 %all-to-all-done.2 = bf16[64,48,128]{2,1,0:T(8,128)(2,1)S(1)} async-done(((bf16[64,48,128]{2,1,0:T(8,128)(2,1)}), bf16[64,48,128]{2,1,0:T(8,128)(2,1)S(1)}, u32[]{:S(2)}, u32[]{:S(2)}) %all-to-all-start.2) | async-done | bytes 786464 | tf_op jit(solution)/shard_map/all_to_all | solution.py:102
  171.4 0.1 convert_reduce_fusion.1
  171.5 0.2 fusion.25
  171.7 1.0 fusion.18
  172.7 9.9 %psum.30 = f32[16,2]{0,1:T(2,128)S(1)} all-reduce(f32[16,2]{0,1:T(2,128)S(1)} %pad_maximum_fusion), channel_id=1, replica_groups=mesh['section'=4,'ex'=4,'ez'=8,'ec'=2] {'section'}, use_global_device_ids=true, to_apply=%region_12.13 | all-reduce | flops 32 | bytes 256 | tf_op jit(solution)/shard_map/psum | solution.py:133
  182.7 0.0 all-gather.6.cloned.1.call-done
  182.7 3.9 %multiply_convert_fusion.3 = (bf16[384,256]{1,0:T(8,128)(2,1)S(1)}, bf16[384,256]{1,0:T(8,128)(2,1)S(1)}) fusion(f32[384,256]{1,0:T(8,128)} %copy-done.10, f32[384,256]{1,0:T(8,128)} %get-tuple-element.62, bf16[1,256,4096]{2,1,0:T(8,128)(2,1)} %param.15, bf16[384,4096]{1,0:T(8,128)(2,1)} %all-gather.6.cloned.1.call-done, f32[384]{0:T(512)S(1)} %add_divide_fusion.1), kind=kOutput, calls=%fused_computation.24 | convolution fusion | flops 811302912 | bytes 6424064 | tf_op jit(solution)/shard_map/pd,fd->pf/dot_general | solution.py:105
  186.6 1.0 fusion.14
  187.6 2.9 %add_convert_fusion = bf16[384,4,1024]{2,0,1:T(8,128)(2,1)} fusion(f32[384,4,1024]{2,0,1:T(8,128)S(1)} %fusion.14, bf16[4,1024,256]{2,1,0:T(8,128)(2,1)S(1)} %bitcast.96, bf16[384,256]{1,0:T(8,128)(2,1)S(1)} %get-tuple-element.50), kind=kOutput, calls=%fused_computation | convolution fusion | flops 808452096 | bytes 11730944 | tf_op jit(solution)/shard_map/pf,sdf->spd/dot_general | solution.py:130
  190.5 0.1 convolution_bitcast_fusion
  190.7 3.4 %psum.31 = f32[1,8,1024]{2,1,0:T(8,128)S(1)} all-reduce(f32[1,8,1024]{2,1,0:T(8,128)S(1)} %convolution_bitcast_fusion), channel_id=1, replica_groups=mesh['section'=4,'ex'=4,'ez'=8,'ec'=2] {'ec'}, use_global_device_ids=true, to_apply=%region_13.14 | all-reduce | flops 8192 | bytes 65536 | tf_op jit(solution)/shard_map/psum | solution.py:144
  194.1 24.9 %all_gather.21 = f32[8,8,1024]{2,1,0:T(8,128)S(1)} all-gather(f32[1,8,1024]{2,1,0:T(8,128)S(1)} %psum.31), channel_id=1, replica_groups=mesh['section'=4,'ex'=4,'ez'=8,'ec'=2] {'ez'}, dimensions={0}, use_global_device_ids=true | all-gather | bytes 294912 | tf_op jit(solution)/shard_map/all_gather | solution.py:146
  219.0 12.0 %all-gather = f32[32,1024]{1,0:T(8,128)S(1)} all-gather(f32[8,1024]{1,0:T(8,128)S(1)} %reduce_sum.107), channel_id=2, replica_groups=mesh['section'=4,'ex'=4,'ez'=8,'ec'=2] {'ex'}, dimensions={0}, use_global_device_ids=true | all-gather | bytes 163840 | tf_op jit(solution)/shard_map/all_gather | solution.py:146
  231.0 0.6 bitcast_reduce_fusion
  231.6 2.2 reshape.145
  233.8 8.0 %all-to-all-start.3 = ((bf16[64,48,128]{2,1,0:T(8,128)(2,1)}), bf16[64,48,128]{2,1,0:T(8,128)(2,1)S(1)}, u32[]{:S(2)}, u32[]{:S(2)}) async-start(bf16[64,48,128]{2,1,0:T(8,128)(2,1)} %reshape.145), calls=%async_computation.5 | async-start | bytes 1572864 | tf_op jit(solution)/shard_map/all_to_all | solution.py:148
  241.8 4.7 %fusion.2 = bf16[1,256,4096]{2,1,0:T(8,128)(2,1)} fusion(bf16[384,256]{1,0:T(8,128)(2,1)S(1)} %get-tuple-element.61, bf16[384,4096]{1,0:T(8,128)(2,1)} %all-gather.6.cloned.1.call-done, f32[384]{0:T(512)S(1)} %add_divide_fusion.1), kind=kOutput, calls=%fused_computation.7 | convolution fusion | flops 811073536 | bytes 5441024 | tf_op jit(solution)/shard_map/pf,pd->fd/dot_general | solution.py:106
  246.5 2.6 fusion
  249.1 2.6 fusion.1
  251.7 13.0 %all-to-all-done.3 = bf16[64,48,128]{2,1,0:T(8,128)(2,1)S(1)} async-done(((bf16[64,48,128]{2,1,0:T(8,128)(2,1)}), bf16[64,48,128]{2,1,0:T(8,128)(2,1)S(1)}, u32[]{:S(2)}, u32[]{:S(2)}) %all-to-all-start.3) | async-done | bytes 786464 | tf_op jit(solution)/shard_map/all_to_all | solution.py:148
  264.7 0.1 convert_reduce_fusion
  264.9 0.2 fusion.27
  265.1 0.2 convolution_add_fusion.1
  265.3 0.8 fusion.10
  (41 shorter events, 0.4 us)
Async XLA Ops:
  7.2 82.5 %copy-start = (bf16[1,4096,256]{2,1,0:T(8,128)(2,1)S(1)}, bf16[1,4096,256]{2,1,0:T(8,128)(2,1)}, u32[]{:S(2)}) copy-start(bf16[1,4096,256]{2,1,0:T(8,128)(2,1)} %param.14) | copy-start | bytes 6291460
  7.2 78.8 %all-gather.4.cloned.1.call-start = ((), (), s32[]{:S(2)}) async-start(), calls=%async_computation.6 | async-start | bytes 3932160 | tf_op jit(solution)/shard_map/all_gather | solution.py:61
  47.3 91.5 %reduce-scatter.3.cloned.1.call-start = ((), (), s32[]{:S(2)}) async-start(), calls=%async_computation.7 | async-start | bytes 3932160 | tf_op jit(solution)/shard_map/reduce_scatter | solution.py:95
  86.0 3.7 %copy-start.8 = (bf16[384,4096]{1,0:T(8,128)(2,1)S(1)}, bf16[384,4096]{1,0:T(8,128)(2,1)}, u32[]{:S(2)}) copy-start(bf16[384,4096]{1,0:T(8,128)(2,1)} %all-gather.4.cloned.1.call-done) | copy-start | bytes 9437188
  89.7 1.8 copy-start.10
  89.7 1.8 copy-start.1
  94.9 12.3 %copy-start.4 = (bf16[16,1024]{1,0:T(8,128)(2,1)S(1)}, bf16[16,1024]{1,0:T(8,128)(2,1)}, u32[]{:S(2)}) copy-start(bf16[16,1024]{1,0:T(8,128)(2,1)} %param.9) | copy-start | bytes 98308
  94.9 12.3 %copy-start.5 = (bf16[1024,8]{0,1:T(8,128)(2,1)S(1)}, bf16[1024,8]{0,1:T(8,128)(2,1)}, u32[]{:S(2)}) copy-start(bf16[1024,8]{0,1:T(8,128)(2,1)} %param.12) | copy-start | bytes 49156
  94.9 12.5 %copy-start.2 = (bf16[384,1024]{1,0:T(8,128)(2,1)S(1)}, bf16[384,1024]{1,0:T(8,128)(2,1)}, u32[]{:S(2)}) copy-start(bf16[384,1024]{1,0:T(8,128)(2,1)} %reshape.137) | copy-start | bytes 2359300
  94.9 27.7 %copy-start.7 = (s32[16,2]{0,1:T(2,128)S(1)}, s32[16,2]{0,1:T(2,128)}, u32[]{:S(2)}) copy-start(s32[16,2]{0,1:T(2,128)} %param.11) | copy-start | bytes 388
  96.4 38.7 %all-to-all-start.1 = ((bf16[64,64,128]{2,1,0:T(8,128)(2,1)}), bf16[64,64,128]{2,1,0:T(8,128)(2,1)}, u32[]{:S(2)}, u32[]{:S(2)}) async-start(bf16[64,64,128]{2,1,0:T(8,128)(2,1)} %bitcast.99), calls=%async_computation.2 | async-start | bytes 2097152 | tf_op jit(solution)/shard_map/all_to_all | solution.py:63
  107.1 75.6 %all-gather.6.cloned.1.call-start = ((), (), s32[]{:S(2)}) async-start(), calls=%async_computation.8 | async-start | bytes 3932160 | tf_op jit(solution)/shard_map/all_gather | solution.py:99
  138.7 33.0 %copy-start.6 = (bf16[16,1024]{1,0:T(8,128)(2,1)S(1)}, bf16[16,1024]{1,0:T(8,128)(2,1)}, u32[]{:S(2)}) copy-start(bf16[16,1024]{1,0:T(8,128)(2,1)} %param.10) | copy-start | bytes 98308
  141.0 30.3 %all-to-all-start.2 = ((bf16[64,48,128]{2,1,0:T(8,128)(2,1)}), bf16[64,48,128]{2,1,0:T(8,128)(2,1)S(1)}, u32[]{:S(2)}, u32[]{:S(2)}) async-start(bf16[64,48,128]{2,1,0:T(8,128)(2,1)} %reshape.142), calls=%async_computation.3 | async-start | bytes 1572864 | tf_op jit(solution)/shard_map/all_to_all | solution.py:102
  148.4 83.2 %reduce-scatter.5.cloned.1.call-start = ((), (), s32[]{:S(2)}) async-start(), calls=%async_computation.9 | async-start | bytes 3932160 | tf_op jit(solution)/shard_map/reduce_scatter | solution.py:140
  182.7 3.9 %copy-start.3 = (bf16[1,4096,256]{2,1,0:T(8,128)(2,1)S(1)}, bf16[1,4096,256]{2,1,0:T(8,128)(2,1)}, u32[]{:S(2)}) copy-start(bf16[1,4096,256]{2,1,0:T(8,128)(2,1)} %param.13) | copy-start | bytes 6291460
  233.8 30.9 %all-to-all-start.3 = ((bf16[64,48,128]{2,1,0:T(8,128)(2,1)}), bf16[64,48,128]{2,1,0:T(8,128)(2,1)S(1)}, u32[]{:S(2)}, u32[]{:S(2)}) async-start(bf16[64,48,128]{2,1,0:T(8,128)(2,1)} %reshape.145), calls=%async_computation.5 | async-start | bytes 1572864 | tf_op jit(solution)/shard_map/all_to_all | solution.py:148
  241.8 4.7 %copy-start.9 = (bf16[384,4096]{1,0:T(8,128)(2,1)S(1)}, bf16[384,4096]{1,0:T(8,128)(2,1)}, u32[]{:S(2)}) copy-start(bf16[384,4096]{1,0:T(8,128)(2,1)} %all-gather.4.cloned.1.call-done) | copy-start | bytes 9437188
Sparse Core Ops, SparseCore 0:
  47.5 38.5 all-gather.3
  95.0 40.7 reduce-scatter.2
  139.0 41.6 all-gather.5
  190.6 38.4 reduce-scatter.4

commit v11 on v10

--- a/solution.py
+++ b/solution.py
@@ -35,9 +35,8 @@
     pick_first = slot_row[:, 0:1] == slot_ids
     pick_second = slot_row[:, 1:2] == slot_ids
     pick_both = (pick_first | pick_second).astype(jnp.bfloat16)
-    both_rows = jnp.concatenate([tokens, cotangent], axis=1)
-    selected = jnp.einsum(
-        "ts,td->sd", pick_both, both_rows, preferred_element_type=jnp.float32
+    x_source = jnp.einsum(
+        "ts,td->sd", pick_both, tokens, preferred_element_type=jnp.float32
     ).astype(jnp.bfloat16)
     zero_i = jnp.zeros((), jnp.int32)
     other_slot = jnp.sum(
@@ -53,9 +52,12 @@
             experts * groups, rows, LANES
         )
 
-    x_block = selected[:, :width].reshape(experts, half, LANES)
-    c_block = jnp.concatenate([selected[:, width:].reshape(experts, half, LANES), meta], axis=1)
+    x_block = x_source.reshape(experts, half, LANES)
     x_recv = lax.all_to_all(spread(x_block), EXPERT_AXES, 0, 0, tiled=True)
+    cot_source = jnp.einsum(
+        "ts,td->sd", pick_both, cotangent, preferred_element_type=jnp.float32
+    ).astype(jnp.bfloat16)
+    c_block = jnp.concatenate([cot_source.reshape(experts, half, LANES), meta], axis=1)
     row_total = x_recv.shape[0] * capacity
     x_recv = x_recv.reshape(row_total, width)
     x_rows = lax.all_gather(x_recv, "section", axis=1, tiled=True)

time: 276 us -> 276 us (level)
  no operation moved by 1% of the time
where the time goes in v11:
time: 276 us; the launch traced here: 273 us
  blocking collectives  99.9 us (36%)
  waiting for transfers between devices  82.5 us (30%)
  matrix products  30.9 us (11%)
  starting transfers between devices  26 us (9%)
  local copies, waits for them, and re-layouts  16.1 us (6%)
  between operations  14.1 us (5%)
  other arithmetic  3.16 us (1%)
    all_gather x2, blocking collectives, per_device(): router_part = jnp.sum(lax.all_gather(router_part, name, axis=0), axis=0)  36.9 us
    all_to_all x1, blocking collectives, per_device(): x_recv = lax.all_to_all(spread(x_block), EXPERT_AXES, 0, 0, tiled=True)  34.7 us
    all_gather x1, waiting for transfers between devices, per_device(): x_rows = lax.all_gather(x_recv, 'section', axis=1, tiled=True)  34.1 us
    all_to_all x1, waiting for transfers between devices, per_device(): lax.all_to_all(out_red.reshape(n_dev, half, LANES), EXPERT_AXES, 0, 0, ti...  22.9 us
    psum x1, blocking collectives, per_device(): lax.psum(jnp.dot(x_recv, w_router, preferred_element_type=jnp.float32), '...  15 us
    all_to_all x1, waiting for transfers between devices, per_device(): lax.all_to_all(dx_red.reshape(n_dev, half, LANES), EXPERT_AXES, 0, 0, til...  13 us
    all_to_all x1, waiting for transfers between devices, per_device(): c_recv = lax.all_to_all(spread(c_block), EXPERT_AXES, 0, 0, tiled=True)  12.5 us
    all_to_all x1, starting transfers between devices, per_device(): c_recv = lax.all_to_all(spread(c_block), EXPERT_AXES, 0, 0, tiled=True)  10.7 us
  transfers between devices with their start and end apart: 7, of which 4 were waited for; matrix products, arithmetic and copies ran while one was open for 9% of the time, Pallas kernels for 0%

profile of v11, /device:TPU:8, one launch (start us, length us, event | category | flops | bytes accessed | tf_op | source)
XLA Modules:
  0.0 272.6 jit_solution(3696435519088308416)
XLA Ops:
  7.2 0.0 all-gather.4.cloned.1.call-start
  7.2 0.9 copy.41
  8.1 0.1 eq.76
  8.2 0.1 fusion.21
  8.3 0.1 reduce_window_sum.11
  8.3 0.2 select_reduce_fusion
  8.5 0.1 reshape.135
  8.6 0.1 copy.42
  8.7 0.7 multiply_add_fusion
  9.4 0.8 slice_bitcast_fusion.3
  10.2 1.0 convolution_convert_fusion.5
  11.2 0.1 broadcast_in_dim.97
  11.3 0.1 broadcast_in_dim.98
  11.4 34.7 %all_to_all.20 = bf16[64,48,128]{2,1,0:T(8,128)(2,1)S(1)} all-to-all(bf16[64,48,128]{2,1,0:T(8,128)(2,1)S(1)} %bitcast.102), channel_id=1, replica_groups=mesh['section'=4,'ex'=4,'ez'=8,'ec'=2] {'ex','ez','ec'}, dimensions={0} | all-to-all | bytes 1572864 | tf_op jit(solution)/shard_map/all_to_all | solution.py:56
  46.0 1.2 reshape.137
  47.3 0.0 reduce-scatter.3.cloned.1.call-start
  47.3 4.5 %reshape_squeeze.9 = bf16[256,4,1024]{2,1,0:T(4,128)(2,1)} reshape(bf16[1,256,4096]{2,1,0:T(8,128)(2,1)} %param.15) | data formatting | bytes 4194304 | tf_op jit(solution)/shard_map/reshape;squeeze | solution.py:92
  51.8 34.1 %all-gather.4.cloned.1.call-done = bf16[384,4096]{1,0:T(8,128)(2,1)} async-done(((bf16[384,1024]{1,0:T(8,128)(2,1)}), bf16[384,4096]{1,0:T(8,128)(2,1)}) %all-gather.4.cloned.1.call-update) | async-done | bytes 3145744 | tf_op jit(solution)/shard_map/all_gather | solution.py:63
  85.9 3.7 %fusion.7 = f32[384,256]{1,0:T(8,128)S(1)} fusion(bf16[384,4096]{1,0:T(8,128)(2,1)} %all-gather.4.cloned.1.call-done, bf16[1,4096,256]{2,1,0:T(8,128)(2,1)} %param.13), kind=kOutput, calls=%fused_computation.13 | convolution fusion | flops 805306368 | bytes 5636096 | tf_op jit(solution)/shard_map/dot_general | solution.py:86
  89.6 1.7 multiply_convert_fusion.5
  91.4 3.4 %convolution_convert_fusion.3 = bf16[384,4,1024]{2,0,1:T(8,128)(2,1)} fusion(bf16[256,4,1024]{2,1,0:T(4,128)(2,1)S(1)} %copy-done.1, bf16[384,256]{1,0:T(8,128)(2,1)S(1)} %get-tuple-element.59), kind=kOutput, calls=%fused_computation.8 | convolution fusion | flops 806879232 | bytes 5439488 | tf_op jit(solution)/shard_map/pf,fsd->spd/dot_general | solution.py:95
  94.8 0.1 add_reduce_fusion
  94.9 0.1 convert_element_type.122
  95.0 0.3 convolution_convert_fusion.4
  95.3 0.1 reshape.139
  95.4 1.2 broadcast_in_dim.104
  96.6 10.7 %all-to-all-start.1 = ((bf16[64,64,128]{2,1,0:T(8,128)(2,1)}), bf16[64,64,128]{2,1,0:T(8,128)(2,1)}, u32[]{:S(2)}, u32[]{:S(2)}) async-start(bf16[64,64,128]{2,1,0:T(8,128)(2,1)} %bitcast.101), calls=%async_computation.2 | async-start | bytes 2097152 | tf_op jit(solution)/shard_map/all_to_all | solution.py:65
  107.3 0.0 all-gather.6.cloned.1.call-start
  107.4 0.1 convolution_bitcast_fusion.1
  107.6 0.3 fusion.36
  107.9 15.0 %all-reduce.1 = (f32[384,8]{0,1:T(8,128)S(1)}, f32[16,8]{0,1:T(8,128)S(1)}) all-reduce(f32[384,8]{0,1:T(8,128)S(1)} %fusion.36, f32[16,8]{0,1:T(8,128)S(1)} %convolution_bitcast_fusion.1), channel_id=1, replica_groups=mesh['section'=4,'ex'=4,'ez'=8,'ec'=2] {'section'}, use_global_device_ids=true, to_apply=%region_4.5 | all-reduce | flops 3200 | bytes 25600 | tf_op jit(solution)/shard_map/psum | solution.py:75
  122.9 12.5 %all-to-all-done.1 = bf16[64,64,128]{2,1,0:T(8,128)(2,1)} async-done(((bf16[64,64,128]{2,1,0:T(8,128)(2,1)}), bf16[64,64,128]{2,1,0:T(8,128)(2,1)}, u32[]{:S(2)}, u32[]{:S(2)}) %all-to-all-start.1) | async-done | bytes 1048608 | tf_op jit(solution)/shard_map/all_to_all | solution.py:65
  135.4 1.0 fusion.20
  136.4 0.1 reshape.147
  136.5 1.2 slice.73
  137.7 1.2 reshape.141
  138.9 0.1 select_reduce_fusion.1
  139.0 0.0 all-gather.6.cloned.1.call-update
  139.1 2.2 reshape.142
  141.2 7.1 %all-to-all-start.2 = ((bf16[64,48,128]{2,1,0:T(8,128)(2,1)}), bf16[64,48,128]{2,1,0:T(8,128)(2,1)S(1)}, u32[]{:S(2)}, u32[]{:S(2)}) async-start(bf16[64,48,128]{2,1,0:T(8,128)(2,1)} %reshape.142), calls=%async_computation.3 | async-start | bytes 1572864 | tf_op jit(solution)/shard_map/all_to_all | solution.py:104
  148.3 0.0 reduce-scatter.5.cloned.1.call-start
  148.4 22.9 %all-to-all-done.2 = bf16[64,48,128]{2,1,0:T(8,128)(2,1)S(1)} async-done(((bf16[64,48,128]{2,1,0:T(8,128)(2,1)}), bf16[64,48,128]{2,1,0:T(8,128)(2,1)S(1)}, u32[]{:S(2)}, u32[]{:S(2)}) %all-to-all-start.2) | async-done | bytes 786464 | tf_op jit(solution)/shard_map/all_to_all | solution.py:104
  171.3 0.1 convert_reduce_fusion.1
  171.4 0.2 fusion.22
  171.6 1.0 fusion.18
  172.6 10.0 %psum.30 = f32[16,2]{0,1:T(2,128)S(1)} all-reduce(f32[16,2]{0,1:T(2,128)S(1)} %pad_maximum_fusion), channel_id=1, replica_groups=mesh['section'=4,'ex'=4,'ez'=8,'ec'=2] {'section'}, use_global_device_ids=true, to_apply=%region_12.13 | all-reduce | flops 32 | bytes 256 | tf_op jit(solution)/shard_map/psum | solution.py:135
  182.7 3.9 %multiply_convert_fusion.3 = (bf16[384,256]{1,0:T(8,128)(2,1)S(1)}, bf16[384,256]{1,0:T(8,128)(2,1)S(1)}) fusion(f32[384,256]{1,0:T(8,128)} %copy-done.10, f32[384,256]{1,0:T(8,128)} %get-tuple-element.60, bf16[1,256,4096]{2,1,0:T(8,128)(2,1)} %param.15, bf16[384,4096]{1,0:T(8,128)(2,1)} %all-gather.6.cloned.1.call-done, f32[384]{0:T(512)S(1)} %add_divide_fusion.1), kind=kOutput, calls=%fused_computation.25 | convolution fusion | flops 811302912 | bytes 6424064 | tf_op jit(solution)/shard_map/pd,fd->pf/dot_general | solution.py:107
  186.6 1.0 fusion.14
  187.6 2.9 %add_convert_fusion = bf16[384,4,1024]{2,0,1:T(8,128)(2,1)} fusion(f32[384,4,1024]{2,0,1:T(8,128)S(1)} %fusion.14, bf16[4,1024,256]{2,1,0:T(8,128)(2,1)S(1)} %bitcast.98, bf16[384,256]{1,0:T(8,128)(2,1)S(1)} %get-tuple-element.50), kind=kOutput, calls=%fused_computation | convolution fusion | flops 808452096 | bytes 11730944 | tf_op jit(solution)/shard_map/pf,sdf->spd/dot_general | solution.py:132
  190.5 0.1 convolution_bitcast_fusion
  190.6 3.4 %psum.31 = f32[1,8,1024]{2,1,0:T(8,128)S(1)} all-reduce(f32[1,8,1024]{2,1,0:T(8,128)S(1)} %convolution_bitcast_fusion), channel_id=1, replica_groups=mesh['section'=4,'ex'=4,'ez'=8,'ec'=2] {'ec'}, use_global_device_ids=true, to_apply=%region_13.14 | all-reduce | flops 8192 | bytes 65536 | tf_op jit(solution)/shard_map/psum | solution.py:146
  194.0 24.9 %all_gather.21 = f32[8,8,1024]{2,1,0:T(8,128)S(1)} all-gather(f32[1,8,1024]{2,1,0:T(8,128)S(1)} %psum.31), channel_id=1, replica_groups=mesh['section'=4,'ex'=4,'ez'=8,'ec'=2] {'ez'}, dimensions={0}, use_global_device_ids=true | all-gather | bytes 294912 | tf_op jit(solution)/shard_map/all_gather | solution.py:148
  218.9 12.0 %all-gather = f32[32,1024]{1,0:T(8,128)S(1)} all-gather(f32[8,1024]{1,0:T(8,128)S(1)} %reduce_sum.107), channel_id=2, replica_groups=mesh['section'=4,'ex'=4,'ez'=8,'ec'=2] {'ex'}, dimensions={0}, use_global_device_ids=true | all-gather | bytes 163840 | tf_op jit(solution)/shard_map/all_gather | solution.py:148
  230.9 0.6 bitcast_reduce_fusion
  231.5 2.2 reshape.145
  233.7 8.0 %all-to-all-start.3 = ((bf16[64,48,128]{2,1,0:T(8,128)(2,1)}), bf16[64,48,128]{2,1,0:T(8,128)(2,1)S(1)}, u32[]{:S(2)}, u32[]{:S(2)}) async-start(bf16[64,48,128]{2,1,0:T(8,128)(2,1)} %reshape.145), calls=%async_computation.5 | async-start | bytes 1572864 | tf_op jit(solution)/shard_map/all_to_all | solution.py:150
  241.7 4.7 %fusion.2 = bf16[1,256,4096]{2,1,0:T(8,128)(2,1)} fusion(bf16[384,256]{1,0:T(8,128)(2,1)S(1)} %get-tuple-element.59, bf16[384,4096]{1,0:T(8,128)(2,1)} %all-gather.6.cloned.1.call-done, f32[384]{0:T(512)S(1)} %add_divide_fusion.1), kind=kOutput, calls=%fused_computation.7 | convolution fusion | flops 811073536 | bytes 5441024 | tf_op jit(solution)/shard_map/pf,pd->fd/dot_general | solution.py:108
  246.4 2.6 fusion
  249.0 2.6 fusion.1
  251.7 13.0 %all-to-all-done.3 = bf16[64,48,128]{2,1,0:T(8,128)(2,1)S(1)} async-done(((bf16[64,48,128]{2,1,0:T(8,128)(2,1)}), bf16[64,48,128]{2,1,0:T(8,128)(2,1)S(1)}, u32[]{:S(2)}, u32[]{:S(2)}) %all-to-all-start.3) | async-done | bytes 786464 | tf_op jit(solution)/shard_map/all_to_all | solution.py:150
  264.6 0.1 convert_reduce_fusion
  264.8 0.2 fusion.24
  265.0 0.2 convolution_add_fusion.1
  265.2 0.8 fusion.10
  (41 shorter events, 0.3 us)
Async XLA Ops:
  7.2 82.4 %copy-start = (bf16[1,4096,256]{2,1,0:T(8,128)(2,1)S(1)}, bf16[1,4096,256]{2,1,0:T(8,128)(2,1)}, u32[]{:S(2)}) copy-start(bf16[1,4096,256]{2,1,0:T(8,128)(2,1)} %param.14) | copy-start | bytes 6291460
  7.2 78.7 %all-gather.4.cloned.1.call-start = ((), (), s32[]{:S(2)}) async-start(), calls=%async_computation.6 | async-start | bytes 3932160 | tf_op jit(solution)/shard_map/all_gather | solution.py:63
  47.3 91.8 %reduce-scatter.3.cloned.1.call-start = ((), (), s32[]{:S(2)}) async-start(), calls=%async_computation.7 | async-start | bytes 3932160 | tf_op jit(solution)/shard_map/reduce_scatter | solution.py:97
  85.9 3.7 %copy-start.8 = (bf16[384,4096]{1,0:T(8,128)(2,1)S(1)}, bf16[384,4096]{1,0:T(8,128)(2,1)}, u32[]{:S(2)}) copy-start(bf16[384,4096]{1,0:T(8,128)(2,1)} %all-gather.4.cloned.1.call-done) | copy-start | bytes 9437188
  89.6 1.8 copy-start.10
  89.6 1.8 copy-start.1
  91.4 3.6 %copy-start.6 = (bf16[16,1024]{1,0:T(8,128)(2,1)S(1)}, bf16[16,1024]{1,0:T(8,128)(2,1)}, u32[]{:S(2)}) copy-start(bf16[16,1024]{1,0:T(8,128)(2,1)} %param.10) | copy-start | bytes 98308
  94.8 12.6 %copy-start.4 = (bf16[16,1024]{1,0:T(8,128)(2,1)S(1)}, bf16[16,1024]{1,0:T(8,128)(2,1)}, u32[]{:S(2)}) copy-start(bf16[16,1024]{1,0:T(8,128)(2,1)} %param.9) | copy-start | bytes 98308
  94.8 12.6 %copy-start.5 = (bf16[1024,8]{0,1:T(8,128)(2,1)S(1)}, bf16[1024,8]{0,1:T(8,128)(2,1)}, u32[]{:S(2)}) copy-start(bf16[1024,8]{0,1:T(8,128)(2,1)} %param.12) | copy-start | bytes 49156
  94.8 12.8 %copy-start.2 = (bf16[384,1024]{1,0:T(8,128)(2,1)S(1)}, bf16[384,1024]{1,0:T(8,128)(2,1)}, u32[]{:S(2)}) copy-start(bf16[384,1024]{1,0:T(8,128)(2,1)} %reshape.137) | copy-start | bytes 2359300
  94.8 28.0 %copy-start.7 = (s32[16,2]{0,1:T(2,128)S(1)}, s32[16,2]{0,1:T(2,128)}, u32[]{:S(2)}) copy-start(s32[16,2]{0,1:T(2,128)} %param.11) | copy-start | bytes 388
  96.6 38.7 %all-to-all-start.1 = ((bf16[64,64,128]{2,1,0:T(8,128)(2,1)}), bf16[64,64,128]{2,1,0:T(8,128)(2,1)}, u32[]{:S(2)}, u32[]{:S(2)}) async-start(bf16[64,64,128]{2,1,0:T(8,128)(2,1)} %bitcast.101), calls=%async_computation.2 | async-start | bytes 2097152 | tf_op jit(solution)/shard_map/all_to_all | solution.py:65
  107.3 75.3 %all-gather.6.cloned.1.call-start = ((), (), s32[]{:S(2)}) async-start(), calls=%async_computation.8 | async-start | bytes 3932160 | tf_op jit(solution)/shard_map/all_gather | solution.py:101
  141.2 30.0 %all-to-all-start.2 = ((bf16[64,48,128]{2,1,0:T(8,128)(2,1)}), bf16[64,48,128]{2,1,0:T(8,128)(2,1)S(1)}, u32[]{:S(2)}, u32[]{:S(2)}) async-start(bf16[64,48,128]{2,1,0:T(8,128)(2,1)} %reshape.142), calls=%async_computation.3 | async-start | bytes 1572864 | tf_op jit(solution)/shard_map/all_to_all | solution.py:104
  148.3 83.2 %reduce-scatter.5.cloned.1.call-start = ((), (), s32[]{:S(2)}) async-start(), calls=%async_computation.9 | async-start | bytes 3932160 | tf_op jit(solution)/shard_map/reduce_scatter | solution.py:142
  182.6 3.9 %copy-start.3 = (bf16[1,4096,256]{2,1,0:T(8,128)(2,1)S(1)}, bf16[1,4096,256]{2,1,0:T(8,128)(2,1)}, u32[]{:S(2)}) copy-start(bf16[1,4096,256]{2,1,0:T(8,128)(2,1)} %param.13) | copy-start | bytes 6291460
  233.7 30.9 %all-to-all-start.3 = ((bf16[64,48,128]{2,1,0:T(8,128)(2,1)}), bf16[64,48,128]{2,1,0:T(8,128)(2,1)S(1)}, u32[]{:S(2)}, u32[]{:S(2)}) async-start(bf16[64,48,128]{2,1,0:T(8,128)(2,1)} %reshape.145), calls=%async_computation.5 | async-start | bytes 1572864 | tf_op jit(solution)/shard_map/all_to_all | solution.py:150
  241.7 4.7 %copy-start.9 = (bf16[384,4096]{1,0:T(8,128)(2,1)S(1)}, bf16[384,4096]{1,0:T(8,128)(2,1)}, u32[]{:S(2)}) copy-start(bf16[384,4096]{1,0:T(8,128)(2,1)} %all-gather.4.cloned.1.call-done) | copy-start | bytes 9437188
Sparse Core Ops, SparseCore 0:
  47.4 38.5 all-gather.3
  94.9 40.7 reduce-scatter.2
  139.2 41.3 all-gather.5
  190.6 38.4 reduce-scatter.4
